TPU v7x, 128 devices: a whole 4x4x4 slice. The times are simulated.
128 devices in a mesh: row: 8 (over x, core), col: 16 (over y, z).
Axes of the slice: x: 4, y: 4, z: 4, core: 2. Of those that a mesh axis runs over, the one named last changes fastest.
Arguments:
- front_matrix: float32 [16384, 16384], P('row', 'col'), may hold values from -2.5 to 202.5, as said below
- child_schur: float32 [2, 8192, 8192], P(None, 'row', 'col'), may hold values from -1.25 to 1.25
- child_index: int32 [2, 128], replicated, may hold values from 0 to 255, as said below
- child_valid: int32 [2, 128], replicated, may hold values 0 or 1
Outputs:
- trailing: float32 [16384, 16384], P('row', 'col')
- panel_factor: float32 [16384, 512], P('row')
Inputs may be any that keep to these rules, and one draw needn't show every extreme that they name: `front_matrix`: off the logical diagonal the entries lie in -2.5 to 2.5, on it in 97.5 to 202.5. `child_index`: each child's 128 entries are distinct front blocks. Among the child blocks a that share a mod 8, exactly 2 land in front blocks of each value mod 8; among the child blocks b that share b mod 16, at most 1 land in front blocks of any one value mod 16, and some value takes exactly 1.
All inputs are finite; a program needn't handle non-finite values.
Results may differ from a plain program's by a relative error of at most 0.00005.
Values sent between devices are 32-bit elements; how exact they have to be, the bound alone decides.
No kernel may reach another device: no remote copies, remote signals or barrier semaphores. Data moves between devices by JAX's collectives and lax.ppermute only.
A program may use at most 256 MiB of HBM per device.

v0:
```python
import jax
import jax.numpy as jnp
from jax import lax
from jax.sharding import PartitionSpec as P

CHILD = 8192
PANEL = 512
BLK = 64


exact_mode = lax.Precision.HIGHEST


def spread_2(shard, axis, root):
    mine = lax.axis_index(axis) == root
    return lax.psum(jnp.where(mine, shard, jnp.zeros_like(shard)), axis)


def take_rows(source, indices):
    return jnp.take(source, indices, axis=0)


def place_blocks(arrived, col_source, row_source):
    picked = jnp.take(arrived, col_source, axis=0)
    return jnp.take(picked, row_source, axis=1)


def on_device(front_matrix, child_schur, child_index, child_valid):
    row_count = lax.axis_size("row")
    col_count = lax.axis_size("col")
    row_place = lax.axis_index("row")
    col_place = lax.axis_index("col")
    local_rows, local_cols = front_matrix.shape
    row_blocks = local_rows // BLK
    col_blocks = local_cols // BLK
    child_blocks = CHILD // BLK
    child_rowblk = child_schur.shape[1] // BLK
    child_colblk = child_schur.shape[2] // BLK
    per_owner = child_blocks // (row_count * row_count)
    col_multi = max(1, child_blocks // (col_count * col_count))
    row_slots = row_count * per_owner
    col_slots = col_count * col_multi
    validity = child_valid.astype(jnp.float32)
    all_blocks = jnp.arange(child_blocks)
    owner_row = child_index % row_count
    owner_col = child_index % col_count
    sender_row = all_blocks % row_count
    sender_col = all_blocks % col_count
    before = all_blocks[None, :] < all_blocks[:, None]
    earlier_row = (sender_row[:, None] == sender_row[None, :]) & before
    earlier_col = (sender_col[:, None] == sender_col[None, :]) & before
    row_rank = jnp.sum(
        (earlier_row[None] & (owner_row[:, :, None] == owner_row[:, None, :])).astype(jnp.int32),
        axis=2,
    )
    col_rank = jnp.sum(
        (earlier_col[None] & (owner_col[:, :, None] == owner_col[:, None, :])).astype(jnp.int32),
        axis=2,
    )
    row_key = owner_row * per_owner + row_rank
    col_key = owner_col * col_multi + col_rank
    local_arow = row_place + row_count * jnp.arange(child_rowblk)
    mine_rowkey = jnp.take(row_key, local_arow, axis=1)
    row_hit_send = mine_rowkey[:, :, None] == jnp.arange(row_slots)[None, None, :]
    src_row = jnp.sum(
        row_hit_send.astype(jnp.int32) * jnp.arange(child_rowblk)[None, :, None], axis=1
    )
    local_bcol = col_place + col_count * jnp.arange(child_colblk)
    mine_colkey = jnp.take(col_key, local_bcol, axis=1)
    col_hit_send = mine_colkey[:, :, None] == jnp.arange(col_slots)[None, None, :]
    src_col = jnp.sum(
        col_hit_send.astype(jnp.int32) * jnp.arange(child_colblk)[None, :, None], axis=1
    )
    has_col = jnp.sum(col_hit_send.astype(jnp.float32), axis=1)
    blocks = child_schur.reshape(2, child_rowblk, BLK, child_colblk * BLK)
    outgoing = jax.vmap(take_rows)(blocks, src_row)
    outgoing = outgoing.reshape(2, row_slots * BLK, child_colblk * BLK)
    section_one = lax.all_to_all(outgoing, "row", split_axis=1, concat_axis=1, tiled=True)
    section_one = section_one.reshape(2, row_slots, BLK, child_colblk, BLK).transpose(0, 3, 1, 2, 4)
    onward = jax.vmap(take_rows)(section_one, src_col) * has_col[:, :, None, None, None]
    onward = onward.reshape(2, col_slots * row_slots, BLK * BLK)
    section_two = lax.all_to_all(onward, "col", split_axis=1, concat_axis=1, tiled=True)
    arrived = section_two.reshape(2, col_slots, row_slots, BLK, BLK)
    front_rowblk = row_place + row_count * jnp.arange(row_blocks)
    match_rows = (child_index[:, None, :] == front_rowblk[None, :, None]).astype(jnp.int32)
    row_slot_of = sender_row[None, :] * per_owner + row_rank
    row_source = jnp.sum(match_rows * row_slot_of[:, None, :], axis=2)
    row_weight = jnp.sum(match_rows.astype(jnp.float32) * validity[:, None, :], axis=2)
    front_colblk = col_place + col_count * jnp.arange(col_blocks)
    match_cols = (child_index[:, None, :] == front_colblk[None, :, None]).astype(jnp.int32)
    col_slot_of = sender_col[None, :] * col_multi + col_rank
    col_source = jnp.sum(match_cols * col_slot_of[:, None, :], axis=2)
    col_weight = jnp.sum(match_cols.astype(jnp.float32) * validity[:, None, :], axis=2)
    placed = jax.vmap(place_blocks)(arrived, col_source, row_source)
    placed = placed * col_weight[:, :, None, None, None] * row_weight[:, None, :, None, None]
    contributions = placed.transpose(0, 2, 3, 1, 4).reshape(2, local_rows, local_cols)
    extended = front_matrix + contributions[0] + contributions[1]
    panel_width = PANEL // BLK
    columns = []
    for root_index in range(panel_width):
        columns.append(spread_2(extended[:, :BLK], "col", root_index))
    panel_cols = jnp.concatenate(columns, axis=1)
    corner_rows = []
    for root_index in range(panel_width):
        start = root_index // row_count * BLK
        corner_rows.append(spread_2(panel_cols[start : start + BLK], "row", root_index % row_count))
    corner = jnp.concatenate(corner_rows, axis=0)
    lower_factor = jnp.linalg.cholesky(corner)
    solved = jax.scipy.linalg.solve_triangular(lower_factor, panel_cols.T, lower=True).T
    logical_blk = jnp.arange(row_blocks) * row_count + row_place
    factor_blocks = lower_factor.reshape(panel_width, BLK, PANEL)
    picked = jnp.take(factor_blocks, jnp.minimum(logical_blk, panel_width - 1), axis=0)
    in_panel = (logical_blk < panel_width)[:, None, None]
    panel_factor = jnp.where(in_panel, picked, solved.reshape(row_blocks, BLK, PANEL)).reshape(
        local_rows, PANEL
    )
    spread = col_count // row_count
    arranged = panel_factor.reshape(col_blocks, spread, BLK, PANEL)
    chosen = lax.dynamic_index_in_dim(arranged, col_place // row_count, axis=1, keepdims=False)
    chosen = chosen.reshape(col_blocks * BLK, PANEL)
    across = spread_2(chosen, "row", col_place % row_count)
    update = jnp.einsum("rp,cp->rc", panel_factor, across, precision=exact_mode)
    logical_row = jnp.arange(local_rows) // BLK * row_count + row_place
    logical_col = jnp.arange(local_cols) // BLK * col_count + col_place
    retained = (logical_row >= panel_width)[:, None] & (logical_col >= panel_width)[None, :]
    trailing = jnp.where(retained, extended - update, jnp.zeros_like(update))
    return (trailing, panel_factor)


def solution(mesh):
    in_specs = (P("row", "col"), P(None, "row", "col"), P(), P())
    out_specs = (P("row", "col"), P("row", None))
    return jax.shard_map(
        on_device, mesh=mesh, in_specs=in_specs, out_specs=out_specs, check_vma=False
    )
```

profile of v0, /device:TPU:1, one launch (start us, length us, event | category | flops | bytes accessed | tf_op | source)
XLA Modules:
  0.0 927.7 jit_solution(2429928960758117711)
XLA Ops:
  30.1 48.2 %all-to-all-done = f32[2,1024,512]{2,0,1:T(2,128)} async-done(((f32[2,1024,512]{2,0,1:T(2,128)}), f32[2,1024,512]{2,0,1:T(2,128)}, u32[]{:S(2)}, u32[]{:S(2)}) %all-to-all-start) | async-done | bytes 4194336 | tf_op jit(solution)/shard_map/all_to_all | solution.py:78
  96.1 11.8 %gather_fusion.4 = f32[32,16,64,64]{3,2,1,0:T(8,128)} fusion(f32[2,8,16,64,64]{4,3,2,1,0:T(8,128)} %bitcast.112, s32[32]{0:T(128)S(1)} %reshape.513), kind=kCustom, calls=%fused_computation.4 | custom fusion | bytes 16777472 | tf_op jit(solution)/shard_map/vmap(jit(_take))/gather | solution.py:20
  107.9 14.7 %gather.44 = f32[2,256,4096]{2,1,0:T(8,128)} reshape(f32[32,16,64,64]{3,2,1,0:T(8,128)} %gather_fusion.4) | data formatting | bytes 16777216 | tf_op jit(solution)/shard_map/vmap(jit(_take))/gather | solution.py:20
  156.1 131.8 %all-to-all-done.1 = f32[2,256,4096]{2,0,1:T(2,128)} async-done(((f32[2,256,4096]{2,0,1:T(2,128)}), f32[2,256,4096]{2,0,1:T(2,128)}, u32[]{:S(2)}, u32[]{:S(2)}) %all-to-all-start.1) | async-done | bytes 8388640 | tf_op jit(solution)/shard_map/all_to_all | solution.py:82
  287.8 16.0 %reshape.461 = f32[2,16,16,64,64]{4,3,0,2,1:T(8,128)} reshape(f32[2,256,4096]{2,0,1:T(2,128)} %all-to-all-done.1) | data formatting | bytes 16777216 | tf_op jit(solution)/shard_map/reshape | solution.py:83
  303.9 14.2 %gather_fusion.5 = f32[32,16,64,64]{3,2,1,0:T(8,128)} fusion(f32[2,16,16,64,64]{4,3,0,2,1:T(8,128)} %reshape.461, s32[32]{0:T(128)S(1)} %reshape.519), kind=kCustom, calls=%fused_computation.5 | custom fusion | bytes 16777472 | tf_op jit(solution)/shard_map/vmap(jit(_take))/gather | solution.py:24
  318.1 12.3 %broadcast_select_fusion = f32[2,16,16,64,64]{4,3,2,1,0:T(8,128)} fusion(f32[2,16,16,64,64]{4,3,2,1,0:T(8,128)} %bitcast.113, pred[2,16]{1,0:T(4,128)(4,1)S(1)} %compare_and_fusion.6), kind=kLoop, calls=%fused_computation.13 | loop fusion | flops 2097152 | bytes 16777248 | tf_op jit(solution)/shard_map/vmap(jit(_take))/select_n | solution.py:24
  330.4 19.1 %gather_fusion.6 = f32[64,16,64,64]{3,2,1,0:T(8,128)} fusion(f32[2,16,16,64,64]{4,3,2,1,0:T(8,128)} %broadcast_select_fusion, s32[64]{0:T(128)S(1)} %reshape.525), kind=kCustom, calls=%fused_computation.6 | custom fusion | bytes 33554944 | tf_op jit(solution)/shard_map/vmap(jit(_take))/gather | solution.py:25
  349.5 25.0 %multiply_bitcast_fusion = f32[2,32,64,16,64]{4,2,3,1,0:T(8,128)} fusion(f32[2,32,16,64,64]{4,3,2,1,0:T(8,128)} %bitcast.111, f32[2,32]{1,0:T(2,128)S(1)} %fusion.39, f32[2,16]{1,0:T(2,128)S(1)} %fusion.43, pred[2,32]{1,0:T(4,128)(4,1)S(1)} %compare_and_fusion.7), kind=kLoop, calls=%fused_computation.9 | loop fusion | flops 12582912 | bytes 33554880 | tf_op jit(solution)/shard_map/mul | solution.py:95
  374.5 21.8 %fusion.75 = (f32[1,32,64,16,64]{4,2,3,1,0:T(8,128)}, f32[1,32,64,16,64]{4,2,3,1,0:T(8,128)}) fusion(f32[2,32,64,16,64]{4,2,3,1,0:T(8,128)} %multiply_bitcast_fusion), kind=kLoop, calls=%fused_computation.216 | loop fusion | bytes 33554432 | tf_op jit(solution)/shard_map/slice | solution.py:97
  396.3 18.4 %copy.165 = f32[1,32,64,16,64]{2,1,4,3,0:T(8,128)} copy(f32[1,32,64,16,64]{4,2,3,1,0:T(8,128)} %get-tuple-element.52) | data formatting | bytes 16777216 | tf_op jit(solution)/shard_map/slice | solution.py:97
  414.7 14.8 %squeeze.8 = f32[2048,1024]{0,1:T(8,128)} reshape(f32[1,32,64,16,64]{2,1,4,3,0:T(8,128)} %copy.165) | data formatting | bytes 16777216 | tf_op jit(solution)/shard_map/squeeze | solution.py:97
  429.5 18.4 %copy.167 = f32[1,32,64,16,64]{2,1,4,3,0:T(8,128)} copy(f32[1,32,64,16,64]{4,2,3,1,0:T(8,128)} %get-tuple-element.53) | data formatting | bytes 16777216 | tf_op jit(solution)/shard_map/slice | solution.py:97
  447.9 14.8 %squeeze.9 = f32[2048,1024]{0,1:T(8,128)} reshape(f32[1,32,64,16,64]{2,1,4,3,0:T(8,128)} %copy.167) | data formatting | bytes 16777216 | tf_op jit(solution)/shard_map/squeeze | solution.py:97
  478.1 110.4 %all-reduce.9.cloned.1.call-done = (f32[2048,64]{0,1:T(8,128)}, f32[2048,64]{0,1:T(8,128)}, f32[2048,64]{0,1:T(8,128)}, f32[2048,64]{0,1:T(8,128)}, f32[2048,64]...) async-done(((f32[2048,64]{0,1:T(8,128)}, f32[2048,64]{0,1:T(8,128)}, f32[2048,64]{0,1:T(8,128)}, f32[2048,64]{0,1:T(8,128)}, ...) | async-done | bytes 4194320 | tf_op jit(solution)/shard_map/psum | solution.py:16
  596.9 64.0 %all-reduce.11.cloned.1.call-done = (f32[64,512]{0,1:T(8,128)}, f32[64,512]{0,1:T(8,128)}, f32[64,512]{0,1:T(8,128)}, f32[64,512]{0,1:T(8,128)}, f32[64,512]{0,1...) async-done(((f32[64,512]{0,1:T(8,128)}, f32[64,512]{0,1:T(8,128)}, f32[64,512]{0,1:T(8,128)}, f32[64,512]{0,1:T(8,128)}, f32[64,512]{0,1:T(8,128)}, ...) | async-done | bytes 1048592 | tf_op jit(solution)/shard_map/psum | solution.py:16
  663.6 11.7 %cholesky.104 = f32[128,128]{1,0:T(8,128)S(1)} custom-call(f32[128,128]{1,0:T(8,128)S(1)} %cholesky.266), custom_call_target="Cholesky" | custom-call | tf_op jit(solution)/shard_map/jit(cholesky)/cholesky | solution.py:108
  686.0 11.7 %cholesky.217 = f32[128,128]{1,0:T(8,128)S(1)} custom-call(f32[128,128]{1,0:T(8,128)S(1)} %cholesky.270), custom_call_target="Cholesky" | custom-call | tf_op jit(solution)/shard_map/jit(cholesky)/cholesky | solution.py:108
  709.7 11.7 %cholesky.238 = f32[128,128]{1,0:T(8,128)S(1)} custom-call(f32[128,128]{1,0:T(8,128)S(1)} %cholesky.275), custom_call_target="Cholesky" | custom-call | tf_op jit(solution)/shard_map/jit(cholesky)/cholesky | solution.py:108
  732.6 11.7 %cholesky.255 = f32[128,128]{1,0:T(8,128)S(1)} custom-call(f32[128,128]{1,0:T(8,128)S(1)} %convolution_subtract_fusion.4), custom_call_target="Cholesky" | custom-call | tf_op jit(solution)/shard_map/jit(cholesky)/cholesky | solution.py:108
  748.2 10.5 %while.1 = (s32[]{:T(128)}, f32[512,512]{1,0:T(8,128)S(1)}, s32[4,2]{0,1:T(2,128)S(1)}, f32[4,128,128]{2,1,0:T(8,128)}, s32[]{:T(128)}) while((s32[]{:T(128)}, f32[512,512]{1,0:T(8,128)S(1)}, s32[4,2]{0,1:T(2,128)S(1)}, f32[4,128,128]{2,1,0:T(8,128)}, s32[]{:T(128)}) %tuple.59), condition=%wide.while_cond, body=%wide.while_body.sunk | while | flops 2 | bytes 132705 | solution.py:109
  758.8 40.2 %custom-call.34 = f32[4,128,128]{1,2,0:T(8,128)S(1)} custom-call(f32[4,128,128]{2,1,0:T(8,128)} %get-tuple-element.9), custom_call_target="InvertDiagBlocksLowerTriangular" | custom-call | tf_op jit(solution)/shard_map/jit(_solve_triangular)/triangular_solve | solution.py:109
  844.9 48.7 %all-reduce.7.cloned.1.call-done = f32[1024,512]{1,0:T(8,128)} async-done(((f32[1024,512]{1,0:T(8,128)}), f32[1024,512]{1,0:T(8,128)}) %all-reduce.7.cloned.1.call-update) | async-done | bytes 2097168 | tf_op jit(solution)/shard_map/psum | solution.py:16
  893.5 18.2 %subtract_select_fusion = f32[2048,1024]{0,1:T(8,128)} fusion(f32[2048,1024]{0,1:T(8,128)} %copy-done, pred[2048]{0:T(1024)(128)(4,1)S(1)} %fusion.46, pred[1024]{0:T(1024)(128)(4,1)S(1)} %fusion.52, f32[2048,512]{0,1:T(8,128)} %select_select_fusion, f32[1024,512]{1,0:T(8,128)} %all-reduce.7.cloned.1.call-done), kind=kOutput, calls=%fused_computation.11 | convolution fusion | flops 12891193344 | bytes 23071744 | tf_op jit(solution)/shard_map/rp,cp->rc/dot_general | solution.py:122
  (173 shorter events, 200.7 us)
Async XLA Ops:
  23.4 54.9 %all-to-all-start = ((f32[2,1024,512]{2,0,1:T(2,128)}), f32[2,1024,512]{2,0,1:T(2,128)}, u32[]{:S(2)}, u32[]{:S(2)}) async-start(f32[2,1024,512]{2,0,1:T(2,128)} %copy.161), calls=%async_computation | async-start | bytes 8388608 | tf_op jit(solution)/shard_map/all_to_all | solution.py:78
  137.3 8.7 copy-start.11
  137.3 9.2 copy-start.12
  137.3 150.5 %all-to-all-start.1 = ((f32[2,256,4096]{2,0,1:T(2,128)}), f32[2,256,4096]{2,0,1:T(2,128)}, u32[]{:S(2)}, u32[]{:S(2)}) async-start(f32[2,256,4096]{2,0,1:T(2,128)} %copy.164), calls=%async_computation.1 | async-start | bytes 16777216 | tf_op jit(solution)/shard_map/all_to_all | solution.py:82
  145.4 443.1 %all-reduce.9.cloned.1.call-start = ((), (), s32[]{:S(2)}) async-start(), calls=%async_computation.3 | async-start | bytes 8388608 | tf_op jit(solution)/shard_map/psum | solution.py:16
  472.3 3.4 copy-start
  477.8 183.1 %all-reduce.11.cloned.1.call-start = ((), (), s32[]{:S(2)}) async-start(), calls=%async_computation.4 | async-start | bytes 4194304 | tf_op jit(solution)/shard_map/psum | solution.py:16
  588.5 4.5 copy-start.10
  588.5 4.5 copy-start.9
  588.6 4.6 copy-start.8
  588.6 4.6 copy-start.7
  593.2 2.0 copy-start.4
  596.6 296.9 %all-reduce.7.cloned.1.call-start = ((), (), s32[]{:S(2)}) async-start(), calls=%async_computation.2 | async-start | bytes 4194304 | tf_op jit(solution)/shard_map/psum | solution.py:16
  758.7 42.6 %copy-start.6 = (f32[512,512]{1,0:T(8,128)}, f32[512,512]{1,0:T(8,128)S(1)}, u32[]{:S(2)}) copy-start(f32[512,512]{1,0:T(8,128)S(1)} %get-tuple-element.177) | copy-start | bytes 3145732
  798.9 5.7 copy-start.5
  807.9 4.2 copy-start.1
  812.2 1.0 copy-start.3
  828.5 5.5 copy-start.2
Sparse Core Ops, SparseCore 0:
  477.9 110.5 all-reduce.8
  596.8 64.1 all-reduce.10
  828.3 65.2 all-reduce.6
where the time goes:
time: 936 us; the launch traced here: 928 us
  waiting for transfers between devices  403 us (43%)
  local copies, waits for them, and re-layouts  267 us (29%)
  other arithmetic  193 us (21%)
  matrix products  33.2 us (4%)
  between operations  17.1 us (2%)
  starting transfers between devices  14.9 us (2%)
    psum x3, waiting for transfers between devices, spread_2(): return lax.psum(jnp.where(mine, shard, jnp.zeros_like(shard)), axis)  223 us
    all_to_all x1, waiting for transfers between devices, on_device(): lax.all_to_all(onward, 'col', split_axis=1, concat_axis=1, tiled=True)  132 us
    another operation x15, other arithmetic, on_device(): lower_factor = jnp.linalg.cholesky(corner)  79.3 us
    slice x3, local copies, waits for them, and re-layouts, on_device(): extended = front_matrix + contributions[0] + contributions[1]  58.6 us
    all_to_all x1, waiting for transfers between devices, on_device(): lax.all_to_all(outgoing, 'row', split_axis=1, concat_axis=1, tiled=True)  48.2 us
    another operation x3, other arithmetic, on_device(): jax.scipy.linalg.solve_triangular(lower_factor, panel_cols.T, lower=True)  40.8 us
    unnamed x36, local copies, waits for them, and re-layouts  34.8 us
    gather x5, local copies, waits for them, and re-layouts, take_rows(): return jnp.take(source, indices, axis=0)  31.8 us
  transfers between devices with their start and end apart: 5, of which 5 were waited for; matrix products, arithmetic and copies ran while one was open for 3% of the time, Pallas kernels for 0%

commit v1 on v0

--- a/solution.py
+++ b/solution.py
@@ -11,18 +11,8 @@
 exact_mode = lax.Precision.HIGHEST
 
 
-def spread_2(shard, axis, root):
-    mine = lax.axis_index(axis) == root
-    return lax.psum(jnp.where(mine, shard, jnp.zeros_like(shard)), axis)
-
-
-def take_rows(source, indices):
+def take_slabs(source, indices):
     return jnp.take(source, indices, axis=0)
-
-
-def place_blocks(arrived, col_source, row_source):
-    picked = jnp.take(arrived, col_source, axis=0)
-    return jnp.take(picked, row_source, axis=1)
 
 
 def on_device(front_matrix, child_schur, child_index, child_valid):
@@ -72,15 +62,17 @@
         col_hit_send.astype(jnp.int32) * jnp.arange(child_colblk)[None, :, None], axis=1
     )
     has_col = jnp.sum(col_hit_send.astype(jnp.float32), axis=1)
+
     blocks = child_schur.reshape(2, child_rowblk, BLK, child_colblk * BLK)
-    outgoing = jax.vmap(take_rows)(blocks, src_row)
+    outgoing = jax.vmap(take_slabs)(blocks, src_row)
     outgoing = outgoing.reshape(2, row_slots * BLK, child_colblk * BLK)
     section_one = lax.all_to_all(outgoing, "row", split_axis=1, concat_axis=1, tiled=True)
-    section_one = section_one.reshape(2, row_slots, BLK, child_colblk, BLK).transpose(0, 3, 1, 2, 4)
-    onward = jax.vmap(take_rows)(section_one, src_col) * has_col[:, :, None, None, None]
-    onward = onward.reshape(2, col_slots * row_slots, BLK * BLK)
+    flipped = jnp.swapaxes(section_one, 1, 2).reshape(2, child_colblk, BLK, row_slots * BLK)
+    onward = jax.vmap(take_slabs)(flipped, src_col) * has_col[:, :, None, None]
+    onward = onward.reshape(2, col_slots * BLK, row_slots * BLK)
     section_two = lax.all_to_all(onward, "col", split_axis=1, concat_axis=1, tiled=True)
-    arrived = section_two.reshape(2, col_slots, row_slots, BLK, BLK)
+    arrived = section_two.reshape(2, col_slots, BLK, row_slots * BLK)
+
     front_rowblk = row_place + row_count * jnp.arange(row_blocks)
     match_rows = (child_index[:, None, :] == front_rowblk[None, :, None]).astype(jnp.int32)
     row_slot_of = sender_row[None, :] * per_owner + row_rank
@@ -91,20 +83,28 @@
     col_slot_of = sender_col[None, :] * col_multi + col_rank
     col_source = jnp.sum(match_cols * col_slot_of[:, None, :], axis=2)
     col_weight = jnp.sum(match_cols.astype(jnp.float32) * validity[:, None, :], axis=2)
-    placed = jax.vmap(place_blocks)(arrived, col_source, row_source)
-    placed = placed * col_weight[:, :, None, None, None] * row_weight[:, None, :, None, None]
-    contributions = placed.transpose(0, 2, 3, 1, 4).reshape(2, local_rows, local_cols)
-    extended = front_matrix + contributions[0] + contributions[1]
+
+    by_col = jax.vmap(take_slabs)(arrived, col_source) * col_weight[:, :, None, None]
+    by_col = by_col.reshape(2, local_cols, row_slots * BLK)
+    unflipped = jnp.swapaxes(by_col, 1, 2).reshape(2, row_slots, BLK, local_cols)
+    placed = jax.vmap(take_slabs)(unflipped, row_source) * row_weight[:, :, None, None]
+    placed = placed.reshape(2, local_rows, local_cols)
+    extended = front_matrix + placed[0] + placed[1]
+
     panel_width = PANEL // BLK
-    columns = []
-    for root_index in range(panel_width):
-        columns.append(spread_2(extended[:, :BLK], "col", root_index))
-    panel_cols = jnp.concatenate(columns, axis=1)
-    corner_rows = []
-    for root_index in range(panel_width):
-        start = root_index // row_count * BLK
-        corner_rows.append(spread_2(panel_cols[start : start + BLK], "row", root_index % row_count))
-    corner = jnp.concatenate(corner_rows, axis=0)
+    spread = col_count // panel_width
+    lead = extended[:, :BLK]
+    lifted = lax.ppermute(
+        lead, "col", [(c, c + panel_width * s) for s in range(1, spread) for c in range(panel_width)]
+    )
+    mine = jnp.where(col_place < panel_width, lead, lifted)
+    part_rows = local_rows // spread
+    part = lax.dynamic_slice_in_dim(mine, (col_place // panel_width) * part_rows, part_rows, axis=0)
+    gathered = lax.all_gather(part, "col", axis=0, tiled=False)
+    gathered = gathered.reshape(spread, panel_width, part_rows, BLK)
+    panel_cols = gathered.transpose(0, 2, 1, 3).reshape(local_rows, PANEL)
+
+    corner = lax.all_gather(panel_cols[: PANEL // row_count], "row", axis=0, tiled=True)
     lower_factor = jnp.linalg.cholesky(corner)
     solved = jax.scipy.linalg.solve_triangular(lower_factor, panel_cols.T, lower=True).T
     logical_blk = jnp.arange(row_blocks) * row_count + row_place
@@ -114,11 +114,18 @@
     panel_factor = jnp.where(in_panel, picked, solved.reshape(row_blocks, BLK, PANEL)).reshape(
         local_rows, PANEL
     )
-    spread = col_count // row_count
-    arranged = panel_factor.reshape(col_blocks, spread, BLK, PANEL)
+
+    ratio = col_count // row_count
+    arranged = panel_factor.reshape(col_blocks, ratio, BLK, PANEL)
     chosen = lax.dynamic_index_in_dim(arranged, col_place // row_count, axis=1, keepdims=False)
     chosen = chosen.reshape(col_blocks * BLK, PANEL)
-    across = spread_2(chosen, "row", col_place % row_count)
+    pairs = []
+    for r0 in range(row_count):
+        for c1 in range(col_count):
+            dest_row = c1 % row_count
+            dest_col = r0 + row_count * (c1 // row_count)
+            pairs.append((r0 * col_count + c1, dest_row * col_count + dest_col))
+    across = lax.ppermute(chosen, ("row", "col"), pairs)
     update = jnp.einsum("rp,cp->rc", panel_factor, across, precision=exact_mode)
     logical_row = jnp.arange(local_rows) // BLK * row_count + row_place
     logical_col = jnp.arange(local_cols) // BLK * col_count + col_place

time: 936 us -> 777 us (0.83)
  the two profiles are of different devices: /device:TPU:1 before, /device:TPU:7 now
where the time goes in v1:
time: 777 us; the launch traced here: 768 us
  waiting for transfers between devices  378 us (49%)
  other arithmetic  166 us (21%)
  local copies, waits for them, and re-layouts  138 us (18%)
  matrix products  46.7 us (6%)
  starting transfers between devices  22 us (3%)
  between operations  17.6 us (2%)
    all_to_all x1, waiting for transfers between devices, on_device(): lax.all_to_all(onward, 'col', split_axis=1, concat_axis=1, tiled=True)  141 us
    all_gather x1, waiting for transfers between devices, on_device(): gathered = lax.all_gather(part, 'col', axis=0, tiled=False)  84.5 us
    another operation x15, other arithmetic, on_device(): lower_factor = jnp.linalg.cholesky(corner)  79.5 us
    ppermute x1, waiting for transfers between devices, on_device(): across = lax.ppermute(chosen, ('row', 'col'), pairs)  75.5 us
    all_to_all x1, waiting for transfers between devices, on_device(): lax.all_to_all(outgoing, 'row', split_axis=1, concat_axis=1, tiled=True)  46.6 us
    another operation x3, other arithmetic, on_device(): jax.scipy.linalg.solve_triangular(lower_factor, panel_cols.T, lower=True)  40.4 us
    gather x8, local copies, waits for them, and re-layouts, take_slabs(): return jnp.take(source, indices, axis=0)  32.2 us
    dot_general x1, matrix products, on_device(): update = jnp.einsum('rp,cp->rc', panel_factor, across, precision=exact_mode)  31.7 us
  transfers between devices with their start and end apart: 6, of which 6 were waited for; matrix products, arithmetic and copies ran while one was open for 2% of the time, Pallas kernels for 0%

profile of v1, /device:TPU:7, one launch (start us, length us, event | category | flops | bytes accessed | tf_op | source)
XLA Modules:
  0.0 768.0 jit_solution(1678104543497816341)
XLA Ops:
  29.0 46.6 %all-to-all-done = f32[2,1024,512]{2,0,1:T(2,128)} async-done(((f32[2,1024,512]{2,0,1:T(2,128)}), f32[2,1024,512]{2,0,1:T(2,128)}, u32[]{:S(2)}, u32[]{:S(2)}) %all-to-all-start) | async-done | bytes 4194336 | tf_op jit(solution)/shard_map/all_to_all | solution.py:69
  93.4 12.9 %copy.128 = f32[2,1024,1024]{2,0,1:T(2,128)} copy(f32[2,1024,1024]{2,1,0:T(8,128)S(1)} %fusion.2) | data formatting | bytes 16777216 | tf_op jit(solution)/shard_map/mul | solution.py:71
  106.3 8.1 %all-to-all-start.1 = ((f32[2,1024,1024]{2,0,1:T(2,128)}), f32[2,1024,1024]{2,0,1:T(2,128)}, u32[]{:S(2)}, u32[]{:S(2)}) async-start(f32[2,1024,1024]{2,0,1:T(2,128)} %copy.128), calls=%async_computation.1 | async-start | bytes 16777216 | tf_op jit(solution)/shard_map/all_to_all | solution.py:73
  115.9 140.9 %all-to-all-done.1 = f32[2,1024,1024]{2,0,1:T(2,128)} async-done(((f32[2,1024,1024]{2,0,1:T(2,128)}), f32[2,1024,1024]{2,0,1:T(2,128)}, u32[]{:S(2)}, u32[]{:S(2)}) %all-to-all-start.1) | async-done | bytes 8388640 | tf_op jit(solution)/shard_map/all_to_all | solution.py:73
  256.8 9.5 %copy.129 = f32[2,1024,1024]{2,1,0:T(8,128)} copy(f32[2,1024,1024]{2,0,1:T(2,128)} %all-to-all-done.1) | data formatting | bytes 16777216 | tf_op jit(solution)/shard_map/all_to_all | solution.py:73
  266.3 7.7 %gather_fusion.5 = f32[32,64,1024]{2,1,0:T(8,128)} fusion(f32[2,16,64,1024]{3,2,1,0:T(8,128)} %bitcast.129, s32[32]{0:T(128)S(1)} %reshape.535), kind=kCustom, calls=%fused_computation.5 | custom fusion | bytes 16777472 | tf_op jit(solution)/shard_map/vmap(jit(_take))/gather | solution.py:15
  280.0 8.7 %copy.130 = f32[2,1024,1024]{2,1,0:T(8,128)} copy(f32[2,1024,1024]{1,2,0:T(8,128)} %fusion.1) | data formatting | bytes 16777216 | tf_op jit(solution)/shard_map/transpose | solution.py:89
  288.7 12.5 %gather_fusion.6 = f32[64,64,1024]{2,1,0:T(8,128)} fusion(f32[2,16,64,1024]{3,2,1,0:T(8,128)} %bitcast.124, s32[64]{0:T(128)S(1)} %reshape.541), kind=kCustom, calls=%fused_computation.6 | custom fusion | bytes 33554944 | tf_op jit(solution)/shard_map/vmap(jit(_take))/gather | solution.py:15
  315.2 9.7 %bitcast_add_fusion = f32[2048,1024]{1,0:T(8,128)S(1)} fusion(f32[1,32,64,1024]{3,2,1,0:T(8,128)} %get-tuple-element.35, f32[2048,1024]{1,0:T(8,128)} %param.4, f32[1,32,64,1024]{3,2,1,0:T(8,128)} %get-tuple-element.34), kind=kLoop, calls=%fused_computation.10 | loop fusion | flops 4194304 | bytes 33554432 | tf_op jit(solution)/shard_map/add | solution.py:92
  330.2 8.5 %collective-permute-done = f32[2048,64]{0,1:T(8,128)S(1)} collective-permute-done((f32[2048,64]{0,1:T(8,128)S(1)}, f32[2048,64]{0,1:T(8,128)S(1)}, u32[]{:S(2)}, u32[]{:S(2)}) %collective-permute-start) | collective-permute-done | bytes 524320 | tf_op jit(solution)/shard_map/ppermute | solution.py:97
  339.9 84.5 %all-gather.6.cloned.1.call-done = f32[16384,64]{1,0:T(8,128)} async-done(((f32[1024,64]{1,0:T(8,128)}), f32[16384,64]{1,0:T(8,128)}) %all-gather.6.cloned.1.call-update) | async-done | bytes 4194320 | tf_op jit(solution)/shard_map/all_gather | solution.py:103
  424.4 9.0 %copy.133 = f32[2,8,1024,64]{2,0,3,1:T(2,128)} copy(f32[2,8,1024,64]{3,2,1,0:T(8,128)} %bitcast.141) | data formatting | bytes 8388608 | tf_op jit(solution)/shard_map/reshape | solution.py:104
  440.8 21.5 %all-gather.4.cloned.1.call-done = f32[512,512]{1,0:T(8,128)} async-done(((f32[64,512]{1,0:T(8,128)}), f32[512,512]{1,0:T(8,128)}) %all-gather.4.cloned.1.call-update) | async-done | bytes 1048592 | tf_op jit(solution)/shard_map/all_gather | solution.py:107
  465.3 11.7 %cholesky.104 = f32[128,128]{1,0:T(8,128)S(1)} custom-call(f32[128,128]{1,0:T(8,128)S(1)} %cholesky.266), custom_call_target="Cholesky" | custom-call | tf_op jit(solution)/shard_map/jit(cholesky)/cholesky | solution.py:108
  477.2 9.8 %custom-call.31 = f32[1,128,128]{1,2,0:T(8,128)S(1)} custom-call(f32[1,128,128]{2,1,0:T(8,128)S(1)} %get-tuple-element.45), custom_call_target="InvertDiagBlocksLowerTriangular" | custom-call | tf_op jit(solution)/shard_map/jit(cholesky)/cholesky | solution.py:108
  487.7 11.9 %cholesky.217 = f32[128,128]{1,0:T(8,128)S(1)} custom-call(f32[128,128]{1,0:T(8,128)S(1)} %cholesky.270), custom_call_target="Cholesky" | custom-call | tf_op jit(solution)/shard_map/jit(cholesky)/cholesky | solution.py:108
  500.9 9.8 %custom-call.32 = f32[1,128,128]{1,2,0:T(8,128)S(1)} custom-call(f32[1,128,128]{2,1,0:T(8,128)S(1)} %get-tuple-element.42), custom_call_target="InvertDiagBlocksLowerTriangular" | custom-call | tf_op jit(solution)/shard_map/jit(cholesky)/cholesky | solution.py:108
  511.4 11.7 %cholesky.238 = f32[128,128]{1,0:T(8,128)S(1)} custom-call(f32[128,128]{1,0:T(8,128)S(1)} %cholesky.275), custom_call_target="Cholesky" | custom-call | tf_op jit(solution)/shard_map/jit(cholesky)/cholesky | solution.py:108
  523.8 9.8 %custom-call.33 = f32[1,128,128]{1,2,0:T(8,128)S(1)} custom-call(f32[1,128,128]{2,1,0:T(8,128)S(1)} %get-tuple-element.39), custom_call_target="InvertDiagBlocksLowerTriangular" | custom-call | tf_op jit(solution)/shard_map/jit(cholesky)/cholesky | solution.py:108
  534.2 11.9 %cholesky.255 = f32[128,128]{1,0:T(8,128)S(1)} custom-call(f32[128,128]{1,0:T(8,128)S(1)} %convolution_subtract_fusion.4), custom_call_target="Cholesky" | custom-call | tf_op jit(solution)/shard_map/jit(cholesky)/cholesky | solution.py:108
  549.7 10.5 %while.1 = (s32[]{:T(128)}, f32[512,512]{1,0:T(8,128)S(1)}, s32[4,2]{0,1:T(2,128)S(1)}, f32[4,128,128]{2,1,0:T(8,128)}, s32[]{:T(128)}) while((s32[]{:T(128)}, f32[512,512]{1,0:T(8,128)S(1)}, s32[4,2]{0,1:T(2,128)S(1)}, f32[4,128,128]{2,1,0:T(8,128)}, s32[]{:T(128)}) %tuple.44), condition=%wide.while_cond, body=%wide.while_body.sunk | while | flops 2 | bytes 132705 | solution.py:109
  560.2 40.2 %custom-call.34 = f32[4,128,128]{1,2,0:T(8,128)S(1)} custom-call(f32[4,128,128]{2,1,0:T(8,128)} %get-tuple-element.9), custom_call_target="InvertDiagBlocksLowerTriangular" | custom-call | tf_op jit(solution)/shard_map/jit(_solve_triangular)/triangular_solve | solution.py:109
  653.5 75.5 %collective-permute-done.1 = f32[1024,512]{1,0:T(8,128)} collective-permute-done((f32[1024,512]{1,0:T(8,128)}, f32[1024,512]{1,0:T(8,128)}, u32[]{:S(2)}, u32[]{:S(2)}) %collective-permute-start.1) | collective-permute-done | bytes 2097184 | tf_op jit(solution)/shard_map/ppermute | solution.py:128
  729.1 31.7 %subtract_select_fusion = f32[2048,1024]{1,0:T(8,128)} fusion(f32[2048,1024]{1,0:T(8,128)} %copy-done, pred[1024]{0:T(1024)(128)(4,1)S(1)} %fusion.54, pred[2048]{0:T(1024)(128)(4,1)S(1)} %fusion.48, f32[2048,512]{0,1:T(8,128)} %select_select_fusion, f32[1024,512]{1,0:T(8,128)} %collective-permute-done.1), kind=kOutput, calls=%fused_computation.17 | convolution fusion | flops 12891193344 | bytes 23071744 | tf_op jit(solution)/shard_map/rp,cp->rc/dot_general | solution.py:129
  (161 shorter events, 146.3 us)
Async XLA Ops:
  23.4 52.2 %all-to-all-start = ((f32[2,1024,512]{2,0,1:T(2,128)}), f32[2,1024,512]{2,0,1:T(2,128)}, u32[]{:S(2)}, u32[]{:S(2)}) async-start(f32[2,1024,512]{2,0,1:T(2,128)} %copy.126), calls=%async_computation | async-start | bytes 8388608 | tf_op jit(solution)/shard_map/all_to_all | solution.py:69
  106.3 8.3 %copy-start.7 = (s32[2,128]{1,0:T(2,128)S(1)}, s32[2,128]{1,0:T(2,128)}, u32[]{:S(2)}) copy-start(s32[2,128]{1,0:T(2,128)} %param.6) | copy-start | bytes 3076
  106.3 8.8 %copy-start.8 = (s32[2,128]{1,0:T(2,128)S(1)}, s32[2,128]{1,0:T(2,128)}, u32[]{:S(2)}) copy-start(s32[2,128]{1,0:T(2,128)} %param.7) | copy-start | bytes 3076
  106.3 150.5 %all-to-all-start.1 = ((f32[2,1024,1024]{2,0,1:T(2,128)}), f32[2,1024,1024]{2,0,1:T(2,128)}, u32[]{:S(2)}, u32[]{:S(2)}) async-start(f32[2,1024,1024]{2,0,1:T(2,128)} %copy.128), calls=%async_computation.1 | async-start | bytes 16777216 | tf_op jit(solution)/shard_map/all_to_all | solution.py:73
  114.4 310.0 %all-gather.6.cloned.1.call-start = ((), (), s32[]{:S(2)}) async-start(), calls=%async_computation.3 | async-start | bytes 8912896 | tf_op jit(solution)/shard_map/all_gather | solution.py:103
  325.0 3.4 copy-start
  328.8 9.9 %collective-permute-start = (f32[2048,64]{0,1:T(8,128)S(1)}, f32[2048,64]{0,1:T(8,128)S(1)}, u32[]{:S(2)}, u32[]{:S(2)}) collective-permute-start(f32[2048,64]{0,1:T(8,128)S(1)} %copy.131), channel_id=1, source_target_pairs={{0,8},{1,9},{2,10},{3,11},{4,12},{5,13},{6,14},{7,15},{16,24},{17,... | collective-permute-start | bytes 1572872 | tf_op jit(solution)/shard_map/ppermute | solution.py:97
  339.8 122.5 %all-gather.4.cloned.1.call-start = ((), (), s32[]{:S(2)}) async-start(), calls=%async_computation.2 | async-start | bytes 1179648 | tf_op jit(solution)/shard_map/all_gather | solution.py:107
  437.6 2.0 copy-start.1
  560.2 42.6 %copy-start.6 = (f32[512,512]{1,0:T(8,128)}, f32[512,512]{1,0:T(8,128)S(1)}, u32[]{:S(2)}) copy-start(f32[512,512]{1,0:T(8,128)S(1)} %get-tuple-element.112) | copy-start | bytes 3145732
  600.4 5.7 copy-start.2
  609.4 4.2 copy-start.3
  613.7 1.1 copy-start.5
  629.5 99.5 %collective-permute-start.1 = (f32[1024,512]{1,0:T(8,128)}, f32[1024,512]{1,0:T(8,128)}, u32[]{:S(2)}, u32[]{:S(2)}) collective-permute-start(f32[1024,512]{1,0:T(8,128)} %bitcast.40), channel_id=1, source_target_pairs={{0,0},{1,16},{2,32},{3,48},{4,64},{5,80},{6,96},{7,112},{8,8},{9,2... | collective-permute-start | bytes 6291464 | tf_op jit(solution)/shard_map/ppermute | solution.py:128
  637.1 5.7 copy-start.4
Sparse Core Ops, SparseCore 0:
  339.9 84.4 all-gather.5
  440.5 21.7 all-gather.3

commit v2 on v1

--- a/solution.py
+++ b/solution.py
@@ -64,14 +64,16 @@
     has_col = jnp.sum(col_hit_send.astype(jnp.float32), axis=1)
 
     blocks = child_schur.reshape(2, child_rowblk, BLK, child_colblk * BLK)
-    outgoing = jax.vmap(take_slabs)(blocks, src_row)
-    outgoing = outgoing.reshape(2, row_slots * BLK, child_colblk * BLK)
-    section_one = lax.all_to_all(outgoing, "row", split_axis=1, concat_axis=1, tiled=True)
-    flipped = jnp.swapaxes(section_one, 1, 2).reshape(2, child_colblk, BLK, row_slots * BLK)
-    onward = jax.vmap(take_slabs)(flipped, src_col) * has_col[:, :, None, None]
-    onward = onward.reshape(2, col_slots * BLK, row_slots * BLK)
-    section_two = lax.all_to_all(onward, "col", split_axis=1, concat_axis=1, tiled=True)
-    arrived = section_two.reshape(2, col_slots, BLK, row_slots * BLK)
+    arrived = []
+    for k in range(2):
+        outgoing = take_slabs(blocks[k], src_row[k]).reshape(row_slots * BLK, child_colblk * BLK)
+        section_one = lax.all_to_all(outgoing, "row", split_axis=0, concat_axis=0, tiled=True)
+        flipped = section_one.T.reshape(child_colblk, BLK, row_slots * BLK)
+        onward = take_slabs(flipped, src_col[k]) * has_col[k][:, None, None]
+        onward = onward.reshape(col_slots * BLK, row_slots * BLK)
+        section_two = lax.all_to_all(onward, "col", split_axis=0, concat_axis=0, tiled=True)
+        arrived.append(section_two.reshape(col_slots, BLK, row_slots * BLK))
+    arrived = jnp.stack(arrived)
 
     front_rowblk = row_place + row_count * jnp.arange(row_blocks)
     match_rows = (child_index[:, None, :] == front_rowblk[None, :, None]).astype(jnp.int32)
@@ -100,13 +102,17 @@
     mine = jnp.where(col_place < panel_width, lead, lifted)
     part_rows = local_rows // spread
     part = lax.dynamic_slice_in_dim(mine, (col_place // panel_width) * part_rows, part_rows, axis=0)
+    part = part.reshape(part_rows * BLK // 128, 128)
     gathered = lax.all_gather(part, "col", axis=0, tiled=False)
     gathered = gathered.reshape(spread, panel_width, part_rows, BLK)
     panel_cols = gathered.transpose(0, 2, 1, 3).reshape(local_rows, PANEL)
 
     corner = lax.all_gather(panel_cols[: PANEL // row_count], "row", axis=0, tiled=True)
     lower_factor = jnp.linalg.cholesky(corner)
-    solved = jax.scipy.linalg.solve_triangular(lower_factor, panel_cols.T, lower=True).T
+    inverse = jax.scipy.linalg.solve_triangular(
+        lower_factor, jnp.eye(PANEL, dtype=lower_factor.dtype), lower=True
+    )
+    solved = jnp.einsum("rp,qp->rq", panel_cols, inverse, precision=exact_mode)
     logical_blk = jnp.arange(row_blocks) * row_count + row_place
     factor_blocks = lower_factor.reshape(panel_width, BLK, PANEL)
     picked = jnp.take(factor_blocks, jnp.minimum(logical_blk, panel_width - 1), axis=0)
@@ -125,7 +131,10 @@
             dest_row = c1 % row_count
             dest_col = r0 + row_count * (c1 // row_count)
             pairs.append((r0 * col_count + c1, dest_row * col_count + dest_col))
-    across = lax.ppermute(chosen, ("row", "col"), pairs)
+    piece_rows = chosen.shape[0] // row_count
+    piece = lax.dynamic_slice_in_dim(chosen, (col_place % row_count) * piece_rows, piece_rows, axis=0)
+    piece = lax.ppermute(piece, ("row", "col"), pairs)
+    across = lax.all_gather(piece, "row", axis=0, tiled=True)
     update = jnp.einsum("rp,cp->rc", panel_factor, across, precision=exact_mode)
     logical_row = jnp.arange(local_rows) // BLK * row_count + row_place
     logical_col = jnp.arange(local_cols) // BLK * col_count + col_place

time: 777 us -> 640 us (0.82)
  the two profiles are of different devices: /device:TPU:7 before, /device:TPU:1 now
where the time goes in v2:
time: 640 us; the launch traced here: 634 us
  waiting for transfers between devices  243 us (38%)
  other arithmetic  172 us (27%)
  local copies, waits for them, and re-layouts  123 us (19%)
  matrix products  41.4 us (6%)
  starting transfers between devices  37.4 us (6%)
  between operations  17.2 us (3%)
    all_to_all x2, waiting for transfers between devices, on_device(): lax.all_to_all(onward, 'col', split_axis=0, concat_axis=0, tiled=True)  97.4 us
    another operation x15, other arithmetic, on_device(): lower_factor = jnp.linalg.cholesky(corner)  79.2 us
    all_gather x1, waiting for transfers between devices, on_device(): gathered = lax.all_gather(part, 'col', axis=0, tiled=False)  59.1 us
    another operation x3, other arithmetic, on_device(): jax.scipy.linalg.solve_triangular(lower_factor, jnp.eye(PANEL, dtype=lowe...  41.6 us
    all_gather x1, waiting for transfers between devices, on_device(): across = lax.all_gather(piece, 'row', axis=0, tiled=True)  35.8 us
    all_to_all x2, waiting for transfers between devices, on_device(): lax.all_to_all(outgoing, 'row', split_axis=0, concat_axis=0, tiled=True)  35.5 us
    gather x8, local copies, waits for them, and re-layouts, take_slabs(): return jnp.take(source, indices, axis=0)  31.9 us
    transpose x2, local copies, waits for them, and re-layouts, on_device(): panel_cols = gathered.transpose(0, 2, 1, 3).reshape(local_rows, PANEL)  20.1 us
  transfers between devices with their start and end apart: 9, of which 9 were waited for; matrix products, arithmetic and copies ran while one was open for 7% of the time, Pallas kernels for 0%

profile of v2, /device:TPU:1, one launch (start us, length us, event | category | flops | bytes accessed | tf_op | source)
XLA Modules:
  0.0 634.2 jit_solution(8023197945735742555)
XLA Ops:
  31.8 19.3 %all-to-all-done = f32[8,128,512]{2,1,0:T(8,128)S(1)} async-done(((f32[8,128,512]{2,1,0:T(8,128)}), f32[8,128,512]{2,1,0:T(8,128)S(1)}, u32[]{:S(2)}, u32[]{:S(2)}) %all-to-all-start) | async-done | bytes 2097184 | tf_op jit(solution)/shard_map/all_to_all | solution.py:70
  66.4 16.2 %all-to-all-done.2 = f32[8,128,512]{2,1,0:T(8,128)} async-done(((f32[8,128,512]{2,1,0:T(8,128)}), f32[8,128,512]{2,1,0:T(8,128)}, u32[]{:S(2)}, u32[]{:S(2)}) %all-to-all-start.2) | async-done | bytes 2097184 | tf_op jit(solution)/shard_map/all_to_all | solution.py:70
  100.4 48.1 %all-to-all-done.1 = f32[16,64,1024]{2,1,0:T(8,128)} async-done(((f32[16,64,1024]{2,1,0:T(8,128)}), f32[16,64,1024]{2,1,0:T(8,128)}, u32[]{:S(2)}, u32[]{:S(2)}) %all-to-all-start.1) | async-done | bytes 4194336 | tf_op jit(solution)/shard_map/all_to_all | solution.py:74
  148.5 11.2 %all-to-all-start.3 = ((f32[16,64,1024]{2,1,0:T(8,128)}), f32[16,64,1024]{2,1,0:T(8,128)}, u32[]{:S(2)}, u32[]{:S(2)}) async-start(f32[16,64,1024]{2,1,0:T(8,128)} %select_multiply_fusion.1), calls=%async_computation.3 | async-start | bytes 8388608 | tf_op jit(solution)/shard_map/all_to_all | solution.py:74
  161.2 49.4 %all-to-all-done.3 = f32[16,64,1024]{2,1,0:T(8,128)} async-done(((f32[16,64,1024]{2,1,0:T(8,128)}), f32[16,64,1024]{2,1,0:T(8,128)}, u32[]{:S(2)}, u32[]{:S(2)}) %all-to-all-start.3) | async-done | bytes 4194336 | tf_op jit(solution)/shard_map/all_to_all | solution.py:74
  210.6 8.5 %pad_maximum_fusion = f32[2,16,64,1024]{3,2,1,0:T(8,128)} fusion(f32[1,16,64,1024]{3,2,1,0:T(8,128)} %bitcast.21, f32[1,16,64,1024]{3,2,1,0:T(8,128)} %bitcast.12), kind=kLoop, calls=%fused_computation.12 | loop fusion | flops 2097152 | bytes 16777216 | tf_op jit(solution)/shard_map/stack | solution.py:76
  232.8 8.7 %copy.137 = f32[2,1024,1024]{2,1,0:T(8,128)} copy(f32[2,1024,1024]{1,2,0:T(8,128)} %fusion.1) | data formatting | bytes 16777216 | tf_op jit(solution)/shard_map/transpose | solution.py:91
  241.5 12.5 %gather_fusion.4 = f32[64,64,1024]{2,1,0:T(8,128)} fusion(f32[2,16,64,1024]{3,2,1,0:T(8,128)} %bitcast.133, s32[64]{0:T(128)S(1)} %reshape.540), kind=kCustom, calls=%fused_computation.8 | custom fusion | bytes 33554944 | tf_op jit(solution)/shard_map/vmap(jit(_take))/gather | solution.py:15
  268.0 9.7 %bitcast_add_fusion = f32[2048,1024]{1,0:T(8,128)S(1)} fusion(f32[1,32,64,1024]{3,2,1,0:T(8,128)} %get-tuple-element.33, f32[2048,1024]{1,0:T(8,128)} %param.8, f32[1,32,64,1024]{3,2,1,0:T(8,128)} %get-tuple-element.32), kind=kLoop, calls=%fused_computation.13 | loop fusion | flops 4194304 | bytes 33554432 | tf_op jit(solution)/shard_map/add | solution.py:94
  292.3 59.1 %all-gather.4.cloned.1.call-done = f32[16,512,128]{2,1,0:T(8,128)} async-done(((f32[1,512,128]{2,1,0:T(8,128)}), f32[16,512,128]{2,1,0:T(8,128)}) %all-gather.4.cloned.1.call-update) | async-done | bytes 4194320 | tf_op jit(solution)/shard_map/all_gather | solution.py:106
  358.4 8.6 %copy.140 = f32[2,1024,8,64]{1,0,3,2:T(2,128)} copy(f32[2,1024,8,64]{3,1,2,0:T(8,128)} %bitcast.131) | data formatting | bytes 8388608 | tf_op jit(solution)/shard_map/transpose | solution.py:108
  372.7 11.4 %copy.143 = f32[2,1024,8,64]{3,2,1,0:T(8,128)} copy(f32[2,1024,8,64]{3,1,2,0:T(8,128)} %bitcast.132) | data formatting | bytes 8388608 | tf_op jit(solution)/shard_map/transpose | solution.py:108
  398.5 11.7 %cholesky.104 = f32[128,128]{1,0:T(8,128)S(1)} custom-call(f32[128,128]{1,0:T(8,128)S(1)} %cholesky.266), custom_call_target="Cholesky" | custom-call | tf_op jit(solution)/shard_map/jit(cholesky)/cholesky | solution.py:111
  410.4 9.8 %custom-call.31 = f32[1,128,128]{1,2,0:T(8,128)S(1)} custom-call(f32[1,128,128]{2,1,0:T(8,128)S(1)} %get-tuple-element.45), custom_call_target="InvertDiagBlocksLowerTriangular" | custom-call | tf_op jit(solution)/shard_map/jit(cholesky)/cholesky | solution.py:111
  422.7 11.7 %cholesky.217 = f32[128,128]{1,0:T(8,128)S(1)} custom-call(f32[128,128]{1,0:T(8,128)S(1)} %cholesky.270), custom_call_target="Cholesky" | custom-call | tf_op jit(solution)/shard_map/jit(cholesky)/cholesky | solution.py:111
  435.8 9.9 %custom-call.32 = f32[1,128,128]{1,2,0:T(8,128)S(1)} custom-call(f32[1,128,128]{2,1,0:T(8,128)S(1)} %get-tuple-element.42), custom_call_target="InvertDiagBlocksLowerTriangular" | custom-call | tf_op jit(solution)/shard_map/jit(cholesky)/cholesky | solution.py:111
  447.3 11.7 %cholesky.238 = f32[128,128]{1,0:T(8,128)S(1)} custom-call(f32[128,128]{1,0:T(8,128)S(1)} %cholesky.275), custom_call_target="Cholesky" | custom-call | tf_op jit(solution)/shard_map/jit(cholesky)/cholesky | solution.py:111
  459.8 9.8 %custom-call.33 = f32[1,128,128]{1,2,0:T(8,128)S(1)} custom-call(f32[1,128,128]{2,1,0:T(8,128)S(1)} %get-tuple-element.39), custom_call_target="InvertDiagBlocksLowerTriangular" | custom-call | tf_op jit(solution)/shard_map/jit(cholesky)/cholesky | solution.py:111
  471.0 11.7 %cholesky.255 = f32[128,128]{1,0:T(8,128)S(1)} custom-call(f32[128,128]{1,0:T(8,128)S(1)} %convolution_subtract_fusion.5), custom_call_target="Cholesky" | custom-call | tf_op jit(solution)/shard_map/jit(cholesky)/cholesky | solution.py:111
  487.4 13.8 %while.1 = (s32[]{:T(128)}, f32[512,512]{1,0:T(8,128)}, s32[4,2]{0,1:T(2,128)S(1)}, f32[4,128,128]{2,1,0:T(8,128)}, s32[]{:T(128)}) while((s32[]{:T(128)}, f32[512,512]{1,0:T(8,128)}, s32[4,2]{0,1:T(2,128)S(1)}, f32[4,128,128]{2,1,0:T(8,128)}, s32[]{:T(128)}) %tuple.52), condition=%wide.while_cond, body=%wide.while_body.sunk | while | flops 2 | bytes 132705 | solution.py:112
  501.2 40.1 %custom-call.34 = f32[4,128,128]{1,2,0:T(8,128)S(1)} custom-call(f32[4,128,128]{2,1,0:T(8,128)} %get-tuple-element.11), custom_call_target="InvertDiagBlocksLowerTriangular" | custom-call | tf_op jit(solution)/shard_map/jit(_solve_triangular)/triangular_solve | solution.py:112
  551.6 9.6 %select_select_fusion = f32[32,64,512]{2,1,0:T(8,128)S(1)} fusion(f32[32,64,512]{2,1,0:T(8,128)} %gather_fusion.2, f32[32,64,512]{2,1,0:T(8,128)} %dot_general.8, pred[32]{0:T(512)(128)(4,1)S(1)} %get-tuple-element.64, pred[32]{0:T(512)(128)(4,1)S(1)} %get-tuple-element.65, f32[128,512]{1,0:T(8,128)S(1)} %fusion.29, f32[128,512]{1,0:T(8,128)S(1)} %fusion.30, ...), kind=kOutput, calls=%fused_computation.21 | convolution fusion | flops 6445334528 | bytes 13631552 | tf_op jit(solution)/shard_map/rp,qp->rq/dot_general | solution.py:115
  572.6 35.8 %all-gather.8.cloned.1.call-done = f32[1024,512]{1,0:T(8,128)} async-done(((f32[128,512]{1,0:T(8,128)}), f32[1024,512]{1,0:T(8,128)}) %all-gather.8.cloned.1.call-update) | async-done | bytes 2097168 | tf_op jit(solution)/shard_map/all_gather | solution.py:137
  608.4 19.0 %subtract_select_fusion = f32[2048,1024]{1,0:T(8,128)} fusion(f32[2048,1024]{1,0:T(8,128)} %copy-done, pred[1024]{0:T(1024)(128)(4,1)S(1)} %fusion.56, pred[2048]{0:T(1024)(128)(4,1)S(1)} %fusion.50, f32[2048,512]{1,0:T(8,128)} %bitcast.136, f32[1024,512]{1,0:T(8,128)} %all-gather.8.cloned.1.call-done), kind=kOutput, calls=%fused_computation.18 | convolution fusion | flops 12891193344 | bytes 23071744 | tf_op jit(solution)/shard_map/rp,cp->rc/dot_general | solution.py:138
  (159 shorter events, 173.3 us)
Async XLA Ops:
  19.1 32.0 %all-to-all-start = ((f32[8,128,512]{2,1,0:T(8,128)}), f32[8,128,512]{2,1,0:T(8,128)S(1)}, u32[]{:S(2)}, u32[]{:S(2)}) async-start(f32[8,128,512]{2,1,0:T(8,128)} %bitcast.145), calls=%async_computation | async-start | bytes 4194304 | tf_op jit(solution)/shard_map/all_to_all | solution.py:70
  51.1 5.3 copy-start.2
  51.1 31.5 %all-to-all-start.2 = ((f32[8,128,512]{2,1,0:T(8,128)}), f32[8,128,512]{2,1,0:T(8,128)}, u32[]{:S(2)}, u32[]{:S(2)}) async-start(f32[8,128,512]{2,1,0:T(8,128)} %bitcast.144), calls=%async_computation.2 | async-start | bytes 4194304 | tf_op jit(solution)/shard_map/all_to_all | solution.py:70
  82.6 65.9 %all-to-all-start.1 = ((f32[16,64,1024]{2,1,0:T(8,128)}), f32[16,64,1024]{2,1,0:T(8,128)}, u32[]{:S(2)}, u32[]{:S(2)}) async-start(f32[16,64,1024]{2,1,0:T(8,128)} %select_multiply_fusion.2), calls=%async_computation.1 | async-start | bytes 8388608 | tf_op jit(solution)/shard_map/all_to_all | solution.py:74
  100.4 59.5 %copy-start.6 = (s32[2,128]{1,0:T(2,128)S(1)}, s32[2,128]{1,0:T(2,128)}, u32[]{:S(2)}) copy-start(s32[2,128]{1,0:T(2,128)} %param.10) | copy-start | bytes 3076
  100.4 60.0 %copy-start.7 = (s32[2,128]{1,0:T(2,128)S(1)}, s32[2,128]{1,0:T(2,128)}, u32[]{:S(2)}) copy-start(s32[2,128]{1,0:T(2,128)} %param.11) | copy-start | bytes 3076
  148.5 62.1 %all-to-all-start.3 = ((f32[16,64,1024]{2,1,0:T(8,128)}), f32[16,64,1024]{2,1,0:T(8,128)}, u32[]{:S(2)}, u32[]{:S(2)}) async-start(f32[16,64,1024]{2,1,0:T(8,128)} %select_multiply_fusion.1), calls=%async_computation.3 | async-start | bytes 8388608 | tf_op jit(solution)/shard_map/all_to_all | solution.py:74
  159.7 191.7 %all-gather.4.cloned.1.call-start = ((), (), s32[]{:S(2)}) async-start(), calls=%async_computation.4 | async-start | bytes 4456448 | tf_op jit(solution)/shard_map/all_gather | solution.py:106
  277.8 3.4 copy-start
  281.7 9.4 %collective-permute-start = (f32[2048,64]{0,1:T(8,128)S(1)}, f32[2048,64]{0,1:T(8,128)S(1)}, u32[]{:S(2)}, u32[]{:S(2)}) collective-permute-start(f32[2048,64]{0,1:T(8,128)S(1)} %copy.138), channel_id=1, source_target_pairs={{0,8},{1,9},{2,10},{3,11},{4,12},{5,13},{6,14},{7,15},{16,24},{17,... | collective-permute-start | bytes 1572872 | tf_op jit(solution)/shard_map/ppermute | solution.py:99
  292.2 103.2 %all-gather.6.cloned.1.call-start = ((), (), s32[]{:S(2)}) async-start(), calls=%async_computation.5 | async-start | bytes 1179648 | tf_op jit(solution)/shard_map/all_gather | solution.py:110
  371.9 236.5 %all-gather.8.cloned.1.call-start = ((), (), s32[]{:S(2)}) async-start(), calls=%async_computation.6 | async-start | bytes 2359296 | tf_op jit(solution)/shard_map/all_gather | solution.py:137
  398.4 11.7 %copy-start.3 = (f32[512,512]{1,0:T(8,128)}, f32[512,512]{1,0:T(8,128)S(1)}, u32[]{:S(2)}) copy-start(f32[512,512]{1,0:T(8,128)S(1)} %fusion.8) | copy-start | bytes 3145732
  541.3 1.6 copy-start.4
  561.2 2.0 copy-start.1
  563.5 8.4 %collective-permute-start.1 = (f32[128,512]{1,0:T(8,128)S(1)}, f32[128,512]{1,0:T(8,128)S(1)}, u32[]{:S(2)}, u32[]{:S(2)}) collective-permute-start(f32[128,512]{1,0:T(8,128)S(1)} %constant_dynamic-slice_fusion.3), channel_id=1, source_target_pairs={{0,0},{1,16},{2,32},{3,48},{4,64},{5,80},{6,96},{7,112},{8,8},{9,2... | collective-permute-start | bytes 786440 | tf_op jit(solution)/shard_map/ppermute | solution.py:136
  571.9 0.7 copy-start.5
Sparse Core Ops, SparseCore 0:
  292.4 58.9 all-gather.3
  372.1 23.3 all-gather.5
  572.7 35.6 all-gather.7

commit v3 on v2

--- a/solution.py
+++ b/solution.py
@@ -63,15 +63,50 @@
     )
     has_col = jnp.sum(col_hit_send.astype(jnp.float32), axis=1)
 
+    panel_width = PANEL // BLK
+    corner_blk = jnp.arange(panel_width)
+    row_hit = (jnp.take(child_index, local_arow, axis=1)[:, None, :] == corner_blk[None, :, None])
+    corner_rpick = jnp.sum(row_hit.astype(jnp.int32) * jnp.arange(child_rowblk)[None, None, :], axis=2)
+    corner_rw = jnp.sum(
+        row_hit.astype(jnp.float32) * jnp.take(validity, local_arow, axis=1)[:, None, :], axis=2
+    )
+    col_hit = (jnp.take(child_index, local_bcol, axis=1)[:, None, :] == corner_blk[None, :, None])
+    corner_cpick = jnp.sum(col_hit.astype(jnp.int32) * jnp.arange(child_colblk)[None, None, :], axis=2)
+    corner_cw = jnp.sum(
+        col_hit.astype(jnp.float32) * jnp.take(validity, local_bcol, axis=1)[:, None, :], axis=2
+    )
+    own = jnp.where(col_place < panel_width, front_matrix[:BLK, :BLK], jnp.zeros((BLK, BLK), jnp.float32))
+    partial = lax.dynamic_update_slice(
+        jnp.zeros((PANEL, PANEL), jnp.float32),
+        own,
+        (row_place * BLK, jnp.minimum(col_place, panel_width - 1) * BLK),
+    )
+    for k in range(2):
+        rows_k = take_slabs(child_schur[k].reshape(child_rowblk, BLK, -1), corner_rpick[k])
+        rows_k = (rows_k * corner_rw[k][:, None, None]).reshape(PANEL, child_colblk, BLK)
+        cols_k = jnp.take(rows_k, corner_cpick[k], axis=1) * corner_cw[k][None, :, None]
+        partial = partial + cols_k.reshape(PANEL, PANEL)
+    corner = lax.psum(partial, ("row", "col"))
+
     blocks = child_schur.reshape(2, child_rowblk, BLK, child_colblk * BLK)
     arrived = []
     for k in range(2):
         outgoing = take_slabs(blocks[k], src_row[k]).reshape(row_slots * BLK, child_colblk * BLK)
+        if k == 0:
+            outgoing, corner = lax.optimization_barrier((outgoing, corner))
+            lower_factor = jnp.linalg.cholesky(corner)
+            inverse = jax.scipy.linalg.solve_triangular(
+                lower_factor, jnp.eye(PANEL, dtype=lower_factor.dtype), lower=True
+            )
         section_one = lax.all_to_all(outgoing, "row", split_axis=0, concat_axis=0, tiled=True)
         flipped = section_one.T.reshape(child_colblk, BLK, row_slots * BLK)
         onward = take_slabs(flipped, src_col[k]) * has_col[k][:, None, None]
         onward = onward.reshape(col_slots * BLK, row_slots * BLK)
         section_two = lax.all_to_all(onward, "col", split_axis=0, concat_axis=0, tiled=True)
+        if k == 1:
+            section_two, lower_factor, inverse = lax.optimization_barrier(
+                (section_two, lower_factor, inverse)
+            )
         arrived.append(section_two.reshape(col_slots, BLK, row_slots * BLK))
     arrived = jnp.stack(arrived)
 
@@ -93,7 +128,6 @@
     placed = placed.reshape(2, local_rows, local_cols)
     extended = front_matrix + placed[0] + placed[1]
 
-    panel_width = PANEL // BLK
     spread = col_count // panel_width
     lead = extended[:, :BLK]
     lifted = lax.ppermute(
@@ -107,11 +141,6 @@
     gathered = gathered.reshape(spread, panel_width, part_rows, BLK)
     panel_cols = gathered.transpose(0, 2, 1, 3).reshape(local_rows, PANEL)
 
-    corner = lax.all_gather(panel_cols[: PANEL // row_count], "row", axis=0, tiled=True)
-    lower_factor = jnp.linalg.cholesky(corner)
-    inverse = jax.scipy.linalg.solve_triangular(
-        lower_factor, jnp.eye(PANEL, dtype=lower_factor.dtype), lower=True
-    )
     solved = jnp.einsum("rp,qp->rq", panel_cols, inverse, precision=exact_mode)
     logical_blk = jnp.arange(row_blocks) * row_count + row_place
     factor_blocks = lower_factor.reshape(panel_width, BLK, PANEL)

time: 640 us -> 680 us (1.062)
  waiting for transfers between devices: 243 us -> 263 us
  local copies, waits for them, and re-layouts: 123 us -> 137 us
  other arithmetic: 172 us -> 183 us
    psum x0 -> x1, waiting for transfers between devices: none -> 146 us  [on_device(): corner = lax.psum(partial, ('row', 'col'))]
    all_to_all x2, waiting for transfers between devices: 97.4 us -> 0.01 us  [on_device(): lax.all_to_all(onward, 'col', split_axis=0, concat_axis=0, tiled=True)]
    all_to_all x2, waiting for transfers between devices: 35.5 us -> 15.5 us  [on_device(): lax.all_to_all(outgoing, 'row', split_axis=0, concat_axis=0, tiled=True)]
    reshape x0 -> x4, local copies, waits for them, and re-layouts: none -> 8.77 us  [on_device(): (rows_k * corner_rw[k][:, None, None]).reshape(PANEL, child_colblk, BLK)]
    transpose x2 -> x1, local copies, waits for them, and re-layouts: 20.1 us -> 11.4 us  [on_device(): panel_cols = gathered.transpose(0, 2, 1, 3).reshape(local_rows, PANEL)]
    all_to_all x2, starting transfers between devices: 19 us -> 12 us  [on_device(): lax.all_to_all(onward, 'col', split_axis=0, concat_axis=0, tiled=True)]
    all_gather x1, waiting for transfers between devices: 59.1 us -> 52.1 us  [on_device(): gathered = lax.all_gather(part, 'col', axis=0, tiled=False)]
    gather x8 -> x10, local copies, waits for them, and re-layouts: 31.9 us -> 36.8 us  [take_slabs(): return jnp.take(source, indices, axis=0)]
  transfers between devices with their start and end apart: 9 -> 9, of which waited for: 9 -> 6; matrix products, arithmetic and copies ran while one was open for 7% -> 31% of each run, Pallas kernels for 0% -> 0%
where the time goes in v3:
time: 680 us; the launch traced here: 672 us
  waiting for transfers between devices  263 us (39%)
  other arithmetic  183 us (27%)
  local copies, waits for them, and re-layouts  137 us (20%)
  matrix products  39.8 us (6%)
  starting transfers between devices  31.4 us (5%)
  between operations  17.5 us (3%)
    psum x1, waiting for transfers between devices, on_device(): corner = lax.psum(partial, ('row', 'col'))  146 us
    another operation x15, other arithmetic, on_device(): lower_factor = jnp.linalg.cholesky(corner)  79.4 us
    all_gather x1, waiting for transfers between devices, on_device(): gathered = lax.all_gather(part, 'col', axis=0, tiled=False)  52.1 us
    another operation x4, other arithmetic, on_device(): jax.scipy.linalg.solve_triangular(lower_factor, jnp.eye(PANEL, dtype=lowe...  41.4 us
    gather x10, local copies, waits for them, and re-layouts, take_slabs(): return jnp.take(source, indices, axis=0)  36.8 us
    all_gather x1, waiting for transfers between devices, on_device(): across = lax.all_gather(piece, 'row', axis=0, tiled=True)  36 us
    dot_general x1, matrix products, on_device(): update = jnp.einsum('rp,cp->rc', panel_factor, across, precision=exact_mode)  19 us
    all_to_all x2, waiting for transfers between devices, on_device(): lax.all_to_all(outgoing, 'row', split_axis=0, concat_axis=0, tiled=True)  15.5 us
  transfers between devices with their start and end apart: 9, of which 6 were waited for; matrix products, arithmetic and copies ran while one was open for 31% of the time, Pallas kernels for 0%

profile of v3, /device:TPU:1, one launch (start us, length us, event | category | flops | bytes accessed | tf_op | source)
XLA Modules:
  0.0 671.9 jit_solution(6912003081059378645)
XLA Ops:
  64.0 146.1 %all-reduce.3.cloned.1.call-done = f32[512,512]{0,1:T(8,128)} async-done(((f32[512,512]{0,1:T(8,128)}), f32[512,512]{0,1:T(8,128)}) %all-reduce.3.cloned.1.call-update) | async-done | bytes 1048592 | tf_op jit(solution)/shard_map/psum | solution.py:89
  226.9 15.5 %all-to-all-done = f32[8,128,512]{1,2,0:T(8,128)} async-done(((f32[8,128,512]{1,2,0:T(8,128)}), f32[8,128,512]{1,2,0:T(8,128)}, u32[]{:S(2)}, u32[]{:S(2)}) %all-to-all-start) | async-done | bytes 2097184 | tf_op jit(solution)/shard_map/all_to_all | solution.py:101
  251.3 11.7 %cholesky.103 = f32[128,128]{1,0:T(8,128)S(1)} custom-call(f32[128,128]{1,0:T(8,128)S(1)} %cholesky.263), custom_call_target="Cholesky" | custom-call | tf_op jit(solution)/shard_map/jit(cholesky)/cholesky | solution.py:97
  263.1 9.8 %custom-call.31 = f32[1,128,128]{1,2,0:T(8,128)S(1)} custom-call(f32[1,128,128]{2,1,0:T(8,128)S(1)} %get-tuple-element.67), custom_call_target="InvertDiagBlocksLowerTriangular" | custom-call | tf_op jit(solution)/shard_map/jit(cholesky)/cholesky | solution.py:97
  275.5 11.7 %cholesky.215 = f32[128,128]{1,0:T(8,128)S(1)} custom-call(f32[128,128]{1,0:T(8,128)S(1)} %cholesky.267), custom_call_target="Cholesky" | custom-call | tf_op jit(solution)/shard_map/jit(cholesky)/cholesky | solution.py:97
  287.2 10.2 %custom-call.32 = f32[1,128,128]{1,2,0:T(8,128)S(1)} custom-call(f32[1,128,128]{2,1,0:T(8,128)S(1)} %get-tuple-element.64), custom_call_target="InvertDiagBlocksLowerTriangular" | custom-call | tf_op jit(solution)/shard_map/jit(cholesky)/cholesky | solution.py:97
  299.0 11.7 %cholesky.236 = f32[128,128]{1,0:T(8,128)S(1)} custom-call(f32[128,128]{1,0:T(8,128)S(1)} %cholesky.272), custom_call_target="Cholesky" | custom-call | tf_op jit(solution)/shard_map/jit(cholesky)/cholesky | solution.py:97
  310.8 9.8 %custom-call.33 = f32[1,128,128]{1,2,0:T(8,128)S(1)} custom-call(f32[1,128,128]{2,1,0:T(8,128)S(1)} %get-tuple-element.61), custom_call_target="InvertDiagBlocksLowerTriangular" | custom-call | tf_op jit(solution)/shard_map/jit(cholesky)/cholesky | solution.py:97
  340.0 11.7 %cholesky.253 = f32[128,128]{1,0:T(8,128)S(1)} custom-call(f32[128,128]{1,0:T(8,128)S(1)} %convolution_subtract_fusion.5), custom_call_target="Cholesky" | custom-call | tf_op jit(solution)/shard_map/jit(cholesky)/cholesky | solution.py:97
  356.9 13.8 %while.1 = (s32[]{:T(128)}, f32[512,512]{1,0:T(8,128)}, s32[4,2]{0,1:T(2,128)S(1)}, f32[4,128,128]{2,1,0:T(8,128)}, s32[]{:T(128)}) while((s32[]{:T(128)}, f32[512,512]{1,0:T(8,128)}, s32[4,2]{0,1:T(2,128)S(1)}, f32[4,128,128]{2,1,0:T(8,128)}, s32[]{:T(128)}) %tuple.76), condition=%wide.while_cond, body=%wide.while_body.sunk | while | flops 2 | bytes 132705 | solution.py:98
  370.7 40.1 %custom-call.34 = f32[4,128,128]{1,2,0:T(8,128)S(1)} custom-call(f32[4,128,128]{2,1,0:T(8,128)} %get-tuple-element.25), custom_call_target="InvertDiagBlocksLowerTriangular" | custom-call | tf_op jit(solution)/shard_map/jit(_solve_triangular)/triangular_solve | solution.py:98
  416.6 8.5 %pad_maximum_fusion = f32[2,16,64,1024]{3,2,1,0:T(8,128)} fusion(f32[1,16,64,1024]{3,2,1,0:T(8,128)} %bitcast.49, f32[1,16,64,1024]{3,2,1,0:T(8,128)} %bitcast.29), kind=kLoop, calls=%fused_computation.20 | loop fusion | flops 2097152 | bytes 16777216 | tf_op jit(solution)/shard_map/stack | solution.py:111
  425.2 7.7 %gather_fusion.3 = f32[32,64,1024]{2,1,0:T(8,128)} fusion(f32[2,16,64,1024]{3,2,1,0:T(8,128)} %pad_maximum_fusion, s32[32]{0:T(128)S(1)} %reshape.643), kind=kCustom, calls=%fused_computation.15 | custom fusion | bytes 16777472 | tf_op jit(solution)/shard_map/vmap(jit(_take))/gather | solution.py:15
  438.8 8.7 %copy.215 = f32[2,1024,1024]{2,1,0:T(8,128)} copy(f32[2,1024,1024]{1,2,0:T(8,128)} %fusion.1) | data formatting | bytes 16777216 | tf_op jit(solution)/shard_map/transpose | solution.py:126
  447.5 12.5 %gather_fusion.4 = f32[64,64,1024]{2,1,0:T(8,128)} fusion(f32[2,16,64,1024]{3,2,1,0:T(8,128)} %bitcast.167, s32[64]{0:T(128)S(1)} %reshape.649), kind=kCustom, calls=%fused_computation.16 | custom fusion | bytes 33554944 | tf_op jit(solution)/shard_map/vmap(jit(_take))/gather | solution.py:15
  460.0 7.3 %select_multiply_fusion = f32[2,32,64,1024]{3,2,1,0:T(8,128)S(1)} fusion(f32[2,32,64,1024]{3,2,1,0:T(8,128)} %bitcast.168, f32[2,32]{1,0:T(2,128)S(1)} %fusion.38, pred[2,32]{1,0:T(4,128)(4,1)S(1)} %compare_and_fusion.12), kind=kLoop, calls=%fused_computation.19 | loop fusion | flops 8388608 | bytes 33554752 | tf_op jit(solution)/shard_map/mul | solution.py:127
  474.1 10.0 %bitcast_add_fusion = f32[2048,1024]{1,0:T(8,128)S(1)} fusion(f32[1,32,64,1024]{3,2,1,0:T(8,128)} %get-tuple-element.55, f32[2048,1024]{1,0:T(8,128)} %param.16, f32[1,32,64,1024]{3,2,1,0:T(8,128)} %get-tuple-element.54), kind=kLoop, calls=%fused_computation.21 | loop fusion | flops 4194304 | bytes 33554432 | tf_op jit(solution)/shard_map/add | solution.py:129
  494.2 8.7 %collective-permute-done = f32[2048,64]{0,1:T(8,128)} collective-permute-done((f32[2048,64]{0,1:T(8,128)}, f32[2048,64]{0,1:T(8,128)}, u32[]{:S(2)}, u32[]{:S(2)}) %collective-permute-start) | collective-permute-done | bytes 524320 | tf_op jit(solution)/shard_map/ppermute | solution.py:133
  510.6 52.1 %all-gather.3.cloned.1.call-done = f32[16,512,128]{2,1,0:T(8,128)} async-done(((f32[1,512,128]{2,1,0:T(8,128)}), f32[16,512,128]{2,1,0:T(8,128)}) %all-gather.3.cloned.1.call-update) | async-done | bytes 4194320 | tf_op jit(solution)/shard_map/all_gather | solution.py:140
  569.6 11.4 %copy.218 = f32[2,1024,8,64]{3,2,1,0:T(8,128)} copy(f32[2,1024,8,64]{3,1,2,0:T(8,128)} %bitcast.173) | data formatting | bytes 8388608 | tf_op jit(solution)/shard_map/transpose | solution.py:142
  581.1 7.5 %dot_general.8 = f32[32,64,512]{2,1,0:T(8,128)} reshape(f32[2,1024,8,64]{3,2,1,0:T(8,128)} %copy.218) | data formatting | bytes 8388608 | tf_op jit(solution)/shard_map/rp,qp->rq/dot_general | solution.py:144
  588.6 9.6 %select_select_fusion = f32[32,64,512]{2,1,0:T(8,128)S(1)} fusion(f32[32,64,512]{2,1,0:T(8,128)} %gather_fusion.2, f32[32,64,512]{2,1,0:T(8,128)} %dot_general.8, pred[32]{0:T(512)(128)(4,1)S(1)} %get-tuple-element.102, pred[32]{0:T(512)(128)(4,1)S(1)} %get-tuple-element.103, f32[512,512]{1,0:T(8,128)S(1)} %pad_maximum_fusion.1), kind=kOutput, calls=%fused_computation.29 | convolution fusion | flops 6444548096 | bytes 13631552 | tf_op jit(solution)/shard_map/rp,qp->rq/dot_general | solution.py:144
  610.0 36.0 %all-gather.5.cloned.1.call-done = f32[1024,512]{1,0:T(8,128)} async-done(((f32[128,512]{1,0:T(8,128)}), f32[1024,512]{1,0:T(8,128)}) %all-gather.5.cloned.1.call-update) | async-done | bytes 2097168 | tf_op jit(solution)/shard_map/all_gather | solution.py:166
  645.9 19.0 %subtract_select_fusion = f32[2048,1024]{1,0:T(8,128)} fusion(f32[2048,1024]{1,0:T(8,128)} %copy-done, pred[1024]{0:T(1024)(128)(4,1)S(1)} %fusion.51, pred[2048]{0:T(1024)(128)(4,1)S(1)} %fusion.45, f32[2048,512]{1,0:T(8,128)} %bitcast.170, f32[1024,512]{1,0:T(8,128)} %all-gather.5.cloned.1.call-done), kind=kOutput, calls=%fused_computation.26 | convolution fusion | flops 12891193344 | bytes 23071744 | tf_op jit(solution)/shard_map/rp,cp->rc/dot_general | solution.py:167
  (203 shorter events, 176.8 us)
Async XLA Ops:
  19.9 9.6 %copy-start.8 = (s32[2,128]{1,0:T(2,128)S(1)}, s32[2,128]{1,0:T(2,128)}, u32[]{:S(2)}) copy-start(s32[2,128]{1,0:T(2,128)} %param.19) | copy-start | bytes 3076
  23.2 188.7 %all-to-all-start.2 = ((f32[8,128,512]{2,1,0:T(8,128)}), f32[8,128,512]{2,1,0:T(8,128)}, u32[]{:S(2)}, u32[]{:S(2)}) async-start(f32[8,128,512]{2,1,0:T(8,128)} %bitcast.181), calls=%async_computation.2 | async-start | bytes 4194304 | tf_op jit(solution)/shard_map/all_to_all | solution.py:101
  29.0 181.1 %all-reduce.3.cloned.1.call-start = ((), (), s32[]{:S(2)}) async-start(), calls=%async_computation.4 | async-start | bytes 2097152 | tf_op jit(solution)/shard_map/psum | solution.py:89
  43.7 6.0 copy-start.2
  210.1 6.2 copy-start.7
  211.9 30.5 %all-to-all-start = ((f32[8,128,512]{1,2,0:T(8,128)}), f32[8,128,512]{1,2,0:T(8,128)}, u32[]{:S(2)}, u32[]{:S(2)}) async-start(f32[8,128,512]{1,2,0:T(8,128)} %copy.211), calls=%async_computation | async-start | bytes 4194304 | tf_op jit(solution)/shard_map/all_to_all | solution.py:101
  226.9 22.8 %copy-start.3 = (f32[512,512]{0,1:T(8,128)S(1)}, f32[512,512]{0,1:T(8,128)}, u32[]{:S(2)}) copy-start(f32[512,512]{0,1:T(8,128)} %all-reduce.3.cloned.1.call-done) | copy-start | bytes 3145732
  242.4 90.3 %all-to-all-start.3 = ((f32[16,64,1024]{2,1,0:T(8,128)}), f32[16,64,1024]{2,1,0:T(8,128)}, u32[]{:S(2)}, u32[]{:S(2)}) async-start(f32[16,64,1024]{2,1,0:T(8,128)} %select_multiply_fusion.1), calls=%async_computation.3 | async-start | bytes 8388608 | tf_op jit(solution)/shard_map/all_to_all | solution.py:105
  250.3 1.0 copy-start.5
  332.7 83.9 %all-to-all-start.1 = ((f32[16,64,1024]{2,1,0:T(8,128)}), f32[16,64,1024]{2,1,0:T(8,128)}, u32[]{:S(2)}, u32[]{:S(2)}) async-start(f32[16,64,1024]{2,1,0:T(8,128)} %select_multiply_fusion.2), calls=%async_computation.1 | async-start | bytes 8388608 | tf_op jit(solution)/shard_map/all_to_all | solution.py:105
  339.3 71.8 %copy-start.4 = (f32[512,512]{1,0:T(8,128)S(1)}, f32[512,512]{1,0:T(8,128)}, u32[]{:S(2)}) copy-start(f32[512,512]{1,0:T(8,128)} %fusion.13) | copy-start | bytes 3145732
  339.3 223.3 %all-gather.3.cloned.1.call-start = ((), (), s32[]{:S(2)}) async-start(), calls=%async_computation.5 | async-start | bytes 4456448 | tf_op jit(solution)/shard_map/all_gather | solution.py:140
  484.0 3.4 copy-start
  488.7 14.2 %collective-permute-start = (f32[2048,64]{0,1:T(8,128)}, f32[2048,64]{0,1:T(8,128)}, u32[]{:S(2)}, u32[]{:S(2)}) collective-permute-start(f32[2048,64]{0,1:T(8,128)} %copy.216), channel_id=1, source_target_pairs={{0,8},{1,9},{2,10},{3,11},{4,12},{5,13},{6,14},{7,15},{16,24},{17,... | collective-permute-start | bytes 1572872 | tf_op jit(solution)/shard_map/ppermute | solution.py:133
  507.6 138.3 %all-gather.5.cloned.1.call-start = ((), (), s32[]{:S(2)}) async-start(), calls=%async_computation.6 | async-start | bytes 2359296 | tf_op jit(solution)/shard_map/all_gather | solution.py:166
  598.2 2.0 copy-start.1
  600.5 8.7 %collective-permute-start.1 = (f32[128,512]{1,0:T(8,128)S(1)}, f32[128,512]{1,0:T(8,128)S(1)}, u32[]{:S(2)}, u32[]{:S(2)}) collective-permute-start(f32[128,512]{1,0:T(8,128)S(1)} %constant_dynamic-slice_fusion.3), channel_id=1, source_target_pairs={{0,0},{1,16},{2,32},{3,48},{4,64},{5,80},{6,96},{7,112},{8,8},{9,2... | collective-permute-start | bytes 786440 | tf_op jit(solution)/shard_map/ppermute | solution.py:165
  609.2 0.7 copy-start.6
Sparse Core Ops, SparseCore 0:
  60.1 149.9 all-reduce.2
  507.8 54.8 all-gather.2
  610.0 35.8 all-gather.4

commit v4 on v2

--- a/solution.py
+++ b/solution.py
@@ -63,18 +63,6 @@
     )
     has_col = jnp.sum(col_hit_send.astype(jnp.float32), axis=1)
 
-    blocks = child_schur.reshape(2, child_rowblk, BLK, child_colblk * BLK)
-    arrived = []
-    for k in range(2):
-        outgoing = take_slabs(blocks[k], src_row[k]).reshape(row_slots * BLK, child_colblk * BLK)
-        section_one = lax.all_to_all(outgoing, "row", split_axis=0, concat_axis=0, tiled=True)
-        flipped = section_one.T.reshape(child_colblk, BLK, row_slots * BLK)
-        onward = take_slabs(flipped, src_col[k]) * has_col[k][:, None, None]
-        onward = onward.reshape(col_slots * BLK, row_slots * BLK)
-        section_two = lax.all_to_all(onward, "col", split_axis=0, concat_axis=0, tiled=True)
-        arrived.append(section_two.reshape(col_slots, BLK, row_slots * BLK))
-    arrived = jnp.stack(arrived)
-
     front_rowblk = row_place + row_count * jnp.arange(row_blocks)
     match_rows = (child_index[:, None, :] == front_rowblk[None, :, None]).astype(jnp.int32)
     row_slot_of = sender_row[None, :] * per_owner + row_rank
@@ -86,6 +74,50 @@
     col_source = jnp.sum(match_cols * col_slot_of[:, None, :], axis=2)
     col_weight = jnp.sum(match_cols.astype(jnp.float32) * validity[:, None, :], axis=2)
 
+    blocks = child_schur.reshape(2, child_rowblk, BLK, child_colblk * BLK)
+    section_one = []
+    for k in range(2):
+        outgoing = take_slabs(blocks[k], src_row[k]).reshape(row_slots * BLK, child_colblk * BLK)
+        section_one.append(lax.all_to_all(outgoing, "row", split_axis=0, concat_axis=0, tiled=True))
+
+    panel_width = PANEL // BLK
+    corner_blk = jnp.arange(panel_width)
+    col_hit = (jnp.take(child_index, local_bcol, axis=1)[:, None, :] == corner_blk[None, :, None])
+    corner_cpick = jnp.sum(col_hit.astype(jnp.int32) * jnp.arange(child_colblk)[None, None, :], axis=2)
+    corner_cw = jnp.sum(
+        col_hit.astype(jnp.float32) * jnp.take(validity, local_bcol, axis=1)[:, None, :], axis=2
+    )
+    own = jnp.where(col_place < panel_width, front_matrix[:BLK, :BLK], jnp.zeros((BLK, BLK), jnp.float32))
+    partial = lax.dynamic_update_slice(
+        jnp.zeros((BLK, PANEL), jnp.float32), own, (0, jnp.minimum(col_place, panel_width - 1) * BLK)
+    )
+    for k in range(2):
+        slab = lax.dynamic_slice_in_dim(section_one[k], row_source[k, 0] * BLK, BLK, axis=0)
+        slab = (slab * row_weight[k, 0]).reshape(BLK, child_colblk, BLK)
+        picked_cols = jnp.take(slab, corner_cpick[k], axis=1) * corner_cw[k][None, :, None]
+        partial = partial + picked_cols.reshape(BLK, PANEL)
+    corner_row = lax.psum(partial, "col")
+    corner = lax.all_gather(corner_row, "row", axis=0, tiled=True)
+
+    arrived = []
+    for k in range(2):
+        flipped = section_one[k].T.reshape(child_colblk, BLK, row_slots * BLK)
+        onward = take_slabs(flipped, src_col[k]) * has_col[k][:, None, None]
+        onward = onward.reshape(col_slots * BLK, row_slots * BLK)
+        if k == 0:
+            onward, corner = lax.optimization_barrier((onward, corner))
+            lower_factor = jnp.linalg.cholesky(corner)
+            inverse = jax.scipy.linalg.solve_triangular(
+                lower_factor, jnp.eye(PANEL, dtype=lower_factor.dtype), lower=True
+            )
+        section_two = lax.all_to_all(onward, "col", split_axis=0, concat_axis=0, tiled=True)
+        if k == 1:
+            section_two, lower_factor, inverse = lax.optimization_barrier(
+                (section_two, lower_factor, inverse)
+            )
+        arrived.append(section_two.reshape(col_slots, BLK, row_slots * BLK))
+    arrived = jnp.stack(arrived)
+
     by_col = jax.vmap(take_slabs)(arrived, col_source) * col_weight[:, :, None, None]
     by_col = by_col.reshape(2, local_cols, row_slots * BLK)
     unflipped = jnp.swapaxes(by_col, 1, 2).reshape(2, row_slots, BLK, local_cols)
@@ -93,7 +125,6 @@
     placed = placed.reshape(2, local_rows, local_cols)
     extended = front_matrix + placed[0] + placed[1]
 
-    panel_width = PANEL // BLK
     spread = col_count // panel_width
     lead = extended[:, :BLK]
     lifted = lax.ppermute(
@@ -107,11 +138,6 @@
     gathered = gathered.reshape(spread, panel_width, part_rows, BLK)
     panel_cols = gathered.transpose(0, 2, 1, 3).reshape(local_rows, PANEL)
 
-    corner = lax.all_gather(panel_cols[: PANEL // row_count], "row", axis=0, tiled=True)
-    lower_factor = jnp.linalg.cholesky(corner)
-    inverse = jax.scipy.linalg.solve_triangular(
-        lower_factor, jnp.eye(PANEL, dtype=lower_factor.dtype), lower=True
-    )
     solved = jnp.einsum("rp,qp->rq", panel_cols, inverse, precision=exact_mode)
     logical_blk = jnp.arange(row_blocks) * row_count + row_place
     factor_blocks = lower_factor.reshape(panel_width, BLK, PANEL)

time: 640 us -> 618 us (0.966)
  waiting for transfers between devices: 243 us -> 223 us
    all_to_all x2, waiting for transfers between devices: 97.4 us -> 0.01 us  [on_device(): lax.all_to_all(onward, 'col', split_axis=0, concat_axis=0, tiled=True)]
    psum x0 -> x1, waiting for transfers between devices: none -> 77.5 us  [on_device(): corner_row = lax.psum(partial, 'col')]
    transpose x2 -> x1, local copies, waits for them, and re-layouts: 20.1 us -> 11.4 us  [on_device(): panel_cols = gathered.transpose(0, 2, 1, 3).reshape(local_rows, PANEL)]
    all_gather x1, waiting for transfers between devices: 59.1 us -> 51.3 us  [on_device(): gathered = lax.all_gather(part, 'col', axis=0, tiled=False)]
    all_to_all x2, starting transfers between devices: 19 us -> 11.6 us  [on_device(): lax.all_to_all(onward, 'col', split_axis=0, concat_axis=0, tiled=True)]
    another operation x3 -> x4, other arithmetic: 41.6 us -> 41.4 us  [on_device(): jax.scipy.linalg.solve_triangular(lower_factor, jnp.eye(PANEL, dtype=lowe...]
  transfers between devices with their start and end apart: 9 -> 10, of which waited for: 9 -> 8; matrix products, arithmetic and copies ran while one was open for 7% -> 30% of each run, Pallas kernels for 0% -> 0%
where the time goes in v4:
time: 618 us; the launch traced here: 611 us
  waiting for transfers between devices  223 us (36%)
  other arithmetic  177 us (29%)
  local copies, waits for them, and re-layouts  120 us (19%)
  matrix products  39.8 us (6%)
  starting transfers between devices  32 us (5%)
  between operations  18.4 us (3%)
    another operation x15, other arithmetic, on_device(): lower_factor = jnp.linalg.cholesky(corner)  79.3 us
    psum x1, waiting for transfers between devices, on_device(): corner_row = lax.psum(partial, 'col')  77.5 us
    all_gather x1, waiting for transfers between devices, on_device(): gathered = lax.all_gather(part, 'col', axis=0, tiled=False)  51.3 us
    another operation x4, other arithmetic, on_device(): jax.scipy.linalg.solve_triangular(lower_factor, jnp.eye(PANEL, dtype=lowe...  41.4 us
    all_to_all x2, waiting for transfers between devices, on_device(): lax.all_to_all(outgoing, 'row', split_axis=0, concat_axis=0, tiled=True)  38.5 us
    all_gather x1, waiting for transfers between devices, on_device(): across = lax.all_gather(piece, 'row', axis=0, tiled=True)  36 us
    gather x8, local copies, waits for them, and re-layouts, take_slabs(): return jnp.take(source, indices, axis=0)  31.9 us
    dot_general x1, matrix products, on_device(): update = jnp.einsum('rp,cp->rc', panel_factor, across, precision=exact_mode)  19 us
  transfers between devices with their start and end apart: 10, of which 8 were waited for; matrix products, arithmetic and copies ran while one was open for 30% of the time, Pallas kernels for 0%

profile of v4, /device:TPU:1, one launch (start us, length us, event | category | flops | bytes accessed | tf_op | source)
XLA Modules:
  0.0 611.1 jit_solution(1682860600109360148)
XLA Ops:
  35.5 17.1 %all-to-all-done = f32[8,128,512]{2,1,0:T(8,128)S(1)} async-done(((f32[8,128,512]{2,1,0:T(8,128)}), f32[8,128,512]{2,1,0:T(8,128)S(1)}, u32[]{:S(2)}, u32[]{:S(2)}) %all-to-all-start) | async-done | bytes 2097184 | tf_op jit(solution)/shard_map/all_to_all | solution.py:81
  62.8 21.4 %all-to-all-done.1 = f32[8,128,512]{2,1,0:T(8,128)} async-done(((f32[8,128,512]{2,1,0:T(8,128)}), f32[8,128,512]{2,1,0:T(8,128)}, u32[]{:S(2)}, u32[]{:S(2)}) %all-to-all-start.1) | async-done | bytes 2097184 | tf_op jit(solution)/shard_map/all_to_all | solution.py:81
  92.4 77.5 %all-reduce.3.cloned.1.call-done = f32[64,512]{1,0:T(8,128)} async-done(((f32[64,512]{1,0:T(8,128)}), f32[64,512]{1,0:T(8,128)}) %all-reduce.3.cloned.1.call-update) | async-done | bytes 131088 | tf_op jit(solution)/shard_map/psum | solution.py:99
  200.3 11.7 %cholesky.104 = f32[128,128]{1,0:T(8,128)S(1)} custom-call(f32[128,128]{1,0:T(8,128)S(1)} %cholesky.266), custom_call_target="Cholesky" | custom-call | tf_op jit(solution)/shard_map/jit(cholesky)/cholesky | solution.py:109
  212.1 9.8 %custom-call.31 = f32[1,128,128]{1,2,0:T(8,128)S(1)} custom-call(f32[1,128,128]{2,1,0:T(8,128)S(1)} %get-tuple-element.61), custom_call_target="InvertDiagBlocksLowerTriangular" | custom-call | tf_op jit(solution)/shard_map/jit(cholesky)/cholesky | solution.py:109
  224.5 11.7 %cholesky.217 = f32[128,128]{1,0:T(8,128)S(1)} custom-call(f32[128,128]{1,0:T(8,128)S(1)} %cholesky.270), custom_call_target="Cholesky" | custom-call | tf_op jit(solution)/shard_map/jit(cholesky)/cholesky | solution.py:109
  236.2 10.2 %custom-call.32 = f32[1,128,128]{1,2,0:T(8,128)S(1)} custom-call(f32[1,128,128]{2,1,0:T(8,128)S(1)} %get-tuple-element.58), custom_call_target="InvertDiagBlocksLowerTriangular" | custom-call | tf_op jit(solution)/shard_map/jit(cholesky)/cholesky | solution.py:109
  248.0 11.7 %cholesky.238 = f32[128,128]{1,0:T(8,128)S(1)} custom-call(f32[128,128]{1,0:T(8,128)S(1)} %cholesky.275), custom_call_target="Cholesky" | custom-call | tf_op jit(solution)/shard_map/jit(cholesky)/cholesky | solution.py:109
  259.8 9.8 %custom-call.33 = f32[1,128,128]{1,2,0:T(8,128)S(1)} custom-call(f32[1,128,128]{2,1,0:T(8,128)S(1)} %get-tuple-element.55), custom_call_target="InvertDiagBlocksLowerTriangular" | custom-call | tf_op jit(solution)/shard_map/jit(cholesky)/cholesky | solution.py:109
  279.1 11.7 %cholesky.255 = f32[128,128]{1,0:T(8,128)S(1)} custom-call(f32[128,128]{1,0:T(8,128)S(1)} %convolution_subtract_fusion.5), custom_call_target="Cholesky" | custom-call | tf_op jit(solution)/shard_map/jit(cholesky)/cholesky | solution.py:109
  295.9 13.7 %while.1 = (s32[]{:T(128)}, f32[512,512]{1,0:T(8,128)}, s32[4,2]{0,1:T(2,128)S(1)}, f32[4,128,128]{2,1,0:T(8,128)}, s32[]{:T(128)}) while((s32[]{:T(128)}, f32[512,512]{1,0:T(8,128)}, s32[4,2]{0,1:T(2,128)S(1)}, f32[4,128,128]{2,1,0:T(8,128)}, s32[]{:T(128)}) %tuple.67), condition=%wide.while_cond, body=%wide.while_body.sunk | while | flops 2 | bytes 132705 | solution.py:110
  309.6 40.1 %custom-call.34 = f32[4,128,128]{1,2,0:T(8,128)S(1)} custom-call(f32[4,128,128]{2,1,0:T(8,128)} %get-tuple-element.23), custom_call_target="InvertDiagBlocksLowerTriangular" | custom-call | tf_op jit(solution)/shard_map/jit(_solve_triangular)/triangular_solve | solution.py:110
  355.5 8.5 %pad_maximum_fusion = f32[2,16,64,1024]{3,2,1,0:T(8,128)} fusion(f32[1,16,64,1024]{3,2,1,0:T(8,128)} %bitcast.47, f32[1,16,64,1024]{3,2,1,0:T(8,128)} %bitcast.30), kind=kLoop, calls=%fused_computation.16 | loop fusion | flops 2097152 | bytes 16777216 | tf_op jit(solution)/shard_map/stack | solution.py:119
  364.1 7.7 %gather_fusion.3 = f32[32,64,1024]{2,1,0:T(8,128)} fusion(f32[2,16,64,1024]{3,2,1,0:T(8,128)} %pad_maximum_fusion, s32[32]{0:T(128)S(1)} %reshape.601), kind=kCustom, calls=%fused_computation.11 | custom fusion | bytes 16777472 | tf_op jit(solution)/shard_map/vmap(jit(_take))/gather | solution.py:15
  377.7 8.7 %copy.182 = f32[2,1024,1024]{2,1,0:T(8,128)} copy(f32[2,1024,1024]{1,2,0:T(8,128)} %fusion.1) | data formatting | bytes 16777216 | tf_op jit(solution)/shard_map/transpose | solution.py:123
  386.4 12.5 %gather_fusion.4 = f32[64,64,1024]{2,1,0:T(8,128)} fusion(f32[2,16,64,1024]{3,2,1,0:T(8,128)} %bitcast.151, s32[64]{0:T(128)S(1)} %reshape.607), kind=kCustom, calls=%fused_computation.12 | custom fusion | bytes 33554944 | tf_op jit(solution)/shard_map/vmap(jit(_take))/gather | solution.py:15
  413.0 10.0 %bitcast_add_fusion = f32[2048,1024]{1,0:T(8,128)S(1)} fusion(f32[1,32,64,1024]{3,2,1,0:T(8,128)} %get-tuple-element.49, f32[2048,1024]{1,0:T(8,128)} %param.12, f32[1,32,64,1024]{3,2,1,0:T(8,128)} %get-tuple-element.48), kind=kLoop, calls=%fused_computation.17 | loop fusion | flops 4194304 | bytes 33554432 | tf_op jit(solution)/shard_map/add | solution.py:126
  433.1 9.9 %collective-permute-done = f32[2048,64]{0,1:T(8,128)} collective-permute-done((f32[2048,64]{0,1:T(8,128)}, f32[2048,64]{0,1:T(8,128)}, u32[]{:S(2)}, u32[]{:S(2)}) %collective-permute-start) | collective-permute-done | bytes 524320 | tf_op jit(solution)/shard_map/ppermute | solution.py:130
  450.7 51.3 %all-gather.6.cloned.1.call-done = f32[16,512,128]{2,1,0:T(8,128)} async-done(((f32[1,512,128]{2,1,0:T(8,128)}), f32[16,512,128]{2,1,0:T(8,128)}) %all-gather.6.cloned.1.call-update) | async-done | bytes 4194320 | tf_op jit(solution)/shard_map/all_gather | solution.py:137
  509.0 11.4 %copy.185 = f32[2,1024,8,64]{3,2,1,0:T(8,128)} copy(f32[2,1024,8,64]{3,1,2,0:T(8,128)} %bitcast.157) | data formatting | bytes 8388608 | tf_op jit(solution)/shard_map/transpose | solution.py:139
  520.4 7.5 %dot_general.8 = f32[32,64,512]{2,1,0:T(8,128)} reshape(f32[2,1024,8,64]{3,2,1,0:T(8,128)} %copy.185) | data formatting | bytes 8388608 | tf_op jit(solution)/shard_map/rp,qp->rq/dot_general | solution.py:141
  527.9 9.6 %select_select_fusion = f32[32,64,512]{2,1,0:T(8,128)S(1)} fusion(f32[32,64,512]{2,1,0:T(8,128)} %gather_fusion.2, f32[32,64,512]{2,1,0:T(8,128)} %dot_general.8, pred[32]{0:T(512)(128)(4,1)S(1)} %get-tuple-element.90, pred[32]{0:T(512)(128)(4,1)S(1)} %get-tuple-element.91, f32[512,512]{1,0:T(8,128)S(1)} %pad_maximum_fusion.1), kind=kOutput, calls=%fused_computation.25 | convolution fusion | flops 6444548096 | bytes 13631552 | tf_op jit(solution)/shard_map/rp,qp->rq/dot_general | solution.py:141
  549.3 36.0 %all-gather.8.cloned.1.call-done = f32[1024,512]{1,0:T(8,128)} async-done(((f32[128,512]{1,0:T(8,128)}), f32[1024,512]{1,0:T(8,128)}) %all-gather.8.cloned.1.call-update) | async-done | bytes 2097168 | tf_op jit(solution)/shard_map/all_gather | solution.py:163
  585.3 19.0 %subtract_select_fusion = f32[2048,1024]{1,0:T(8,128)} fusion(f32[2048,1024]{1,0:T(8,128)} %copy-done, pred[1024]{0:T(1024)(128)(4,1)S(1)} %fusion.51, pred[2048]{0:T(1024)(128)(4,1)S(1)} %fusion.45, f32[2048,512]{1,0:T(8,128)} %bitcast.154, f32[1024,512]{1,0:T(8,128)} %all-gather.8.cloned.1.call-done), kind=kOutput, calls=%fused_computation.22 | convolution fusion | flops 12891193344 | bytes 23071744 | tf_op jit(solution)/shard_map/rp,cp->rc/dot_general | solution.py:164
  (190 shorter events, 167.6 us)
Async XLA Ops:
  18.7 7.7 %copy-start.6 = (s32[2,128]{1,0:T(2,128)S(1)}, s32[2,128]{1,0:T(2,128)}, u32[]{:S(2)}) copy-start(s32[2,128]{1,0:T(2,128)} %param.15) | copy-start | bytes 3076
  20.5 10.2 %copy-start.5 = (s32[2,128]{1,0:T(2,128)S(1)}, s32[2,128]{1,0:T(2,128)}, u32[]{:S(2)}) copy-start(s32[2,128]{1,0:T(2,128)} %param.14) | copy-start | bytes 3076
  20.5 32.1 %all-to-all-start = ((f32[8,128,512]{2,1,0:T(8,128)}), f32[8,128,512]{2,1,0:T(8,128)S(1)}, u32[]{:S(2)}, u32[]{:S(2)}) async-start(f32[8,128,512]{2,1,0:T(8,128)} %bitcast.164), calls=%async_computation | async-start | bytes 4194304 | tf_op jit(solution)/shard_map/all_to_all | solution.py:81
  52.6 33.2 %copy-start.2 = (f32[8,128,512]{2,1,0:T(8,128)}, f32[8,128,512]{2,1,0:T(8,128)S(1)}, u32[]{:S(2)}) copy-start(f32[8,128,512]{2,1,0:T(8,128)S(1)} %all-to-all-done) | copy-start | bytes 6291460
  52.6 31.5 %all-to-all-start.1 = ((f32[8,128,512]{2,1,0:T(8,128)}), f32[8,128,512]{2,1,0:T(8,128)}, u32[]{:S(2)}, u32[]{:S(2)}) async-start(f32[8,128,512]{2,1,0:T(8,128)} %bitcast.163), calls=%async_computation.1 | async-start | bytes 4194304 | tf_op jit(solution)/shard_map/all_to_all | solution.py:81
  57.8 112.0 %all-reduce.3.cloned.1.call-start = ((), (), s32[]{:S(2)}) async-start(), calls=%async_computation.4 | async-start | bytes 262144 | tf_op jit(solution)/shard_map/psum | solution.py:99
  87.5 108.8 %all-gather.4.cloned.1.call-start = ((), (), s32[]{:S(2)}) async-start(), calls=%async_computation.5 | async-start | bytes 1179648 | tf_op jit(solution)/shard_map/all_gather | solution.py:100
  175.1 96.6 %all-to-all-start.3 = ((f32[16,64,1024]{2,1,0:T(8,128)}), f32[16,64,1024]{2,1,0:T(8,128)}, u32[]{:S(2)}, u32[]{:S(2)}) async-start(f32[16,64,1024]{2,1,0:T(8,128)} %select_multiply_fusion.1), calls=%async_computation.3 | async-start | bytes 8388608 | tf_op jit(solution)/shard_map/all_to_all | solution.py:113
  199.3 1.0 copy-start.3
  271.6 83.9 %all-to-all-start.2 = ((f32[16,64,1024]{2,1,0:T(8,128)}), f32[16,64,1024]{2,1,0:T(8,128)}, u32[]{:S(2)}, u32[]{:S(2)}) async-start(f32[16,64,1024]{2,1,0:T(8,128)} %select_multiply_fusion.2), calls=%async_computation.2 | async-start | bytes 8388608 | tf_op jit(solution)/shard_map/all_to_all | solution.py:113
  278.4 223.6 %all-gather.6.cloned.1.call-start = ((), (), s32[]{:S(2)}) async-start(), calls=%async_computation.6 | async-start | bytes 4456448 | tf_op jit(solution)/shard_map/all_gather | solution.py:137
  422.9 3.4 copy-start
  427.6 15.5 %collective-permute-start = (f32[2048,64]{0,1:T(8,128)}, f32[2048,64]{0,1:T(8,128)}, u32[]{:S(2)}, u32[]{:S(2)}) collective-permute-start(f32[2048,64]{0,1:T(8,128)} %copy.183), channel_id=1, source_target_pairs={{0,8},{1,9},{2,10},{3,11},{4,12},{5,13},{6,14},{7,15},{16,24},{17,... | collective-permute-start | bytes 1572872 | tf_op jit(solution)/shard_map/ppermute | solution.py:130
  447.8 137.5 %all-gather.8.cloned.1.call-start = ((), (), s32[]{:S(2)}) async-start(), calls=%async_computation.7 | async-start | bytes 2359296 | tf_op jit(solution)/shard_map/all_gather | solution.py:163
  537.6 2.0 copy-start.1
  539.8 8.7 %collective-permute-start.1 = (f32[128,512]{1,0:T(8,128)S(1)}, f32[128,512]{1,0:T(8,128)S(1)}, u32[]{:S(2)}, u32[]{:S(2)}) collective-permute-start(f32[128,512]{1,0:T(8,128)S(1)} %constant_dynamic-slice_fusion.3), channel_id=1, source_target_pairs={{0,0},{1,16},{2,32},{3,48},{4,64},{5,80},{6,96},{7,112},{8,8},{9,2... | collective-permute-start | bytes 786440 | tf_op jit(solution)/shard_map/ppermute | solution.py:162
  548.5 0.7 copy-start.4
Sparse Core Ops, SparseCore 0:
  87.6 82.1 all-reduce.2
  171.5 24.7 all-gather.3
  447.9 54.0 all-gather.5
  549.4 35.8 all-gather.7

commit v5 on v4

--- a/solution.py
+++ b/solution.py
@@ -96,7 +96,7 @@
         slab = (slab * row_weight[k, 0]).reshape(BLK, child_colblk, BLK)
         picked_cols = jnp.take(slab, corner_cpick[k], axis=1) * corner_cw[k][None, :, None]
         partial = partial + picked_cols.reshape(BLK, PANEL)
-    corner_row = lax.psum(partial, "col")
+    corner_row = jnp.sum(lax.all_gather(partial, "col", axis=0, tiled=False), axis=0)
     corner = lax.all_gather(corner_row, "row", axis=0, tiled=True)
 
     arrived = []
@@ -126,7 +126,13 @@
     extended = front_matrix + placed[0] + placed[1]
 
     spread = col_count // panel_width
-    lead = extended[:, :BLK]
+    lead = front_matrix[:, :BLK]
+    for k in range(2):
+        first_col = lax.dynamic_index_in_dim(arrived[k], col_source[k, 0], axis=0, keepdims=False)
+        first_col = (first_col * col_weight[k, 0]).T.reshape(row_slots, BLK, BLK)
+        lead = lead + (take_slabs(first_col, row_source[k]) * row_weight[k][:, None, None]).reshape(
+            local_rows, BLK
+        )
     lifted = lax.ppermute(
         lead, "col", [(c, c + panel_width * s) for s in range(1, spread) for c in range(panel_width)]
     )

time: 618 us -> 564 us (0.913)
  the two profiles are of different devices: /device:TPU:1 before, /device:TPU:6 now
where the time goes in v5:
time: 564 us; the launch traced here: 557 us
  other arithmetic  177 us (31%)
  waiting for transfers between devices  158 us (28%)
  local copies, waits for them, and re-layouts  121 us (21%)
  matrix products  44.8 us (8%)
  starting transfers between devices  33.5 us (6%)
  between operations  22.5 us (4%)
    another operation x15, other arithmetic, on_device(): lower_factor = jnp.linalg.cholesky(corner)  79.6 us
    all_gather x1, waiting for transfers between devices, on_device(): gathered = lax.all_gather(part, 'col', axis=0, tiled=False)  50.8 us
    all_gather x1, waiting for transfers between devices, on_device(): lax.all_gather(partial, 'col', axis=0, tiled=False)  46.2 us
    another operation x4, other arithmetic, on_device(): jax.scipy.linalg.solve_triangular(lower_factor, jnp.eye(PANEL, dtype=lowe...  42.4 us
    all_to_all x2, waiting for transfers between devices, on_device(): lax.all_to_all(outgoing, 'row', split_axis=0, concat_axis=0, tiled=True)  36.4 us
    gather x10, local copies, waits for them, and re-layouts, take_slabs(): return jnp.take(source, indices, axis=0)  33.2 us
    dot_general x1, matrix products, on_device(): update = jnp.einsum('rp,cp->rc', panel_factor, across, precision=exact_mode)  24.1 us
    ppermute x1, waiting for transfers between devices, on_device(): piece = lax.ppermute(piece, ('row', 'col'), pairs)  16.1 us
  transfers between devices with their start and end apart: 10, of which 6 were waited for; matrix products, arithmetic and copies ran while one was open for 45% of the time, Pallas kernels for 0%

profile of v5, /device:TPU:6, one launch (start us, length us, event | category | flops | bytes accessed | tf_op | source)
XLA Modules:
  0.0 557.1 jit_solution(17544130976593790222)
XLA Ops:
  33.1 17.4 %all-to-all-done = f32[8,128,512]{2,1,0:T(8,128)S(1)} async-done(((f32[8,128,512]{2,1,0:T(8,128)}), f32[8,128,512]{2,1,0:T(8,128)S(1)}, u32[]{:S(2)}, u32[]{:S(2)}) %all-to-all-start) | async-done | bytes 2097184 | tf_op jit(solution)/shard_map/all_to_all | solution.py:81
  63.0 19.0 %all-to-all-done.1 = f32[8,128,512]{2,1,0:T(8,128)} async-done(((f32[8,128,512]{2,1,0:T(8,128)}), f32[8,128,512]{2,1,0:T(8,128)}, u32[]{:S(2)}, u32[]{:S(2)}) %all-to-all-start.1) | async-done | bytes 2097184 | tf_op jit(solution)/shard_map/all_to_all | solution.py:81
  86.5 46.2 %all-gather.12.cloned.1.call-done = f32[1024,512]{1,0:T(8,128)} async-done(((f32[64,512]{1,0:T(8,128)}), f32[1024,512]{1,0:T(8,128)}) %all-gather.12.cloned.1.call-update) | async-done | bytes 2097168 | tf_op jit(solution)/shard_map/all_gather | solution.py:99
  170.1 11.7 %cholesky.104 = f32[128,128]{1,0:T(8,128)S(1)} custom-call(f32[128,128]{1,0:T(8,128)S(1)} %cholesky.266), custom_call_target="Cholesky" | custom-call | tf_op jit(solution)/shard_map/jit(cholesky)/cholesky | solution.py:109
  182.0 9.8 %custom-call.31 = f32[1,128,128]{1,2,0:T(8,128)S(1)} custom-call(f32[1,128,128]{2,1,0:T(8,128)S(1)} %get-tuple-element.66), custom_call_target="InvertDiagBlocksLowerTriangular" | custom-call | tf_op jit(solution)/shard_map/jit(cholesky)/cholesky | solution.py:109
  194.3 11.7 %cholesky.217 = f32[128,128]{1,0:T(8,128)S(1)} custom-call(f32[128,128]{1,0:T(8,128)S(1)} %cholesky.270), custom_call_target="Cholesky" | custom-call | tf_op jit(solution)/shard_map/jit(cholesky)/cholesky | solution.py:109
  206.0 10.2 %custom-call.32 = f32[1,128,128]{1,2,0:T(8,128)S(1)} custom-call(f32[1,128,128]{2,1,0:T(8,128)S(1)} %get-tuple-element.63), custom_call_target="InvertDiagBlocksLowerTriangular" | custom-call | tf_op jit(solution)/shard_map/jit(cholesky)/cholesky | solution.py:109
  217.8 11.7 %cholesky.238 = f32[128,128]{1,0:T(8,128)S(1)} custom-call(f32[128,128]{1,0:T(8,128)S(1)} %cholesky.275), custom_call_target="Cholesky" | custom-call | tf_op jit(solution)/shard_map/jit(cholesky)/cholesky | solution.py:109
  229.6 9.8 %custom-call.33 = f32[1,128,128]{1,2,0:T(8,128)S(1)} custom-call(f32[1,128,128]{2,1,0:T(8,128)S(1)} %get-tuple-element.60), custom_call_target="InvertDiagBlocksLowerTriangular" | custom-call | tf_op jit(solution)/shard_map/jit(cholesky)/cholesky | solution.py:109
  240.8 11.9 %cholesky.255 = f32[128,128]{1,0:T(8,128)S(1)} custom-call(f32[128,128]{1,0:T(8,128)S(1)} %convolution_subtract_fusion.5), custom_call_target="Cholesky" | custom-call | tf_op jit(solution)/shard_map/jit(cholesky)/cholesky | solution.py:109
  266.5 14.1 %while.1 = (s32[]{:T(128)}, f32[512,512]{1,0:T(8,128)}, s32[4,2]{0,1:T(2,128)S(1)}, f32[4,128,128]{2,1,0:T(8,128)}, s32[]{:T(128)}) while((s32[]{:T(128)}, f32[512,512]{1,0:T(8,128)}, s32[4,2]{0,1:T(2,128)S(1)}, f32[4,128,128]{2,1,0:T(8,128)}, s32[]{:T(128)}) %tuple.75), condition=%wide.while_cond, body=%wide.while_body.sunk | while | flops 2 | bytes 132705 | solution.py:110
  280.6 40.1 %custom-call.34 = f32[4,128,128]{1,2,0:T(8,128)S(1)} custom-call(f32[4,128,128]{2,1,0:T(8,128)} %get-tuple-element.24), custom_call_target="InvertDiagBlocksLowerTriangular" | custom-call | tf_op jit(solution)/shard_map/jit(_solve_triangular)/triangular_solve | solution.py:110
  345.1 8.5 %collective-permute-done = f32[2048,64]{0,1:T(8,128)S(1)} collective-permute-done((f32[2048,64]{0,1:T(8,128)S(1)}, f32[2048,64]{0,1:T(8,128)S(1)}, u32[]{:S(2)}, u32[]{:S(2)}) %collective-permute-start) | collective-permute-done | bytes 524320 | tf_op jit(solution)/shard_map/ppermute | solution.py:136
  357.6 50.8 %all-gather.8.cloned.1.call-done = f32[16,512,128]{2,1,0:T(8,128)} async-done(((f32[1,512,128]{2,1,0:T(8,128)}), f32[16,512,128]{2,1,0:T(8,128)}) %all-gather.8.cloned.1.call-update) | async-done | bytes 4194320 | tf_op jit(solution)/shard_map/all_gather | solution.py:143
  415.6 11.5 %copy.169 = f32[2,1024,8,64]{3,2,1,0:T(8,128)} copy(f32[2,1024,8,64]{3,1,2,0:T(8,128)} %bitcast.186) | data formatting | bytes 8388608 | tf_op jit(solution)/shard_map/transpose | solution.py:145
  427.0 7.6 %dot_general.8 = f32[32,64,512]{2,1,0:T(8,128)} reshape(f32[2,1024,8,64]{3,2,1,0:T(8,128)} %copy.169) | data formatting | bytes 8388608 | tf_op jit(solution)/shard_map/rp,qp->rq/dot_general | solution.py:147
  434.6 9.6 %select_select_fusion = f32[32,64,512]{2,1,0:T(8,128)S(1)} fusion(f32[32,64,512]{2,1,0:T(8,128)} %gather_fusion.2, f32[32,64,512]{2,1,0:T(8,128)} %dot_general.8, pred[32]{0:T(512)(128)(4,1)S(1)} %get-tuple-element.99, pred[32]{0:T(512)(128)(4,1)S(1)} %broadcast_compare_fusion.1, f32[512,512]{1,0:T(8,128)S(1)} %copy-done.2), kind=kOutput, calls=%fused_computation.28 | convolution fusion | flops 6444548096 | bytes 13631552 | tf_op jit(solution)/shard_map/rp,qp->rq/dot_general | solution.py:147
  451.0 16.1 %collective-permute-done.1 = f32[128,512]{1,0:T(8,128)S(1)} collective-permute-done((f32[128,512]{1,0:T(8,128)S(1)}, f32[128,512]{1,0:T(8,128)S(1)}, u32[]{:S(2)}, u32[]{:S(2)}) %collective-permute-start.1) | collective-permute-done | bytes 262176 | tf_op jit(solution)/shard_map/ppermute | solution.py:168
  468.3 8.5 %pad_maximum_fusion = f32[2,16,64,1024]{3,2,1,0:T(8,128)} fusion(f32[1,16,64,1024]{3,2,1,0:T(8,128)} %bitcast.48, f32[1,16,64,1024]{3,2,1,0:T(8,128)} %bitcast.31), kind=kLoop, calls=%fused_computation.18 | loop fusion | flops 2097152 | bytes 16777216 | tf_op jit(solution)/shard_map/stack | solution.py:119
  476.9 7.7 %gather_fusion.3 = f32[32,64,1024]{2,1,0:T(8,128)} fusion(f32[2,16,64,1024]{3,2,1,0:T(8,128)} %pad_maximum_fusion, s32[32]{0:T(128)S(1)} %reshape.647), kind=kCustom, calls=%fused_computation.13 | custom fusion | bytes 16777472 | tf_op jit(solution)/shard_map/vmap(jit(_take))/gather | solution.py:15
  490.9 8.7 %copy.162 = f32[2,1024,1024]{2,1,0:T(8,128)} copy(f32[2,1024,1024]{1,2,0:T(8,128)} %fusion.3) | data formatting | bytes 16777216 | tf_op jit(solution)/shard_map/transpose | solution.py:123
  499.6 12.5 %gather_fusion.4 = f32[64,64,1024]{2,1,0:T(8,128)} fusion(f32[2,16,64,1024]{3,2,1,0:T(8,128)} %bitcast.183, s32[64]{0:T(128)S(1)} %reshape.653), kind=kCustom, calls=%fused_computation.14 | custom fusion | bytes 33554944 | tf_op jit(solution)/shard_map/vmap(jit(_take))/gather | solution.py:15
  512.1 7.3 %select_multiply_fusion = f32[2,32,64,1024]{3,2,1,0:T(8,128)S(1)} fusion(f32[2,32,64,1024]{3,2,1,0:T(8,128)} %bitcast.184, f32[2,32]{1,0:T(2,128)S(1)} %fusion.40, pred[2,32]{1,0:T(4,128)(4,1)S(1)} %compare_and_fusion.12), kind=kLoop, calls=%fused_computation.17 | loop fusion | flops 8388608 | bytes 33554752 | tf_op jit(solution)/shard_map/mul | solution.py:124
  526.0 24.1 %fusion.1 = f32[2048,1024]{1,0:T(8,128)} fusion(f32[1,32,64,1024]{3,2,1,0:T(8,128)} %get-tuple-element.54, f32[2048,1024]{1,0:T(8,128)} %param.14, f32[1,32,64,1024]{3,2,1,0:T(8,128)} %get-tuple-element.53, pred[1024]{0:T(1024)(128)(4,1)S(1)} %fusion.53, pred[2048]{0:T(1024)(128)(4,1)S(1)} %fusion.47, f32[2048,512]{1,0:T(8,128)} %bitcast.188, ...), kind=kOutput, calls=%fused_computation.21 | convolution fusion | flops 12895387648 | bytes 39848960 | tf_op jit(solution)/shard_map/rp,cp->rc/dot_general | solution.py:170
  (209 shorter events, 162.3 us)
Async XLA Ops:
  20.5 8.5 %copy-start.6 = (s32[2,128]{1,0:T(2,128)S(1)}, s32[2,128]{1,0:T(2,128)}, u32[]{:S(2)}) copy-start(s32[2,128]{1,0:T(2,128)} %param.16) | copy-start | bytes 3076
  20.5 30.0 %all-to-all-start = ((f32[8,128,512]{2,1,0:T(8,128)}), f32[8,128,512]{2,1,0:T(8,128)S(1)}, u32[]{:S(2)}, u32[]{:S(2)}) async-start(f32[8,128,512]{2,1,0:T(8,128)} %bitcast.196), calls=%async_computation | async-start | bytes 4194304 | tf_op jit(solution)/shard_map/all_to_all | solution.py:81
  29.8 28.3 %copy-start.7 = (s32[2,128]{1,0:T(2,128)S(1)}, s32[2,128]{1,0:T(2,128)}, u32[]{:S(2)}) copy-start(s32[2,128]{1,0:T(2,128)} %param.17) | copy-start | bytes 3076
  50.5 33.2 %copy-start.1 = (f32[8,128,512]{2,1,0:T(8,128)}, f32[8,128,512]{2,1,0:T(8,128)S(1)}, u32[]{:S(2)}) copy-start(f32[8,128,512]{2,1,0:T(8,128)S(1)} %all-to-all-done) | copy-start | bytes 6291460
  50.5 31.5 %all-to-all-start.1 = ((f32[8,128,512]{2,1,0:T(8,128)}), f32[8,128,512]{2,1,0:T(8,128)}, u32[]{:S(2)}, u32[]{:S(2)}) async-start(f32[8,128,512]{2,1,0:T(8,128)} %bitcast.195), calls=%async_computation.1 | async-start | bytes 4194304 | tf_op jit(solution)/shard_map/all_to_all | solution.py:81
  56.8 75.8 %all-gather.12.cloned.1.call-start = ((), (), s32[]{:S(2)}) async-start(), calls=%async_computation.7 | async-start | bytes 2228224 | tf_op jit(solution)/shard_map/all_gather | solution.py:99
  85.4 80.7 %all-gather.6.cloned.1.call-start = ((), (), s32[]{:S(2)}) async-start(), calls=%async_computation.4 | async-start | bytes 1179648 | tf_op jit(solution)/shard_map/all_gather | solution.py:100
  145.1 7.6 %slice-start = ((f32[2048,1024]{1,0:T(8,128)}), f32[2048,64]{1,0:T(8,128)S(1)}, s32[]{:S(2)}) async-start(f32[2048,1024]{1,0:T(8,128)} %param.14), calls=%async_computation.8 | async-start | bytes 2097152 | tf_op jit(solution)/shard_map/slice | solution.py:129
  145.1 111.6 %all-to-all-start.3 = ((f32[16,64,1024]{2,1,0:T(8,128)}), f32[16,64,1024]{2,1,0:T(8,128)}, u32[]{:S(2)}, u32[]{:S(2)}) async-start(f32[16,64,1024]{2,1,0:T(8,128)} %select_multiply_fusion.1), calls=%async_computation.3 | async-start | bytes 8388608 | tf_op jit(solution)/shard_map/all_to_all | solution.py:113
  169.1 1.0 copy-start.3
  256.7 76.9 %all-to-all-start.2 = ((f32[16,64,1024]{2,1,0:T(8,128)}), f32[16,64,1024]{2,1,0:T(8,128)}, u32[]{:S(2)}, u32[]{:S(2)}) async-start(f32[16,64,1024]{2,1,0:T(8,128)} %select_multiply_fusion.2), calls=%async_computation.2 | async-start | bytes 8388608 | tf_op jit(solution)/shard_map/all_to_all | solution.py:113
  264.0 144.5 %all-gather.8.cloned.1.call-start = ((), (), s32[]{:S(2)}) async-start(), calls=%async_computation.5 | async-start | bytes 4456448 | tf_op jit(solution)/shard_map/all_gather | solution.py:143
  331.2 7.5 %copy-start.4 = (f32[2048,64]{0,1:T(8,128)S(1)}, f32[2048,64]{0,1:T(8,128)}, u32[]{:S(2)}) copy-start(f32[2048,64]{0,1:T(8,128)} %copy.171) | copy-start | bytes 1572868
  339.8 13.8 %collective-permute-start = (f32[2048,64]{0,1:T(8,128)S(1)}, f32[2048,64]{0,1:T(8,128)S(1)}, u32[]{:S(2)}, u32[]{:S(2)}) collective-permute-start(f32[2048,64]{0,1:T(8,128)S(1)} %add_add_fusion), channel_id=1, source_target_pairs={{0,8},{1,9},{2,10},{3,11},{4,12},{5,13},{6,14},{7,15},{16,24},{17,... | collective-permute-start | bytes 1572872 | tf_op jit(solution)/shard_map/ppermute | solution.py:136
  354.7 171.3 %all-gather.10.cloned.1.call-start = ((), (), s32[]{:S(2)}) async-start(), calls=%async_computation.6 | async-start | bytes 2359296 | tf_op jit(solution)/shard_map/all_gather | solution.py:169
  427.0 7.6 %copy-start.2 = (f32[512,512]{1,0:T(8,128)S(1)}, f32[512,512]{1,0:T(8,128)}, u32[]{:S(2)}) copy-start(f32[512,512]{1,0:T(8,128)} %pad_maximum_fusion.1) | copy-start | bytes 3145732
  444.2 2.0 copy-start
  446.5 20.6 %collective-permute-start.1 = (f32[128,512]{1,0:T(8,128)S(1)}, f32[128,512]{1,0:T(8,128)S(1)}, u32[]{:S(2)}, u32[]{:S(2)}) collective-permute-start(f32[128,512]{1,0:T(8,128)S(1)} %constant_dynamic-slice_fusion.2), channel_id=1, source_target_pairs={{0,0},{1,16},{2,32},{3,48},{4,64},{5,80},{6,96},{7,112},{8,8},{9,2... | collective-permute-start | bytes 786440 | tf_op jit(solution)/shard_map/ppermute | solution.py:168
  467.1 0.7 copy-start.5
Sparse Core Ops, SparseCore 0:
  85.5 47.0 all-gather.11
  135.2 20.8 all-gather.5
  354.8 53.5 all-gather.7
  467.9 22.2 all-gather.9

commit v6 on v5

--- a/solution.py
+++ b/solution.py
@@ -13,6 +13,37 @@
 
 def take_slabs(source, indices):
     return jnp.take(source, indices, axis=0)
+
+
+def factor_and_invert(corner, width=128):
+    count = corner.shape[0] // width
+    sym = (corner + corner.T) / 2
+    grid = [[sym[i * width : (i + 1) * width, j * width : (j + 1) * width] for j in range(count)] for i in range(count)]
+    eye = jnp.eye(width, dtype=corner.dtype)
+    low = [[None] * count for _ in range(count)]
+    diag_inv = []
+    for p in range(count):
+        lpp = lax.linalg.cholesky(grid[p][p], symmetrize_input=False)
+        dinv = jax.scipy.linalg.solve_triangular(lpp, eye, lower=True)
+        low[p][p] = lpp
+        diag_inv.append(dinv)
+        for i in range(p + 1, count):
+            low[i][p] = jnp.dot(grid[i][p], dinv.T, precision=exact_mode)
+        for i in range(p + 1, count):
+            for j in range(p + 1, i + 1):
+                grid[i][j] = grid[i][j] - jnp.dot(low[i][p], low[j][p].T, precision=exact_mode)
+    zero = jnp.zeros((width, width), corner.dtype)
+    inv = [[zero] * count for _ in range(count)]
+    for j in range(count):
+        inv[j][j] = diag_inv[j]
+        for i in range(j + 1, count):
+            acc = jnp.dot(low[i][j], inv[j][j], precision=exact_mode)
+            for k in range(j + 1, i):
+                acc = acc + jnp.dot(low[i][k], inv[k][j], precision=exact_mode)
+            inv[i][j] = -jnp.dot(diag_inv[i], acc, precision=exact_mode)
+    lower = jnp.block([[low[i][j] if j <= i else zero for j in range(count)] for i in range(count)])
+    inverse = jnp.block(inv)
+    return lower, inverse
 
 
 def on_device(front_matrix, child_schur, child_index, child_valid):
@@ -106,10 +137,7 @@
         onward = onward.reshape(col_slots * BLK, row_slots * BLK)
         if k == 0:
             onward, corner = lax.optimization_barrier((onward, corner))
-            lower_factor = jnp.linalg.cholesky(corner)
-            inverse = jax.scipy.linalg.solve_triangular(
-                lower_factor, jnp.eye(PANEL, dtype=lower_factor.dtype), lower=True
-            )
+            lower_factor, inverse = factor_and_invert(corner)
         section_two = lax.all_to_all(onward, "col", split_axis=0, concat_axis=0, tiled=True)
         if k == 1:
             section_two, lower_factor, inverse = lax.optimization_barrier(

time: 564 us -> 557 us (0.988)
  waiting for transfers between devices: 158 us -> 188 us
  other arithmetic: 177 us -> 153 us
  local copies, waits for them, and re-layouts: 121 us -> 113 us
    all_to_all x2, waiting for transfers between devices: 0.01 us -> 41.5 us  [on_device(): lax.all_to_all(onward, 'col', split_axis=0, concat_axis=0, tiled=True)]
    another operation x19 -> x20, other arithmetic: 122 us -> 92.5 us  [the longest x12 50.4 us: factor_and_invert(): lpp = lax.linalg.cholesky(grid[p][p], symmetrize_input=False)]
    another operation x17 -> x5, local copies, waits for them, and re-layouts: 14.2 us -> 0.36 us  [the longest x4 0.36 us: factor_and_invert(): dinv = jax.scipy.linalg.solve_triangular(lpp, eye, lower=True)]
    another operation x13 -> x4, matrix products: 11.1 us -> 1.06 us  [factor_and_invert(): dinv = jax.scipy.linalg.solve_triangular(lpp, eye, lower=True)]
    dot_general x0 -> x32, matrix products: none -> 9.14 us  [the longest x10 2.86 us: factor_and_invert(): jnp.dot(low[i][p], low[j][p].T, precision=exact_mode)]
    all_gather x1, waiting for transfers between devices: 46.2 us -> 39.7 us  [on_device(): lax.all_gather(partial, 'col', axis=0, tiled=False)]
  transfers between devices with their start and end apart: 10 -> 10, of which waited for: 6 -> 7; matrix products, arithmetic and copies ran while one was open for 45% -> 40% of each run, Pallas kernels for 0% -> 0%
where the time goes in v6:
time: 557 us; the launch traced here: 550 us
  waiting for transfers between devices  188 us (34%)
  other arithmetic  153 us (27%)
  local copies, waits for them, and re-layouts  113 us (20%)
  matrix products  43.9 us (8%)
  starting transfers between devices  31.8 us (6%)
  between operations  20.2 us (4%)
    another operation x12, other arithmetic, factor_and_invert(): lpp = lax.linalg.cholesky(grid[p][p], symmetrize_input=False)  50.4 us
    all_gather x1, waiting for transfers between devices, on_device(): gathered = lax.all_gather(part, 'col', axis=0, tiled=False)  50.3 us
    another operation x8, other arithmetic, factor_and_invert(): dinv = jax.scipy.linalg.solve_triangular(lpp, eye, lower=True)  42 us
    all_to_all x2, waiting for transfers between devices, on_device(): lax.all_to_all(onward, 'col', split_axis=0, concat_axis=0, tiled=True)  41.5 us
    all_gather x1, waiting for transfers between devices, on_device(): lax.all_gather(partial, 'col', axis=0, tiled=False)  39.7 us
    gather x10, local copies, waits for them, and re-layouts, take_slabs(): return jnp.take(source, indices, axis=0)  34.8 us
    all_to_all x2, waiting for transfers between devices, on_device(): lax.all_to_all(outgoing, 'row', split_axis=0, concat_axis=0, tiled=True)  33 us
    dot_general x1, matrix products, on_device(): update = jnp.einsum('rp,cp->rc', panel_factor, across, precision=exact_mode)  24.1 us
  transfers between devices with their start and end apart: 10, of which 7 were waited for; matrix products, arithmetic and copies ran while one was open for 40% of the time, Pallas kernels for 0%

profile of v6, /device:TPU:6, one launch (start us, length us, event | category | flops | bytes accessed | tf_op | source)
XLA Modules:
  0.0 550.0 jit_solution(11035229789503652143)
XLA Ops:
  34.4 17.4 %all-to-all-done = f32[8,128,512]{2,1,0:T(8,128)S(1)} async-done(((f32[8,128,512]{2,1,0:T(8,128)}), f32[8,128,512]{2,1,0:T(8,128)S(1)}, u32[]{:S(2)}, u32[]{:S(2)}) %all-to-all-start) | async-done | bytes 2097184 | tf_op jit(solution)/shard_map/all_to_all | solution.py:112
  67.7 15.6 %all-to-all-done.1 = f32[8,128,512]{2,1,0:T(8,128)} async-done(((f32[8,128,512]{2,1,0:T(8,128)}), f32[8,128,512]{2,1,0:T(8,128)}, u32[]{:S(2)}, u32[]{:S(2)}) %all-to-all-start.1) | async-done | bytes 2097184 | tf_op jit(solution)/shard_map/all_to_all | solution.py:112
  96.7 39.7 %all-gather.12.cloned.1.call-done = f32[1024,512]{1,0:T(8,128)} async-done(((f32[64,512]{1,0:T(8,128)}), f32[1024,512]{1,0:T(8,128)}) %all-gather.12.cloned.1.call-update) | async-done | bytes 2097168 | tf_op jit(solution)/shard_map/all_gather | solution.py:130
  170.5 11.7 %custom-call.16 = f32[128,128]{1,0:T(8,128)S(1)} custom-call(f32[128,128]{1,0:T(8,128)S(1)} %slice.192), custom_call_target="Cholesky" | custom-call | tf_op jit(solution)/shard_map/cholesky/custom-call.1 | solution.py:26
  183.7 9.8 %custom-call.17 = f32[1,128,128]{1,2,0:T(8,128)S(1)} custom-call(f32[1,128,128]{2,1,0:T(8,128)S(1)} %get-tuple-element.30), custom_call_target="InvertDiagBlocksLowerTriangular" | custom-call | tf_op jit(solution)/shard_map/jit(_solve_triangular)/triangular_solve | solution.py:27
  195.3 12.1 %custom-call.18 = f32[128,128]{1,0:T(8,128)S(1)} custom-call(f32[128,128]{1,0:T(8,128)S(1)} %convolution_subtract_fusion.9), custom_call_target="Cholesky" | custom-call | tf_op jit(solution)/shard_map/cholesky/custom-call.1 | solution.py:26
  208.8 9.8 %custom-call.19 = f32[1,128,128]{1,2,0:T(8,128)S(1)} custom-call(f32[1,128,128]{2,1,0:T(8,128)S(1)} %get-tuple-element.28), custom_call_target="InvertDiagBlocksLowerTriangular" | custom-call | tf_op jit(solution)/shard_map/jit(_solve_triangular)/triangular_solve | solution.py:27
  220.0 11.7 %custom-call.20 = f32[128,128]{1,0:T(8,128)S(1)} custom-call(f32[128,128]{1,0:T(8,128)S(1)} %convolution_subtract_fusion.6), custom_call_target="Cholesky" | custom-call | tf_op jit(solution)/shard_map/cholesky/custom-call.1 | solution.py:26
  233.2 9.8 %custom-call.21 = f32[1,128,128]{1,2,0:T(8,128)S(1)} custom-call(f32[1,128,128]{2,1,0:T(8,128)S(1)} %get-tuple-element.26), custom_call_target="InvertDiagBlocksLowerTriangular" | custom-call | tf_op jit(solution)/shard_map/jit(_solve_triangular)/triangular_solve | solution.py:27
  246.3 11.9 %custom-call.22 = f32[128,128]{1,0:T(8,128)S(1)} custom-call(f32[128,128]{1,0:T(8,128)S(1)} %convolution_subtract_fusion), custom_call_target="Cholesky" | custom-call | tf_op jit(solution)/shard_map/cholesky/custom-call.1 | solution.py:26
  259.7 9.8 %custom-call.23 = f32[1,128,128]{1,2,0:T(8,128)S(1)} custom-call(f32[1,128,128]{2,1,0:T(8,128)S(1)} %get-tuple-element.24), custom_call_target="InvertDiagBlocksLowerTriangular" | custom-call | tf_op jit(solution)/shard_map/jit(_solve_triangular)/triangular_solve | solution.py:27
  270.4 7.2 %all-to-all-start.2 = ((f32[16,64,1024]{2,1,0:T(8,128)}), f32[16,64,1024]{2,1,0:T(8,128)}, u32[]{:S(2)}, u32[]{:S(2)}) async-start(f32[16,64,1024]{2,1,0:T(8,128)} %select_multiply_fusion.2), calls=%async_computation.2 | async-start | bytes 8388608 | tf_op jit(solution)/shard_map/all_to_all | solution.py:141
  289.0 41.5 %all-to-all-done.2 = f32[16,64,1024]{2,1,0:T(8,128)} async-done(((f32[16,64,1024]{2,1,0:T(8,128)}), f32[16,64,1024]{2,1,0:T(8,128)}, u32[]{:S(2)}, u32[]{:S(2)}) %all-to-all-start.2) | async-done | bytes 4194336 | tf_op jit(solution)/shard_map/all_to_all | solution.py:141
  351.1 50.3 %all-gather.8.cloned.1.call-done = f32[16,512,128]{2,1,0:T(8,128)} async-done(((f32[1,512,128]{2,1,0:T(8,128)}), f32[16,512,128]{2,1,0:T(8,128)}) %all-gather.8.cloned.1.call-update) | async-done | bytes 4194320 | tf_op jit(solution)/shard_map/all_gather | solution.py:171
  408.5 11.5 %copy.265 = f32[2,1024,8,64]{3,2,1,0:T(8,128)} copy(f32[2,1024,8,64]{3,1,2,0:T(8,128)} %bitcast.223) | data formatting | bytes 8388608 | tf_op jit(solution)/shard_map/transpose | solution.py:173
  420.0 7.6 %dot_general.136 = f32[32,64,512]{2,1,0:T(8,128)} reshape(f32[2,1024,8,64]{3,2,1,0:T(8,128)} %copy.265) | data formatting | bytes 8388608 | tf_op jit(solution)/shard_map/rp,qp->rq/dot_general | solution.py:175
  427.5 9.6 %select_select_fusion = f32[32,64,512]{2,1,0:T(8,128)S(1)} fusion(f32[32,64,512]{2,1,0:T(8,128)} %gather_fusion.2, f32[32,64,512]{2,1,0:T(8,128)} %dot_general.136, pred[32]{0:T(512)(128)(4,1)S(1)} %get-tuple-element.78, pred[32]{0:T(512)(128)(4,1)S(1)} %broadcast_compare_fusion.1, f32[512,512]{1,0:T(8,128)S(1)} %copy-done.2), kind=kOutput, calls=%fused_computation.26 | convolution fusion | flops 6444548096 | bytes 13631552 | tf_op jit(solution)/shard_map/rp,qp->rq/dot_general | solution.py:175
  443.9 16.0 %collective-permute-done.1 = f32[128,512]{1,0:T(8,128)S(1)} collective-permute-done((f32[128,512]{1,0:T(8,128)S(1)}, f32[128,512]{1,0:T(8,128)S(1)}, u32[]{:S(2)}, u32[]{:S(2)}) %collective-permute-start.1) | collective-permute-done | bytes 262176 | tf_op jit(solution)/shard_map/ppermute | solution.py:196
  461.3 8.5 %pad_maximum_fusion = f32[2,16,64,1024]{3,2,1,0:T(8,128)} fusion(f32[1,16,64,1024]{3,2,1,0:T(8,128)} %bitcast.46, f32[1,16,64,1024]{3,2,1,0:T(8,128)} %bitcast.31), kind=kLoop, calls=%fused_computation.16 | loop fusion | flops 2097152 | bytes 16777216 | tf_op jit(solution)/shard_map/stack | solution.py:147
  469.8 7.7 %gather_fusion.3 = f32[32,64,1024]{2,1,0:T(8,128)} fusion(f32[2,16,64,1024]{3,2,1,0:T(8,128)} %pad_maximum_fusion, s32[32]{0:T(128)S(1)} %reshape.596), kind=kCustom, calls=%fused_computation.13 | custom fusion | bytes 16777472 | tf_op jit(solution)/shard_map/vmap(jit(_take))/gather | solution.py:15
  483.9 8.7 %copy.258 = f32[2,1024,1024]{2,1,0:T(8,128)} copy(f32[2,1024,1024]{1,2,0:T(8,128)} %fusion.3) | data formatting | bytes 16777216 | tf_op jit(solution)/shard_map/transpose | solution.py:151
  492.5 12.5 %gather_fusion.4 = f32[64,64,1024]{2,1,0:T(8,128)} fusion(f32[2,16,64,1024]{3,2,1,0:T(8,128)} %bitcast.220, s32[64]{0:T(128)S(1)} %reshape.602), kind=kCustom, calls=%fused_computation.14 | custom fusion | bytes 33554944 | tf_op jit(solution)/shard_map/vmap(jit(_take))/gather | solution.py:15
  505.0 7.3 %select_multiply_fusion = f32[2,32,64,1024]{3,2,1,0:T(8,128)S(1)} fusion(f32[2,32,64,1024]{3,2,1,0:T(8,128)} %bitcast.221, f32[2,32]{1,0:T(2,128)S(1)} %fusion.35, pred[2,32]{1,0:T(4,128)(4,1)S(1)} %compare_and_fusion.12), kind=kLoop, calls=%fused_computation.15 | loop fusion | flops 8388608 | bytes 33554752 | tf_op jit(solution)/shard_map/mul | solution.py:152
  518.9 24.1 %fusion.1 = f32[2048,1024]{1,0:T(8,128)} fusion(f32[1,32,64,1024]{3,2,1,0:T(8,128)} %get-tuple-element.45, f32[2048,1024]{1,0:T(8,128)} %param.33, f32[1,32,64,1024]{3,2,1,0:T(8,128)} %get-tuple-element.44, pred[1024]{0:T(1024)(128)(4,1)S(1)} %fusion.48, pred[2048]{0:T(1024)(128)(4,1)S(1)} %fusion.42, f32[2048,512]{1,0:T(8,128)} %bitcast.225, ...), kind=kOutput, calls=%fused_computation.19 | convolution fusion | flops 12895387648 | bytes 39848960 | tf_op jit(solution)/shard_map/rp,cp->rc/dot_general | solution.py:198
  (232 shorter events, 158.0 us)
Async XLA Ops:
  11.0 0.6 copy-start.6
  21.8 8.5 %copy-start.5 = (s32[2,128]{1,0:T(2,128)S(1)}, s32[2,128]{1,0:T(2,128)}, u32[]{:S(2)}) copy-start(s32[2,128]{1,0:T(2,128)} %param.35) | copy-start | bytes 3076
  21.8 30.0 %all-to-all-start = ((f32[8,128,512]{2,1,0:T(8,128)}), f32[8,128,512]{2,1,0:T(8,128)S(1)}, u32[]{:S(2)}, u32[]{:S(2)}) async-start(f32[8,128,512]{2,1,0:T(8,128)} %bitcast.233), calls=%async_computation | async-start | bytes 4194304 | tf_op jit(solution)/shard_map/all_to_all | solution.py:112
  31.1 28.3 %copy-start.10 = (s32[2,128]{1,0:T(2,128)S(1)}, s32[2,128]{1,0:T(2,128)}, u32[]{:S(2)}) copy-start(s32[2,128]{1,0:T(2,128)} %param.36) | copy-start | bytes 3076
  51.8 34.8 %copy-start.1 = (f32[8,128,512]{2,1,0:T(8,128)}, f32[8,128,512]{2,1,0:T(8,128)S(1)}, u32[]{:S(2)}) copy-start(f32[8,128,512]{2,1,0:T(8,128)S(1)} %all-to-all-done) | copy-start | bytes 6291460
  51.8 31.5 %all-to-all-start.1 = ((f32[8,128,512]{2,1,0:T(8,128)}), f32[8,128,512]{2,1,0:T(8,128)}, u32[]{:S(2)}, u32[]{:S(2)}) async-start(f32[8,128,512]{2,1,0:T(8,128)} %bitcast.232), calls=%async_computation.1 | async-start | bytes 4194304 | tf_op jit(solution)/shard_map/all_to_all | solution.py:112
  58.2 78.2 %all-gather.12.cloned.1.call-start = ((), (), s32[]{:S(2)}) async-start(), calls=%async_computation.7 | async-start | bytes 2228224 | tf_op jit(solution)/shard_map/all_gather | solution.py:130
  63.8 29.3 %slice-start = ((f32[2048,1024]{1,0:T(8,128)}), f32[2048,64]{1,0:T(8,128)S(1)}, s32[]{:S(2)}) async-start(f32[2048,1024]{1,0:T(8,128)} %param.33), calls=%async_computation.8 | async-start | bytes 2097152 | tf_op jit(solution)/shard_map/slice | solution.py:157
  86.6 52.9 %copy-start.7 = (s32[2,8]{1,0:T(2,128)S(1)}, s32[2,8]{1,0:T(2,128)}, u32[]{:S(2)}) copy-start(s32[2,8]{1,0:T(2,128)} %copy-done.6) | copy-start | bytes 196
  89.1 78.4 %all-gather.6.cloned.1.call-start = ((), (), s32[]{:S(2)}) async-start(), calls=%async_computation.4 | async-start | bytes 1179648 | tf_op jit(solution)/shard_map/all_gather | solution.py:131
  144.4 4.4 copy-start.9
  154.1 116.4 %all-to-all-start.3 = ((f32[16,64,1024]{2,1,0:T(8,128)}), f32[16,64,1024]{2,1,0:T(8,128)}, u32[]{:S(2)}, u32[]{:S(2)}) async-start(f32[16,64,1024]{2,1,0:T(8,128)} %select_multiply_fusion.1), calls=%async_computation.3 | async-start | bytes 8388608 | tf_op jit(solution)/shard_map/all_to_all | solution.py:141
  159.4 2.8 copy-start.8
  270.4 60.0 %all-to-all-start.2 = ((f32[16,64,1024]{2,1,0:T(8,128)}), f32[16,64,1024]{2,1,0:T(8,128)}, u32[]{:S(2)}, u32[]{:S(2)}) async-start(f32[16,64,1024]{2,1,0:T(8,128)} %select_multiply_fusion.2), calls=%async_computation.2 | async-start | bytes 8388608 | tf_op jit(solution)/shard_map/all_to_all | solution.py:141
  277.7 123.7 %all-gather.8.cloned.1.call-start = ((), (), s32[]{:S(2)}) async-start(), calls=%async_computation.5 | async-start | bytes 4456448 | tf_op jit(solution)/shard_map/all_gather | solution.py:171
  286.5 49.0 %copy-start.3 = (f32[2048,64]{0,1:T(8,128)S(1)}, f32[2048,64]{0,1:T(8,128)}, u32[]{:S(2)}) copy-start(f32[2048,64]{0,1:T(8,128)} %copy.273) | copy-start | bytes 1572868
  336.7 10.4 %collective-permute-start = (f32[2048,64]{0,1:T(8,128)S(1)}, f32[2048,64]{0,1:T(8,128)S(1)}, u32[]{:S(2)}, u32[]{:S(2)}) collective-permute-start(f32[2048,64]{0,1:T(8,128)S(1)} %add_add_fusion), channel_id=1, source_target_pairs={{0,8},{1,9},{2,10},{3,11},{4,12},{5,13},{6,14},{7,15},{16,24},{17,... | collective-permute-start | bytes 1572872 | tf_op jit(solution)/shard_map/ppermute | solution.py:164
  348.1 170.8 %all-gather.10.cloned.1.call-start = ((), (), s32[]{:S(2)}) async-start(), calls=%async_computation.6 | async-start | bytes 2359296 | tf_op jit(solution)/shard_map/all_gather | solution.py:197
  420.0 7.6 %copy-start.2 = (f32[512,512]{1,0:T(8,128)S(1)}, f32[512,512]{1,0:T(8,128)}, u32[]{:S(2)}) copy-start(f32[512,512]{1,0:T(8,128)} %fusion.9) | copy-start | bytes 3145732
  437.2 2.0 copy-start
  439.4 20.6 %collective-permute-start.1 = (f32[128,512]{1,0:T(8,128)S(1)}, f32[128,512]{1,0:T(8,128)S(1)}, u32[]{:S(2)}, u32[]{:S(2)}) collective-permute-start(f32[128,512]{1,0:T(8,128)S(1)} %constant_dynamic-slice_fusion.1), channel_id=1, source_target_pairs={{0,0},{1,16},{2,32},{3,48},{4,64},{5,80},{6,96},{7,112},{8,8},{9,2... | collective-permute-start | bytes 786440 | tf_op jit(solution)/shard_map/ppermute | solution.py:196
  460.0 0.7 copy-start.4
Sparse Core Ops, SparseCore 0:
  89.2 47.0 all-gather.11
  138.9 20.8 all-gather.5
  348.2 53.0 all-gather.7
  460.9 22.2 all-gather.9

commit v7 on v6

--- a/solution.py
+++ b/solution.py
@@ -136,7 +136,6 @@
         onward = take_slabs(flipped, src_col[k]) * has_col[k][:, None, None]
         onward = onward.reshape(col_slots * BLK, row_slots * BLK)
         if k == 0:
-            onward, corner = lax.optimization_barrier((onward, corner))
             lower_factor, inverse = factor_and_invert(corner)
         section_two = lax.all_to_all(onward, "col", split_axis=0, concat_axis=0, tiled=True)
         if k == 1:
@@ -169,6 +168,7 @@
     part = lax.dynamic_slice_in_dim(mine, (col_place // panel_width) * part_rows, part_rows, axis=0)
     part = part.reshape(part_rows * BLK // 128, 128)
     gathered = lax.all_gather(part, "col", axis=0, tiled=False)
+    gathered, extended = lax.optimization_barrier((gathered, extended))
     gathered = gathered.reshape(spread, panel_width, part_rows, BLK)
     panel_cols = gathered.transpose(0, 2, 1, 3).reshape(local_rows, PANEL)
 

time: 557 us -> 527 us (0.946)
  the two profiles are of different devices: /device:TPU:6 before, /device:TPU:1 now
where the time goes in v7:
time: 527 us; the launch traced here: 520 us
  other arithmetic  160 us (30%)
  waiting for transfers between devices  156 us (30%)
  local copies, waits for them, and re-layouts  108 us (20%)
  matrix products  38.6 us (7%)
  starting transfers between devices  37.4 us (7%)
  between operations  20.4 us (4%)
    all_gather x1, waiting for transfers between devices, on_device(): lax.all_gather(partial, 'col', axis=0, tiled=False)  61.1 us
    another operation x12, other arithmetic, factor_and_invert(): lpp = lax.linalg.cholesky(grid[p][p], symmetrize_input=False)  50 us
    another operation x8, other arithmetic, factor_and_invert(): dinv = jax.scipy.linalg.solve_triangular(lpp, eye, lower=True)  41.5 us
    all_to_all x2, waiting for transfers between devices, on_device(): lax.all_to_all(outgoing, 'row', split_axis=0, concat_axis=0, tiled=True)  37.7 us
    all_gather x1, waiting for transfers between devices, on_device(): across = lax.all_gather(piece, 'row', axis=0, tiled=True)  37 us
    gather x10, local copies, waits for them, and re-layouts, take_slabs(): return jnp.take(source, indices, axis=0)  33.9 us
    dot_general x1, matrix products, on_device(): update = jnp.einsum('rp,cp->rc', panel_factor, across, precision=exact_mode)  18.8 us
    all_to_all x2, starting transfers between devices, on_device(): lax.all_to_all(onward, 'col', split_axis=0, concat_axis=0, tiled=True)  18 us
  transfers between devices with their start and end apart: 10, of which 7 were waited for; matrix products, arithmetic and copies ran while one was open for 43% of the time, Pallas kernels for 0%

profile of v7, /device:TPU:1, one launch (start us, length us, event | category | flops | bytes accessed | tf_op | source)
XLA Modules:
  0.0 519.6 jit_solution(3207175311625668408)
XLA Ops:
  34.1 18.5 %all-to-all-done = f32[8,128,512]{2,1,0:T(8,128)S(1)} async-done(((f32[8,128,512]{2,1,0:T(8,128)}), f32[8,128,512]{2,1,0:T(8,128)S(1)}, u32[]{:S(2)}, u32[]{:S(2)}) %all-to-all-start) | async-done | bytes 2097184 | tf_op jit(solution)/shard_map/all_to_all | solution.py:112
  65.5 19.1 %all-to-all-done.2 = f32[8,128,512]{2,1,0:T(8,128)S(1)} async-done(((f32[8,128,512]{2,1,0:T(8,128)}), f32[8,128,512]{2,1,0:T(8,128)S(1)}, u32[]{:S(2)}, u32[]{:S(2)}) %all-to-all-start.2) | async-done | bytes 2097184 | tf_op jit(solution)/shard_map/all_to_all | solution.py:112
  97.3 8.0 %all-to-all-start.1 = ((f32[16,64,1024]{2,1,0:T(8,128)}), f32[16,64,1024]{2,1,0:T(8,128)}, u32[]{:S(2)}, u32[]{:S(2)}) async-start(f32[16,64,1024]{2,1,0:T(8,128)} %select_multiply_fusion.2), calls=%async_computation.1 | async-start | bytes 8388608 | tf_op jit(solution)/shard_map/all_to_all | solution.py:140
  111.2 61.1 %all-gather.12.cloned.1.call-done = f32[1024,512]{1,0:T(8,128)} async-done(((f32[64,512]{1,0:T(8,128)}), f32[1024,512]{1,0:T(8,128)}) %all-gather.12.cloned.1.call-update) | async-done | bytes 2097168 | tf_op jit(solution)/shard_map/all_gather | solution.py:130
  185.4 10.1 %all-to-all-start.3 = ((f32[16,64,1024]{2,1,0:T(8,128)}), f32[16,64,1024]{2,1,0:T(8,128)}, u32[]{:S(2)}, u32[]{:S(2)}) async-start(f32[16,64,1024]{2,1,0:T(8,128)} %select_multiply_fusion.1), calls=%async_computation.3 | async-start | bytes 8388608 | tf_op jit(solution)/shard_map/all_to_all | solution.py:140
  206.3 11.7 %custom-call.16 = f32[128,128]{1,0:T(8,128)S(1)} custom-call(f32[128,128]{1,0:T(8,128)S(1)} %slice.192), custom_call_target="Cholesky" | custom-call | tf_op jit(solution)/shard_map/cholesky/custom-call.1 | solution.py:26
  219.3 9.8 %custom-call.17 = f32[1,128,128]{1,2,0:T(8,128)S(1)} custom-call(f32[1,128,128]{2,1,0:T(8,128)S(1)} %get-tuple-element.32), custom_call_target="InvertDiagBlocksLowerTriangular" | custom-call | tf_op jit(solution)/shard_map/jit(_solve_triangular)/triangular_solve | solution.py:27
  232.0 12.1 %custom-call.18 = f32[128,128]{1,0:T(8,128)S(1)} custom-call(f32[128,128]{1,0:T(8,128)S(1)} %convolution_subtract_fusion.9), custom_call_target="Cholesky" | custom-call | tf_op jit(solution)/shard_map/cholesky/custom-call.1 | solution.py:26
  245.3 9.8 %custom-call.19 = f32[1,128,128]{1,2,0:T(8,128)S(1)} custom-call(f32[1,128,128]{2,1,0:T(8,128)S(1)} %get-tuple-element.30), custom_call_target="InvertDiagBlocksLowerTriangular" | custom-call | tf_op jit(solution)/shard_map/jit(_solve_triangular)/triangular_solve | solution.py:27
  256.9 11.7 %custom-call.20 = f32[128,128]{1,0:T(8,128)S(1)} custom-call(f32[128,128]{1,0:T(8,128)S(1)} %convolution_subtract_fusion.6), custom_call_target="Cholesky" | custom-call | tf_op jit(solution)/shard_map/cholesky/custom-call.1 | solution.py:26
  269.8 9.8 %custom-call.21 = f32[1,128,128]{1,2,0:T(8,128)S(1)} custom-call(f32[1,128,128]{2,1,0:T(8,128)S(1)} %get-tuple-element.28), custom_call_target="InvertDiagBlocksLowerTriangular" | custom-call | tf_op jit(solution)/shard_map/jit(_solve_triangular)/triangular_solve | solution.py:27
  280.8 11.9 %custom-call.22 = f32[128,128]{1,0:T(8,128)S(1)} custom-call(f32[128,128]{1,0:T(8,128)S(1)} %convolution_subtract_fusion), custom_call_target="Cholesky" | custom-call | tf_op jit(solution)/shard_map/cholesky/custom-call.1 | solution.py:26
  293.8 9.8 %custom-call.23 = f32[1,128,128]{1,2,0:T(8,128)S(1)} custom-call(f32[1,128,128]{2,1,0:T(8,128)S(1)} %get-tuple-element.26), custom_call_target="InvertDiagBlocksLowerTriangular" | custom-call | tf_op jit(solution)/shard_map/jit(_solve_triangular)/triangular_solve | solution.py:27
  321.5 10.9 %collective-permute-done = f32[2048,64]{0,1:T(8,128)S(1)} collective-permute-done((f32[2048,64]{0,1:T(8,128)S(1)}, f32[2048,64]{0,1:T(8,128)S(1)}, u32[]{:S(2)}, u32[]{:S(2)}) %collective-permute-start) | collective-permute-done | bytes 524320 | tf_op jit(solution)/shard_map/ppermute | solution.py:163
  334.1 8.5 %pad_maximum_fusion = f32[2,16,64,1024]{3,2,1,0:T(8,128)} fusion(f32[1,16,64,1024]{3,2,1,0:T(8,128)} %bitcast.61, f32[1,16,64,1024]{3,2,1,0:T(8,128)} %bitcast.60), kind=kLoop, calls=%fused_computation.16 | loop fusion | flops 2097152 | bytes 16777216 | tf_op jit(solution)/shard_map/stack | solution.py:146
  342.7 7.9 %gather_fusion.3 = f32[32,64,1024]{2,1,0:T(8,128)} fusion(f32[2,16,64,1024]{3,2,1,0:T(8,128)} %pad_maximum_fusion, s32[32]{0:T(128)S(1)} %reshape.594), kind=kCustom, calls=%fused_computation.13 | custom fusion | bytes 16777472 | tf_op jit(solution)/shard_map/vmap(jit(_take))/gather | solution.py:15
  356.8 8.7 %copy.264 = f32[2,1024,1024]{2,1,0:T(8,128)} copy(f32[2,1024,1024]{1,2,0:T(8,128)} %fusion.1) | data formatting | bytes 16777216 | tf_op jit(solution)/shard_map/transpose | solution.py:150
  365.4 13.1 %gather_fusion.4 = f32[64,64,1024]{2,1,0:T(8,128)} fusion(f32[2,16,64,1024]{3,2,1,0:T(8,128)} %bitcast.214, s32[64]{0:T(128)S(1)} %reshape.600), kind=kCustom, calls=%fused_computation.14 | custom fusion | bytes 33554944 | tf_op jit(solution)/shard_map/vmap(jit(_take))/gather | solution.py:15
  395.4 13.7 %bitcast_add_fusion = f32[2048,1024]{1,0:T(8,128)} fusion(f32[1,32,64,1024]{3,2,1,0:T(8,128)} %get-tuple-element.45, f32[2048,1024]{1,0:T(8,128)} %param.33, f32[1,32,64,1024]{3,2,1,0:T(8,128)} %get-tuple-element.44), kind=kLoop, calls=%fused_computation.17 | loop fusion | flops 4194304 | bytes 33554432 | tf_op jit(solution)/shard_map/add | solution.py:153
  416.0 11.4 %copy.265 = f32[2,1024,8,64]{3,2,1,0:T(8,128)} copy(f32[2,1024,8,64]{3,1,2,0:T(8,128)} %bitcast.220) | data formatting | bytes 8388608 | tf_op jit(solution)/shard_map/transpose | solution.py:173
  427.4 7.8 %dot_general.136 = f32[32,64,512]{2,1,0:T(8,128)} reshape(f32[2,1024,8,64]{3,2,1,0:T(8,128)} %copy.265) | data formatting | bytes 8388608 | tf_op jit(solution)/shard_map/rp,qp->rq/dot_general | solution.py:175
  435.2 9.6 %select_select_fusion = f32[32,64,512]{2,1,0:T(8,128)S(1)} fusion(f32[32,64,512]{2,1,0:T(8,128)} %gather_fusion.2, f32[32,64,512]{2,1,0:T(8,128)} %dot_general.136, pred[32]{0:T(512)(128)(4,1)S(1)} %get-tuple-element.78, pred[32]{0:T(512)(128)(4,1)S(1)} %broadcast_compare_fusion.1, f32[512,512]{1,0:T(8,128)S(1)} %copy-done.3), kind=kOutput, calls=%fused_computation.25 | convolution fusion | flops 6444548096 | bytes 13631552 | tf_op jit(solution)/shard_map/rp,qp->rq/dot_general | solution.py:175
  456.9 37.0 %all-gather.10.cloned.1.call-done = f32[1024,512]{1,0:T(8,128)} async-done(((f32[128,512]{1,0:T(8,128)}), f32[1024,512]{1,0:T(8,128)}) %all-gather.10.cloned.1.call-update) | async-done | bytes 2097168 | tf_op jit(solution)/shard_map/all_gather | solution.py:197
  493.9 18.8 %subtract_select_fusion = f32[2048,1024]{1,0:T(8,128)} fusion(f32[2048,1024]{1,0:T(8,128)} %bitcast_add_fusion, pred[1024]{0:T(1024)(128)(4,1)S(1)} %fusion.46, pred[2048]{0:T(1024)(128)(4,1)S(1)} %fusion.40, f32[2048,512]{1,0:T(8,128)} %bitcast.217, f32[1024,512]{1,0:T(8,128)} %all-gather.10.cloned.1.call-done), kind=kOutput, calls=%fused_computation.22 | convolution fusion | flops 12891193344 | bytes 23071744 | tf_op jit(solution)/shard_map/rp,cp->rc/dot_general | solution.py:198
  (227 shorter events, 148.4 us)
Async XLA Ops:
  20.5 9.5 %copy-start.6 = (s32[2,128]{1,0:T(2,128)S(1)}, s32[2,128]{1,0:T(2,128)}, u32[]{:S(2)}) copy-start(s32[2,128]{1,0:T(2,128)} %param.35) | copy-start | bytes 3076
  20.5 32.1 %all-to-all-start = ((f32[8,128,512]{2,1,0:T(8,128)}), f32[8,128,512]{2,1,0:T(8,128)S(1)}, u32[]{:S(2)}, u32[]{:S(2)}) async-start(f32[8,128,512]{2,1,0:T(8,128)} %bitcast.229), calls=%async_computation | async-start | bytes 4194304 | tf_op jit(solution)/shard_map/all_to_all | solution.py:112
  30.8 28.9 %copy-start.7 = (s32[2,128]{1,0:T(2,128)S(1)}, s32[2,128]{1,0:T(2,128)}, u32[]{:S(2)}) copy-start(s32[2,128]{1,0:T(2,128)} %param.36) | copy-start | bytes 3076
  52.6 1.3 copy-start.2
  53.9 30.7 %all-to-all-start.2 = ((f32[8,128,512]{2,1,0:T(8,128)}), f32[8,128,512]{2,1,0:T(8,128)S(1)}, u32[]{:S(2)}, u32[]{:S(2)}) async-start(f32[8,128,512]{2,1,0:T(8,128)} %bitcast.228), calls=%async_computation.2 | async-start | bytes 4194304 | tf_op jit(solution)/shard_map/all_to_all | solution.py:112
  58.4 113.9 %all-gather.12.cloned.1.call-start = ((), (), s32[]{:S(2)}) async-start(), calls=%async_computation.7 | async-start | bytes 2228224 | tf_op jit(solution)/shard_map/all_gather | solution.py:130
  84.6 2.6 copy-start.1
  97.3 11.4 %slice-start = ((f32[2048,1024]{1,0:T(8,128)}), f32[2048,64]{1,0:T(8,128)S(1)}, s32[]{:S(2)}) async-start(f32[2048,1024]{1,0:T(8,128)} %param.33), calls=%async_computation.8 | async-start | bytes 2097152 | tf_op jit(solution)/shard_map/slice | solution.py:156
  97.3 88.1 %all-to-all-start.1 = ((f32[16,64,1024]{2,1,0:T(8,128)}), f32[16,64,1024]{2,1,0:T(8,128)}, u32[]{:S(2)}, u32[]{:S(2)}) async-start(f32[16,64,1024]{2,1,0:T(8,128)} %select_multiply_fusion.2), calls=%async_computation.1 | async-start | bytes 8388608 | tf_op jit(solution)/shard_map/all_to_all | solution.py:140
  105.2 98.1 %all-gather.6.cloned.1.call-start = ((), (), s32[]{:S(2)}) async-start(), calls=%async_computation.4 | async-start | bytes 1179648 | tf_op jit(solution)/shard_map/all_gather | solution.py:131
  185.4 125.1 %all-to-all-start.3 = ((f32[16,64,1024]{2,1,0:T(8,128)}), f32[16,64,1024]{2,1,0:T(8,128)}, u32[]{:S(2)}, u32[]{:S(2)}) async-start(f32[16,64,1024]{2,1,0:T(8,128)} %select_multiply_fusion.1), calls=%async_computation.3 | async-start | bytes 8388608 | tf_op jit(solution)/shard_map/all_to_all | solution.py:140
  195.5 213.5 %all-gather.8.cloned.1.call-start = ((), (), s32[]{:S(2)}) async-start(), calls=%async_computation.5 | async-start | bytes 4456448 | tf_op jit(solution)/shard_map/all_gather | solution.py:170
  310.5 5.2 copy-start.4
  316.8 15.6 %collective-permute-start = (f32[2048,64]{0,1:T(8,128)S(1)}, f32[2048,64]{0,1:T(8,128)S(1)}, u32[]{:S(2)}, u32[]{:S(2)}) collective-permute-start(f32[2048,64]{0,1:T(8,128)S(1)} %add_add_fusion), channel_id=1, source_target_pairs={{0,8},{1,9},{2,10},{3,11},{4,12},{5,13},{6,14},{7,15},{16,24},{17,... | collective-permute-start | bytes 1572872 | tf_op jit(solution)/shard_map/ppermute | solution.py:163
  333.5 160.4 %all-gather.10.cloned.1.call-start = ((), (), s32[]{:S(2)}) async-start(), calls=%async_computation.6 | async-start | bytes 2359296 | tf_op jit(solution)/shard_map/all_gather | solution.py:197
  427.4 7.8 %copy-start.3 = (f32[512,512]{1,0:T(8,128)S(1)}, f32[512,512]{1,0:T(8,128)}, u32[]{:S(2)}) copy-start(f32[512,512]{1,0:T(8,128)} %fusion.7) | copy-start | bytes 3145732
  444.9 2.0 copy-start
  447.1 9.0 %collective-permute-start.1 = (f32[128,512]{1,0:T(8,128)S(1)}, f32[128,512]{1,0:T(8,128)S(1)}, u32[]{:S(2)}, u32[]{:S(2)}) collective-permute-start(f32[128,512]{1,0:T(8,128)S(1)} %constant_dynamic-slice_fusion.1), channel_id=1, source_target_pairs={{0,0},{1,16},{2,32},{3,48},{4,64},{5,80},{6,96},{7,112},{8,8},{9,2... | collective-permute-start | bytes 786440 | tf_op jit(solution)/shard_map/ppermute | solution.py:196
  456.1 0.7 copy-start.5
Sparse Core Ops, SparseCore 0:
  87.3 84.9 all-gather.11
  174.8 28.4 all-gather.5
  333.6 52.6 all-gather.7
  457.0 36.8 all-gather.9

commit v8 on v7

--- a/solution.py
+++ b/solution.py
@@ -127,7 +127,10 @@
         slab = (slab * row_weight[k, 0]).reshape(BLK, child_colblk, BLK)
         picked_cols = jnp.take(slab, corner_cpick[k], axis=1) * corner_cw[k][None, :, None]
         partial = partial + picked_cols.reshape(BLK, PANEL)
-    corner_row = jnp.sum(lax.all_gather(partial, "col", axis=0, tiled=False), axis=0)
+    share = partial.reshape(col_count, BLK // col_count, PANEL)
+    share = lax.all_to_all(share, "col", split_axis=0, concat_axis=0, tiled=True)
+    share = jnp.sum(share, axis=0)
+    corner_row = lax.all_gather(share, "col", axis=0, tiled=True)
     corner = lax.all_gather(corner_row, "row", axis=0, tiled=True)
 
     arrived = []

time: 527 us -> 531 us (level)
  waiting for transfers between devices: 156 us -> 116 us
  blocking collectives: 0 us -> 18.2 us
  starting transfers between devices: 37.4 us -> 50.8 us
  local copies, waits for them, and re-layouts: 108 us -> 115 us
    all_gather x1 -> x0, waiting for transfers between devices: 61.1 us -> none  [on_device(): lax.all_gather(partial, 'col', axis=0, tiled=False)]
    all_to_all x2, waiting for transfers between devices: 0.01 us -> 34.3 us  [on_device(): lax.all_to_all(onward, 'col', split_axis=0, concat_axis=0, tiled=True)]
    all_gather x0 -> x1, blocking collectives: none -> 18.2 us  [on_device(): corner_row = lax.all_gather(share, 'col', axis=0, tiled=True)]
    ppermute x1, starting transfers between devices: 3.96 us -> 16.7 us  [on_device(): piece = lax.ppermute(piece, ('row', 'col'), pairs)]
    all_to_all x0 -> x1, starting transfers between devices: none -> 7.77 us  [on_device(): lax.all_to_all(share, 'col', split_axis=0, concat_axis=0, tiled=True)]
    all_to_all x2, starting transfers between devices: 18 us -> 11.5 us  [on_device(): lax.all_to_all(onward, 'col', split_axis=0, concat_axis=0, tiled=True)]
  transfers between devices with their start and end apart: 10 -> 10, of which waited for: 7 -> 7; matrix products, arithmetic and copies ran while one was open for 43% -> 45% of each run, Pallas kernels for 0% -> 0%
where the time goes in v8:
time: 531 us; the launch traced here: 524 us
  other arithmetic  165 us (31%)
  waiting for transfers between devices  116 us (22%)
  local copies, waits for them, and re-layouts  115 us (22%)
  starting transfers between devices  50.8 us (10%)
  matrix products  38.6 us (7%)
  between operations  20.1 us (4%)
  blocking collectives  18.2 us (3%)
    another operation x12, other arithmetic, factor_and_invert(): lpp = lax.linalg.cholesky(grid[p][p], symmetrize_input=False)  50 us
    another operation x8, other arithmetic, factor_and_invert(): dinv = jax.scipy.linalg.solve_triangular(lpp, eye, lower=True)  41.5 us
    all_gather x1, waiting for transfers between devices, on_device(): across = lax.all_gather(piece, 'row', axis=0, tiled=True)  37.1 us
    gather x10, local copies, waits for them, and re-layouts, take_slabs(): return jnp.take(source, indices, axis=0)  34.8 us
    all_to_all x2, waiting for transfers between devices, on_device(): lax.all_to_all(onward, 'col', split_axis=0, concat_axis=0, tiled=True)  34.3 us
    all_to_all x2, waiting for transfers between devices, on_device(): lax.all_to_all(outgoing, 'row', split_axis=0, concat_axis=0, tiled=True)  33.9 us
    dot_general x1, matrix products, on_device(): update = jnp.einsum('rp,cp->rc', panel_factor, across, precision=exact_mode)  18.8 us
    all_gather x1, blocking collectives, on_device(): corner_row = lax.all_gather(share, 'col', axis=0, tiled=True)  18.2 us
  transfers between devices with their start and end apart: 10, of which 7 were waited for; matrix products, arithmetic and copies ran while one was open for 45% of the time, Pallas kernels for 0%

profile of v8, /device:TPU:1, one launch (start us, length us, event | category | flops | bytes accessed | tf_op | source)
XLA Modules:
  0.0 524.2 jit_solution(7537856804009024907)
XLA Ops:
  36.3 17.0 %all-to-all-done = f32[8,128,512]{2,1,0:T(8,128)S(1)} async-done(((f32[8,128,512]{2,1,0:T(8,128)}), f32[8,128,512]{2,1,0:T(8,128)S(1)}, u32[]{:S(2)}, u32[]{:S(2)}) %all-to-all-start) | async-done | bytes 2097184 | tf_op jit(solution)/shard_map/all_to_all | solution.py:112
  68.1 16.8 %all-to-all-done.2 = f32[8,128,512]{2,1,0:T(8,128)} async-done(((f32[8,128,512]{2,1,0:T(8,128)}), f32[8,128,512]{2,1,0:T(8,128)}, u32[]{:S(2)}, u32[]{:S(2)}) %all-to-all-start.2) | async-done | bytes 2097184 | tf_op jit(solution)/shard_map/all_to_all | solution.py:112
  90.8 7.8 %all-to-all-start.4 = ((f32[16,4,512]{2,1,0:T(4,128)}), f32[16,4,512]{2,1,0:T(4,128)S(1)}, u32[]{:S(2)}, u32[]{:S(2)}) async-start(f32[16,4,512]{2,1,0:T(4,128)} %reshape.486), calls=%async_computation.4 | async-start | bytes 262144 | tf_op jit(solution)/shard_map/all_to_all | solution.py:131
  105.3 18.2 %all-gather = f32[16,4,512]{2,1,0:T(4,128)S(1)} all-gather(f32[1,4,512]{2,1,0:T(4,128)S(1)} %bitcast.235), channel_id=1, replica_groups=mesh['row'=8,'col'=16] {'col'}, dimensions={0}, use_global_device_ids=true | all-gather | bytes 139264 | tf_op jit(solution)/shard_map/all_gather | solution.py:133
  158.1 11.7 %custom-call.16 = f32[128,128]{1,0:T(8,128)S(1)} custom-call(f32[128,128]{1,0:T(8,128)S(1)} %slice.192), custom_call_target="Cholesky" | custom-call | tf_op jit(solution)/shard_map/cholesky/custom-call.1 | solution.py:26
  171.0 9.8 %custom-call.17 = f32[1,128,128]{1,2,0:T(8,128)S(1)} custom-call(f32[1,128,128]{2,1,0:T(8,128)S(1)} %get-tuple-element.32), custom_call_target="InvertDiagBlocksLowerTriangular" | custom-call | tf_op jit(solution)/shard_map/jit(_solve_triangular)/triangular_solve | solution.py:27
  182.5 12.1 %custom-call.18 = f32[128,128]{1,0:T(8,128)S(1)} custom-call(f32[128,128]{1,0:T(8,128)S(1)} %convolution_subtract_fusion.9), custom_call_target="Cholesky" | custom-call | tf_op jit(solution)/shard_map/cholesky/custom-call.1 | solution.py:26
  195.8 9.8 %custom-call.19 = f32[1,128,128]{1,2,0:T(8,128)S(1)} custom-call(f32[1,128,128]{2,1,0:T(8,128)S(1)} %get-tuple-element.30), custom_call_target="InvertDiagBlocksLowerTriangular" | custom-call | tf_op jit(solution)/shard_map/jit(_solve_triangular)/triangular_solve | solution.py:27
  207.0 11.7 %custom-call.20 = f32[128,128]{1,0:T(8,128)S(1)} custom-call(f32[128,128]{1,0:T(8,128)S(1)} %convolution_subtract_fusion.6), custom_call_target="Cholesky" | custom-call | tf_op jit(solution)/shard_map/cholesky/custom-call.1 | solution.py:26
  219.9 9.8 %custom-call.21 = f32[1,128,128]{1,2,0:T(8,128)S(1)} custom-call(f32[1,128,128]{2,1,0:T(8,128)S(1)} %get-tuple-element.28), custom_call_target="InvertDiagBlocksLowerTriangular" | custom-call | tf_op jit(solution)/shard_map/jit(_solve_triangular)/triangular_solve | solution.py:27
  233.1 11.9 %custom-call.22 = f32[128,128]{1,0:T(8,128)S(1)} custom-call(f32[128,128]{1,0:T(8,128)S(1)} %convolution_subtract_fusion), custom_call_target="Cholesky" | custom-call | tf_op jit(solution)/shard_map/cholesky/custom-call.1 | solution.py:26
  246.1 9.8 %custom-call.23 = f32[1,128,128]{1,2,0:T(8,128)S(1)} custom-call(f32[1,128,128]{2,1,0:T(8,128)S(1)} %get-tuple-element.26), custom_call_target="InvertDiagBlocksLowerTriangular" | custom-call | tf_op jit(solution)/shard_map/jit(_solve_triangular)/triangular_solve | solution.py:27
  275.0 34.3 %all-to-all-done.1 = f32[16,64,1024]{2,1,0:T(8,128)} async-done(((f32[16,64,1024]{2,1,0:T(8,128)}), f32[16,64,1024]{2,1,0:T(8,128)}, u32[]{:S(2)}, u32[]{:S(2)}) %all-to-all-start.1) | async-done | bytes 4194336 | tf_op jit(solution)/shard_map/all_to_all | solution.py:143
  327.0 8.5 %pad_maximum_fusion = f32[2,16,64,1024]{3,2,1,0:T(8,128)} fusion(f32[1,16,64,1024]{3,2,1,0:T(8,128)} %bitcast.61, f32[1,16,64,1024]{3,2,1,0:T(8,128)} %bitcast.60), kind=kLoop, calls=%fused_computation.16 | loop fusion | flops 2097152 | bytes 16777216 | tf_op jit(solution)/shard_map/stack | solution.py:149
  335.5 7.7 %gather_fusion.3 = f32[32,64,1024]{2,1,0:T(8,128)} fusion(f32[2,16,64,1024]{3,2,1,0:T(8,128)} %pad_maximum_fusion, s32[32]{0:T(128)S(1)} %reshape.598), kind=kCustom, calls=%fused_computation.13 | custom fusion | bytes 16777472 | tf_op jit(solution)/shard_map/vmap(jit(_take))/gather | solution.py:15
  349.4 8.7 %copy.266 = f32[2,1024,1024]{2,1,0:T(8,128)} copy(f32[2,1024,1024]{1,2,0:T(8,128)} %fusion.1) | data formatting | bytes 16777216 | tf_op jit(solution)/shard_map/transpose | solution.py:153
  358.1 12.6 %gather_fusion.4 = f32[64,64,1024]{2,1,0:T(8,128)} fusion(f32[2,16,64,1024]{3,2,1,0:T(8,128)} %bitcast.214, s32[64]{0:T(128)S(1)} %reshape.604), kind=kCustom, calls=%fused_computation.14 | custom fusion | bytes 33554944 | tf_op jit(solution)/shard_map/vmap(jit(_take))/gather | solution.py:15
  387.8 13.9 %bitcast_add_fusion = f32[2048,1024]{1,0:T(8,128)} fusion(f32[1,32,64,1024]{3,2,1,0:T(8,128)} %get-tuple-element.45, f32[2048,1024]{1,0:T(8,128)} %param.33, f32[1,32,64,1024]{3,2,1,0:T(8,128)} %get-tuple-element.44), kind=kLoop, calls=%fused_computation.17 | loop fusion | flops 4194304 | bytes 33554432 | tf_op jit(solution)/shard_map/add | solution.py:156
  408.7 11.4 %copy.267 = f32[2,1024,8,64]{3,2,1,0:T(8,128)} copy(f32[2,1024,8,64]{3,1,2,0:T(8,128)} %bitcast.220) | data formatting | bytes 8388608 | tf_op jit(solution)/shard_map/transpose | solution.py:176
  420.1 7.8 %dot_general.136 = f32[32,64,512]{2,1,0:T(8,128)} reshape(f32[2,1024,8,64]{3,2,1,0:T(8,128)} %copy.267) | data formatting | bytes 8388608 | tf_op jit(solution)/shard_map/rp,qp->rq/dot_general | solution.py:178
  427.9 9.6 %select_select_fusion = f32[32,64,512]{2,1,0:T(8,128)S(1)} fusion(f32[32,64,512]{2,1,0:T(8,128)} %gather_fusion.2, f32[32,64,512]{2,1,0:T(8,128)} %dot_general.136, pred[32]{0:T(512)(128)(4,1)S(1)} %copy-done.11, pred[32]{0:T(512)(128)(4,1)S(1)} %broadcast_compare_fusion.1, f32[512,512]{1,0:T(8,128)S(1)} %copy-done.2), kind=kOutput, calls=%fused_computation.25 | convolution fusion | flops 6444548096 | bytes 13631552 | tf_op jit(solution)/shard_map/rp,qp->rq/dot_general | solution.py:178
  439.8 16.7 %collective-permute-start.1 = (f32[128,512]{1,0:T(8,128)S(1)}, f32[128,512]{1,0:T(8,128)S(1)}, u32[]{:S(2)}, u32[]{:S(2)}) collective-permute-start(f32[128,512]{1,0:T(8,128)S(1)} %constant_dynamic-slice_fusion.1), channel_id=1, source_target_pairs={{0,0},{1,16},{2,32},{3,48},{4,64},{5,80},{6,96},{7,112},{8,8},{9,2... | collective-permute-start | bytes 786440 | tf_op jit(solution)/shard_map/ppermute | solution.py:199
  461.3 37.1 %all-gather.9.cloned.1.call-done = f32[1024,512]{1,0:T(8,128)} async-done(((f32[128,512]{1,0:T(8,128)}), f32[1024,512]{1,0:T(8,128)}) %all-gather.9.cloned.1.call-update) | async-done | bytes 2097168 | tf_op jit(solution)/shard_map/all_gather | solution.py:200
  498.4 18.8 %subtract_select_fusion = f32[2048,1024]{1,0:T(8,128)} fusion(f32[2048,1024]{1,0:T(8,128)} %bitcast_add_fusion, pred[1024]{0:T(1024)(128)(4,1)S(1)} %fusion.46, pred[2048]{0:T(1024)(128)(4,1)S(1)} %fusion.40, f32[2048,512]{1,0:T(8,128)} %bitcast.217, f32[1024,512]{1,0:T(8,128)} %all-gather.9.cloned.1.call-done), kind=kOutput, calls=%fused_computation.22 | convolution fusion | flops 12891193344 | bytes 23071744 | tf_op jit(solution)/shard_map/rp,cp->rc/dot_general | solution.py:201
  (245 shorter events, 170.5 us)
Async XLA Ops:
  19.5 7.7 %copy-start.15 = (s32[2,128]{1,0:T(2,128)S(1)}, s32[2,128]{1,0:T(2,128)}, u32[]{:S(2)}) copy-start(s32[2,128]{1,0:T(2,128)} %param.36) | copy-start | bytes 3076
  21.2 10.2 %copy-start.5 = (s32[2,128]{1,0:T(2,128)S(1)}, s32[2,128]{1,0:T(2,128)}, u32[]{:S(2)}) copy-start(s32[2,128]{1,0:T(2,128)} %param.35) | copy-start | bytes 3076
  21.2 32.1 %all-to-all-start = ((f32[8,128,512]{2,1,0:T(8,128)}), f32[8,128,512]{2,1,0:T(8,128)S(1)}, u32[]{:S(2)}, u32[]{:S(2)}) async-start(f32[8,128,512]{2,1,0:T(8,128)} %bitcast.227), calls=%async_computation | async-start | bytes 4194304 | tf_op jit(solution)/shard_map/all_to_all | solution.py:112
  53.4 34.9 %copy-start.1 = (f32[8,128,512]{2,1,0:T(8,128)}, f32[8,128,512]{2,1,0:T(8,128)S(1)}, u32[]{:S(2)}) copy-start(f32[8,128,512]{2,1,0:T(8,128)S(1)} %all-to-all-done) | copy-start | bytes 6291460
  53.4 31.6 %all-to-all-start.2 = ((f32[8,128,512]{2,1,0:T(8,128)}), f32[8,128,512]{2,1,0:T(8,128)}, u32[]{:S(2)}, u32[]{:S(2)}) async-start(f32[8,128,512]{2,1,0:T(8,128)} %bitcast.226), calls=%async_computation.2 | async-start | bytes 4194304 | tf_op jit(solution)/shard_map/all_to_all | solution.py:112
  58.6 4.7 copy-start.12
  60.2 3.1 copy-start.6
  64.9 36.9 %slice-start = ((f32[2048,1024]{1,0:T(8,128)}), f32[2048,64]{1,0:T(8,128)S(1)}, s32[]{:S(2)}) async-start(f32[2048,1024]{1,0:T(8,128)} %param.33), calls=%async_computation.8 | async-start | bytes 2097152 | tf_op jit(solution)/shard_map/slice | solution.py:159
  90.8 14.5 %all-to-all-start.4 = ((f32[16,4,512]{2,1,0:T(4,128)}), f32[16,4,512]{2,1,0:T(4,128)S(1)}, u32[]{:S(2)}, u32[]{:S(2)}) async-start(f32[16,4,512]{2,1,0:T(4,128)} %reshape.486), calls=%async_computation.4 | async-start | bytes 262144 | tf_op jit(solution)/shard_map/all_to_all | solution.py:131
  98.6 56.5 %all-gather.5.cloned.1.call-start = ((), (), s32[]{:S(2)}) async-start(), calls=%async_computation.5 | async-start | bytes 1179648 | tf_op jit(solution)/shard_map/all_gather | solution.py:134
  132.3 4.4 copy-start.10
  142.1 114.8 %all-to-all-start.3 = ((f32[16,64,1024]{2,1,0:T(8,128)}), f32[16,64,1024]{2,1,0:T(8,128)}, u32[]{:S(2)}, u32[]{:S(2)}) async-start(f32[16,64,1024]{2,1,0:T(8,128)} %select_multiply_fusion.1), calls=%async_computation.3 | async-start | bytes 8388608 | tf_op jit(solution)/shard_map/all_to_all | solution.py:143
  146.9 2.8 copy-start.9
  256.9 52.4 %all-to-all-start.1 = ((f32[16,64,1024]{2,1,0:T(8,128)}), f32[16,64,1024]{2,1,0:T(8,128)}, u32[]{:S(2)}, u32[]{:S(2)}) async-start(f32[16,64,1024]{2,1,0:T(8,128)} %select_multiply_fusion.2), calls=%async_computation.1 | async-start | bytes 8388608 | tf_op jit(solution)/shard_map/all_to_all | solution.py:143
  263.6 138.2 %all-gather.7.cloned.1.call-start = ((), (), s32[]{:S(2)}) async-start(), calls=%async_computation.6 | async-start | bytes 4456448 | tf_op jit(solution)/shard_map/all_gather | solution.py:173
  266.0 5.5 %copy-start.14 = (pred[32]{0:T(512)(128)(4,1)S(1)}, pred[32]{0:T(512)(128)(4,1)}, u32[]{:S(2)}) copy-start(pred[32]{0:T(512)(128)(4,1)} %get-tuple-element.50) | copy-start | bytes 100
  270.8 40.9 %copy-start.13 = (pred[32]{0:T(512)(128)(4,1)S(1)}, pred[32]{0:T(512)(128)(4,1)}, u32[]{:S(2)}) copy-start(pred[32]{0:T(512)(128)(4,1)} %get-tuple-element.20) | copy-start | bytes 100
  272.6 41.9 %copy-start.3 = (f32[2048,64]{0,1:T(8,128)S(1)}, f32[2048,64]{0,1:T(8,128)}, u32[]{:S(2)}) copy-start(f32[2048,64]{0,1:T(8,128)} %copy.275) | copy-start | bytes 1572868
  311.7 14.8 %copy-start.7 = (s32[2,16]{1,0:T(2,128)S(1)}, s32[2,16]{1,0:T(2,128)}, u32[]{:S(2)}) copy-start(s32[2,16]{1,0:T(2,128)} %copy-done.6) | copy-start | bytes 388
  315.6 9.7 %collective-permute-start = (f32[2048,64]{0,1:T(8,128)S(1)}, f32[2048,64]{0,1:T(8,128)S(1)}, u32[]{:S(2)}, u32[]{:S(2)}) collective-permute-start(f32[2048,64]{0,1:T(8,128)S(1)} %add_add_fusion), channel_id=1, source_target_pairs={{0,8},{1,9},{2,10},{3,11},{4,12},{5,13},{6,14},{7,15},{16,24},{17,... | collective-permute-start | bytes 1572872 | tf_op jit(solution)/shard_map/ppermute | solution.py:166
  326.3 172.1 %all-gather.9.cloned.1.call-start = ((), (), s32[]{:S(2)}) async-start(), calls=%async_computation.7 | async-start | bytes 2359296 | tf_op jit(solution)/shard_map/all_gather | solution.py:200
  420.1 7.8 %copy-start.2 = (f32[512,512]{1,0:T(8,128)S(1)}, f32[512,512]{1,0:T(8,128)}, u32[]{:S(2)}) copy-start(f32[512,512]{1,0:T(8,128)} %fusion.7) | copy-start | bytes 3145732
  420.1 7.8 %copy-start.11 = (pred[32]{0:T(512)(128)(4,1)S(1)}, pred[32]{0:T(512)(128)(4,1)}, u32[]{:S(2)}) copy-start(pred[32]{0:T(512)(128)(4,1)} %get-tuple-element.78) | copy-start | bytes 100
  439.8 20.8 %collective-permute-start.1 = (f32[128,512]{1,0:T(8,128)S(1)}, f32[128,512]{1,0:T(8,128)S(1)}, u32[]{:S(2)}, u32[]{:S(2)}) collective-permute-start(f32[128,512]{1,0:T(8,128)S(1)} %constant_dynamic-slice_fusion.1), channel_id=1, source_target_pairs={{0,0},{1,16},{2,32},{3,48},{4,64},{5,80},{6,96},{7,112},{8,8},{9,2... | collective-permute-start | bytes 786440 | tf_op jit(solution)/shard_map/ppermute | solution.py:199
  (3 other events, 3.3 us)
Sparse Core Ops, SparseCore 0:
  124.3 27.0 all-gather.4
  326.5 70.0 all-gather.6
  461.4 36.9 all-gather.8

commit v9 on v8

--- a/solution.py
+++ b/solution.py
@@ -130,23 +130,18 @@
     share = partial.reshape(col_count, BLK // col_count, PANEL)
     share = lax.all_to_all(share, "col", split_axis=0, concat_axis=0, tiled=True)
     share = jnp.sum(share, axis=0)
-    corner_row = lax.all_gather(share, "col", axis=0, tiled=True)
-    corner = lax.all_gather(corner_row, "row", axis=0, tiled=True)
-
-    arrived = []
+    corner = lax.all_gather(share, ("row", "col"), axis=0, tiled=True)
+
+    onward = []
     for k in range(2):
         flipped = section_one[k].T.reshape(child_colblk, BLK, row_slots * BLK)
-        onward = take_slabs(flipped, src_col[k]) * has_col[k][:, None, None]
-        onward = onward.reshape(col_slots * BLK, row_slots * BLK)
-        if k == 0:
-            lower_factor, inverse = factor_and_invert(corner)
-        section_two = lax.all_to_all(onward, "col", split_axis=0, concat_axis=0, tiled=True)
-        if k == 1:
-            section_two, lower_factor, inverse = lax.optimization_barrier(
-                (section_two, lower_factor, inverse)
-            )
-        arrived.append(section_two.reshape(col_slots, BLK, row_slots * BLK))
-    arrived = jnp.stack(arrived)
+        sent = take_slabs(flipped, src_col[k]) * has_col[k][:, None, None]
+        onward.append(sent.reshape(col_slots * BLK, row_slots * BLK))
+    onward = jnp.stack(onward)
+    lower_factor, inverse = factor_and_invert(corner)
+    section_two = lax.all_to_all(onward, "col", split_axis=1, concat_axis=1, tiled=True)
+    section_two, lower_factor, inverse = lax.optimization_barrier((section_two, lower_factor, inverse))
+    arrived = section_two.reshape(2, col_slots, BLK, row_slots * BLK)
 
     by_col = jax.vmap(take_slabs)(arrived, col_source) * col_weight[:, :, None, None]
     by_col = by_col.reshape(2, local_cols, row_slots * BLK)

time: 531 us -> 588 us (1.11)
  waiting for transfers between devices: 116 us -> 199 us
  local copies, waits for them, and re-layouts: 115 us -> 139 us
  starting transfers between devices: 50.8 us -> 32.5 us
  blocking collectives: 18.2 us -> 0 us
  other arithmetic: 165 us -> 150 us
    all_gather x1, waiting for transfers between devices: 0.01 us -> 83.8 us  [on_device(): corner = lax.all_gather(share, ('row', 'col'), axis=0, tiled=True)]
    all_to_all x2 -> x1, waiting for transfers between devices: 34.3 us -> 0.01 us  [on_device(): lax.all_to_all(onward, 'col', split_axis=1, concat_axis=1, tiled=True)]
    all_gather x1 -> x0, blocking collectives: 18.2 us -> none  [on_device(): corner_row = lax.all_gather(share, 'col', axis=0, tiled=True)]
    all_gather x1, waiting for transfers between devices: 0.01 us -> 17.8 us  [on_device(): gathered = lax.all_gather(part, 'col', axis=0, tiled=False)]
    ppermute x1, starting transfers between devices: 16.7 us -> 3.7 us  [on_device(): piece = lax.ppermute(piece, ('row', 'col'), pairs)]
    another operation x0 -> x1, local copies, waits for them, and re-layouts: none -> 12.9 us  [on_device(): onward = jnp.stack(onward)]
    all_gather x1, waiting for transfers between devices: 37.1 us -> 47.9 us  [on_device(): across = lax.all_gather(piece, 'row', axis=0, tiled=True)]
    mul x2, other arithmetic: 10.6 us -> 3.6 us  [on_device(): sent = take_slabs(flipped, src_col[k]) * has_col[k][:, None, None]]
  transfers between devices with their start and end apart: 10 -> 9, of which waited for: 7 -> 8; matrix products, arithmetic and copies ran while one was open for 45% -> 39% of each run, Pallas kernels for 0% -> 0%
where the time goes in v9:
time: 588 us; the launch traced here: 579 us
  waiting for transfers between devices  199 us (34%)
  other arithmetic  150 us (26%)
  local copies, waits for them, and re-layouts  139 us (24%)
  matrix products  38.6 us (7%)
  starting transfers between devices  32.5 us (6%)
  between operations  20.3 us (3%)
    all_gather x1, waiting for transfers between devices, on_device(): corner = lax.all_gather(share, ('row', 'col'), axis=0, tiled=True)  83.8 us
    another operation x12, other arithmetic, factor_and_invert(): lpp = lax.linalg.cholesky(grid[p][p], symmetrize_input=False)  49.7 us
    all_gather x1, waiting for transfers between devices, on_device(): across = lax.all_gather(piece, 'row', axis=0, tiled=True)  47.9 us
    another operation x8, other arithmetic, factor_and_invert(): dinv = jax.scipy.linalg.solve_triangular(lpp, eye, lower=True)  42.2 us
    gather x10, local copies, waits for them, and re-layouts, take_slabs(): return jnp.take(source, indices, axis=0)  34.8 us
    all_to_all x2, waiting for transfers between devices, on_device(): lax.all_to_all(outgoing, 'row', split_axis=0, concat_axis=0, tiled=True)  33.2 us
    dot_general x1, matrix products, on_device(): update = jnp.einsum('rp,cp->rc', panel_factor, across, precision=exact_mode)  18.8 us
    all_gather x1, waiting for transfers between devices, on_device(): gathered = lax.all_gather(part, 'col', axis=0, tiled=False)  17.8 us
  transfers between devices with their start and end apart: 9, of which 8 were waited for; matrix products, arithmetic and copies ran while one was open for 39% of the time, Pallas kernels for 0%

profile of v9, /device:TPU:1, one launch (start us, length us, event | category | flops | bytes accessed | tf_op | source)
XLA Modules:
  0.0 579.3 jit_solution(14418973840646010250)
XLA Ops:
  36.9 16.5 %all-to-all-done = f32[8,128,512]{2,1,0:T(8,128)S(1)} async-done(((f32[8,128,512]{2,1,0:T(8,128)}), f32[8,128,512]{2,1,0:T(8,128)S(1)}, u32[]{:S(2)}, u32[]{:S(2)}) %all-to-all-start) | async-done | bytes 2097184 | tf_op jit(solution)/shard_map/all_to_all | solution.py:112
  68.2 16.7 %all-to-all-done.1 = f32[8,128,512]{2,1,0:T(8,128)} async-done(((f32[8,128,512]{2,1,0:T(8,128)}), f32[8,128,512]{2,1,0:T(8,128)}, u32[]{:S(2)}, u32[]{:S(2)}) %all-to-all-start.1) | async-done | bytes 2097184 | tf_op jit(solution)/shard_map/all_to_all | solution.py:112
  90.8 7.8 %all-to-all-start.3 = ((f32[16,4,512]{2,1,0:T(4,128)}), f32[16,4,512]{2,1,0:T(4,128)S(1)}, u32[]{:S(2)}, u32[]{:S(2)}) async-start(f32[16,4,512]{2,1,0:T(4,128)} %reshape.479), calls=%async_computation.3 | async-start | bytes 262144 | tf_op jit(solution)/shard_map/all_to_all | solution.py:131
  126.5 12.9 %copy.242 = f32[2,1024,1024]{2,0,1:T(2,128)} copy(f32[2,1024,1024]{2,1,0:T(8,128)S(1)} %pad_maximum_fusion) | data formatting | bytes 16777216 | tf_op jit(solution)/shard_map/stack | solution.py:140
  146.0 83.8 %all-gather.9.cloned.1.call-done = f32[128,4,512]{2,1,0:T(4,128)} async-done(((f32[1,4,512]{2,1,0:T(4,128)}), f32[128,4,512]{2,1,0:T(4,128)}) %all-gather.9.cloned.1.call-update) | async-done | bytes 1048592 | tf_op jit(solution)/shard_map/all_gather | solution.py:133
  231.9 11.7 %custom-call.16 = f32[128,128]{1,0:T(8,128)S(1)} custom-call(f32[128,128]{1,0:T(8,128)S(1)} %slice.202), custom_call_target="Cholesky" | custom-call | tf_op jit(solution)/shard_map/cholesky/custom-call.1 | solution.py:26
  245.0 9.8 %custom-call.17 = f32[1,128,128]{1,2,0:T(8,128)S(1)} custom-call(f32[1,128,128]{2,1,0:T(8,128)S(1)} %get-tuple-element.30), custom_call_target="InvertDiagBlocksLowerTriangular" | custom-call | tf_op jit(solution)/shard_map/jit(_solve_triangular)/triangular_solve | solution.py:27
  256.6 11.7 %custom-call.18 = f32[128,128]{1,0:T(8,128)S(1)} custom-call(f32[128,128]{1,0:T(8,128)S(1)} %convolution_subtract_fusion.9), custom_call_target="Cholesky" | custom-call | tf_op jit(solution)/shard_map/cholesky/custom-call.1 | solution.py:26
  269.6 10.2 %custom-call.19 = f32[1,128,128]{1,2,0:T(8,128)S(1)} custom-call(f32[1,128,128]{2,1,0:T(8,128)S(1)} %get-tuple-element.28), custom_call_target="InvertDiagBlocksLowerTriangular" | custom-call | tf_op jit(solution)/shard_map/jit(_solve_triangular)/triangular_solve | solution.py:27
  281.2 11.7 %custom-call.20 = f32[128,128]{1,0:T(8,128)S(1)} custom-call(f32[128,128]{1,0:T(8,128)S(1)} %convolution_subtract_fusion.6), custom_call_target="Cholesky" | custom-call | tf_op jit(solution)/shard_map/cholesky/custom-call.1 | solution.py:26
  294.2 9.8 %custom-call.21 = f32[1,128,128]{1,2,0:T(8,128)S(1)} custom-call(f32[1,128,128]{2,1,0:T(8,128)S(1)} %get-tuple-element.26), custom_call_target="InvertDiagBlocksLowerTriangular" | custom-call | tf_op jit(solution)/shard_map/jit(_solve_triangular)/triangular_solve | solution.py:27
  307.4 11.9 %custom-call.22 = f32[128,128]{1,0:T(8,128)S(1)} custom-call(f32[128,128]{1,0:T(8,128)S(1)} %convolution_subtract_fusion), custom_call_target="Cholesky" | custom-call | tf_op jit(solution)/shard_map/cholesky/custom-call.1 | solution.py:26
  320.6 9.8 %custom-call.23 = f32[1,128,128]{1,2,0:T(8,128)S(1)} custom-call(f32[1,128,128]{2,1,0:T(8,128)S(1)} %get-tuple-element.24), custom_call_target="InvertDiagBlocksLowerTriangular" | custom-call | tf_op jit(solution)/shard_map/jit(_solve_triangular)/triangular_solve | solution.py:27
  362.2 10.9 %collective-permute-done = f32[2048,64]{0,1:T(8,128)S(1)} collective-permute-done((f32[2048,64]{0,1:T(8,128)S(1)}, f32[2048,64]{0,1:T(8,128)S(1)}, u32[]{:S(2)}, u32[]{:S(2)}) %collective-permute-start) | collective-permute-done | bytes 524320 | tf_op jit(solution)/shard_map/ppermute | solution.py:161
  374.8 7.7 %gather_fusion.3 = f32[32,64,1024]{2,1,0:T(8,128)} fusion(f32[2,16,64,1024]{3,2,1,0:T(8,128)} %bitcast.215, s32[32]{0:T(128)S(1)} %reshape.594), kind=kCustom, calls=%fused_computation.13 | custom fusion | bytes 16777472 | tf_op jit(solution)/shard_map/vmap(jit(_take))/gather | solution.py:15
  388.5 8.7 %copy.276 = f32[2,1024,1024]{2,1,0:T(8,128)} copy(f32[2,1024,1024]{1,2,0:T(8,128)} %fusion.1) | data formatting | bytes 16777216 | tf_op jit(solution)/shard_map/transpose | solution.py:148
  397.2 12.5 %gather_fusion.4 = f32[64,64,1024]{2,1,0:T(8,128)} fusion(f32[2,16,64,1024]{3,2,1,0:T(8,128)} %bitcast.216, s32[64]{0:T(128)S(1)} %reshape.600), kind=kCustom, calls=%fused_computation.14 | custom fusion | bytes 33554944 | tf_op jit(solution)/shard_map/vmap(jit(_take))/gather | solution.py:15
  426.7 13.7 %bitcast_add_fusion = f32[2048,1024]{1,0:T(8,128)} fusion(f32[1,32,64,1024]{3,2,1,0:T(8,128)} %get-tuple-element.45, f32[2048,1024]{1,0:T(8,128)} %param.33, f32[1,32,64,1024]{3,2,1,0:T(8,128)} %get-tuple-element.44), kind=kLoop, calls=%fused_computation.17 | loop fusion | flops 4194304 | bytes 33554432 | tf_op jit(solution)/shard_map/add | solution.py:151
  440.4 17.8 %all-gather.5.cloned.1.call-done = f32[16,512,128]{2,1,0:T(8,128)} async-done(((f32[1,512,128]{2,1,0:T(8,128)}), f32[16,512,128]{2,1,0:T(8,128)}) %all-gather.5.cloned.1.call-update) | async-done | bytes 4194320 | tf_op jit(solution)/shard_map/all_gather | solution.py:168
  465.1 11.4 %copy.277 = f32[2,1024,8,64]{3,2,1,0:T(8,128)} copy(f32[2,1024,8,64]{3,1,2,0:T(8,128)} %bitcast.222) | data formatting | bytes 8388608 | tf_op jit(solution)/shard_map/transpose | solution.py:171
  476.5 7.8 %dot_general.136 = f32[32,64,512]{2,1,0:T(8,128)} reshape(f32[2,1024,8,64]{3,2,1,0:T(8,128)} %copy.277) | data formatting | bytes 8388608 | tf_op jit(solution)/shard_map/rp,qp->rq/dot_general | solution.py:173
  484.3 9.6 %select_select_fusion = f32[32,64,512]{2,1,0:T(8,128)S(1)} fusion(f32[32,64,512]{2,1,0:T(8,128)} %gather_fusion.2, f32[32,64,512]{2,1,0:T(8,128)} %dot_general.136, pred[32]{0:T(512)(128)(4,1)S(1)} %copy-done.13, pred[32]{0:T(512)(128)(4,1)S(1)} %broadcast_compare_fusion.1, f32[512,512]{1,0:T(8,128)S(1)} %copy-done.4), kind=kOutput, calls=%fused_computation.25 | convolution fusion | flops 6444548096 | bytes 13631552 | tf_op jit(solution)/shard_map/rp,qp->rq/dot_general | solution.py:173
  505.7 47.9 %all-gather.7.cloned.1.call-done = f32[1024,512]{1,0:T(8,128)} async-done(((f32[128,512]{1,0:T(8,128)}), f32[1024,512]{1,0:T(8,128)}) %all-gather.7.cloned.1.call-update) | async-done | bytes 2097168 | tf_op jit(solution)/shard_map/all_gather | solution.py:195
  553.5 18.8 %subtract_select_fusion = f32[2048,1024]{1,0:T(8,128)} fusion(f32[2048,1024]{1,0:T(8,128)} %bitcast_add_fusion, pred[1024]{0:T(1024)(128)(4,1)S(1)} %fusion.46, pred[2048]{0:T(1024)(128)(4,1)S(1)} %fusion.40, f32[2048,512]{1,0:T(8,128)} %bitcast.219, f32[1024,512]{1,0:T(8,128)} %all-gather.7.cloned.1.call-done), kind=kOutput, calls=%fused_computation.22 | convolution fusion | flops 12891193344 | bytes 23071744 | tf_op jit(solution)/shard_map/rp,cp->rc/dot_general | solution.py:196
  (249 shorter events, 168.0 us)
Async XLA Ops:
  19.5 7.7 %copy-start.17 = (s32[2,128]{1,0:T(2,128)S(1)}, s32[2,128]{1,0:T(2,128)}, u32[]{:S(2)}) copy-start(s32[2,128]{1,0:T(2,128)} %param.36) | copy-start | bytes 3076
  21.2 10.8 %copy-start.7 = (s32[2,128]{1,0:T(2,128)S(1)}, s32[2,128]{1,0:T(2,128)}, u32[]{:S(2)}) copy-start(s32[2,128]{1,0:T(2,128)} %param.35) | copy-start | bytes 3076
  21.2 32.1 %all-to-all-start = ((f32[8,128,512]{2,1,0:T(8,128)}), f32[8,128,512]{2,1,0:T(8,128)S(1)}, u32[]{:S(2)}, u32[]{:S(2)}) async-start(f32[8,128,512]{2,1,0:T(8,128)} %bitcast.231), calls=%async_computation | async-start | bytes 4194304 | tf_op jit(solution)/shard_map/all_to_all | solution.py:112
  53.4 34.9 %copy-start.3 = (f32[8,128,512]{2,1,0:T(8,128)}, f32[8,128,512]{2,1,0:T(8,128)S(1)}, u32[]{:S(2)}) copy-start(f32[8,128,512]{2,1,0:T(8,128)S(1)} %all-to-all-done) | copy-start | bytes 6291460
  53.4 31.6 %all-to-all-start.1 = ((f32[8,128,512]{2,1,0:T(8,128)}), f32[8,128,512]{2,1,0:T(8,128)}, u32[]{:S(2)}, u32[]{:S(2)}) async-start(f32[8,128,512]{2,1,0:T(8,128)} %bitcast.230), calls=%async_computation.1 | async-start | bytes 4194304 | tf_op jit(solution)/shard_map/all_to_all | solution.py:112
  58.6 4.8 copy-start.14
  60.2 3.3 copy-start.8
  64.9 36.8 %slice-start = ((f32[2048,1024]{1,0:T(8,128)}), f32[2048,64]{1,0:T(8,128)S(1)}, s32[]{:S(2)}) async-start(f32[2048,1024]{1,0:T(8,128)} %param.33), calls=%async_computation.7 | async-start | bytes 2097152 | tf_op jit(solution)/shard_map/slice | solution.py:154
  90.8 14.5 %all-to-all-start.3 = ((f32[16,4,512]{2,1,0:T(4,128)}), f32[16,4,512]{2,1,0:T(4,128)S(1)}, u32[]{:S(2)}, u32[]{:S(2)}) async-start(f32[16,4,512]{2,1,0:T(4,128)} %reshape.479), calls=%async_computation.3 | async-start | bytes 262144 | tf_op jit(solution)/shard_map/all_to_all | solution.py:131
  98.6 131.2 %all-gather.9.cloned.1.call-start = ((), (), s32[]{:S(2)}) async-start(), calls=%async_computation.6 | async-start | bytes 1056768 | tf_op jit(solution)/shard_map/all_gather | solution.py:133
  120.8 3.5 copy-start.2
  120.8 3.5 copy-start.11
  139.4 197.2 %all-to-all-start.2 = ((f32[2,1024,1024]{2,0,1:T(2,128)}), f32[2,1024,1024]{2,0,1:T(2,128)}, u32[]{:S(2)}, u32[]{:S(2)}) async-start(f32[2,1024,1024]{2,0,1:T(2,128)} %copy.242), calls=%async_computation.2 | async-start | bytes 16777216 | tf_op jit(solution)/shard_map/all_to_all | solution.py:142
  145.7 312.4 %all-gather.5.cloned.1.call-start = ((), (), s32[]{:S(2)}) async-start(), calls=%async_computation.4 | async-start | bytes 4456448 | tf_op jit(solution)/shard_map/all_gather | solution.py:168
  342.7 4.7 copy-start
  342.7 6.1 %copy-start.16 = (pred[32]{0:T(512)(128)(4,1)S(1)}, pred[32]{0:T(512)(128)(4,1)}, u32[]{:S(2)}) copy-start(pred[32]{0:T(512)(128)(4,1)} %get-tuple-element.52) | copy-start | bytes 100
  348.2 6.8 %copy-start.15 = (pred[32]{0:T(512)(128)(4,1)S(1)}, pred[32]{0:T(512)(128)(4,1)}, u32[]{:S(2)}) copy-start(pred[32]{0:T(512)(128)(4,1)} %get-tuple-element.20) | copy-start | bytes 100
  350.0 7.7 %copy-start.5 = (f32[2048,64]{0,1:T(8,128)S(1)}, f32[2048,64]{0,1:T(8,128)}, u32[]{:S(2)}) copy-start(f32[2048,64]{0,1:T(8,128)} %copy.284) | copy-start | bytes 1572868
  355.0 19.5 %copy-start.9 = (s32[2,16]{1,0:T(2,128)S(1)}, s32[2,16]{1,0:T(2,128)}, u32[]{:S(2)}) copy-start(s32[2,16]{1,0:T(2,128)} %copy-done.8) | copy-start | bytes 388
  358.8 14.3 %collective-permute-start = (f32[2048,64]{0,1:T(8,128)S(1)}, f32[2048,64]{0,1:T(8,128)S(1)}, u32[]{:S(2)}, u32[]{:S(2)}) collective-permute-start(f32[2048,64]{0,1:T(8,128)S(1)} %add_add_fusion), channel_id=1, source_target_pairs={{0,8},{1,9},{2,10},{3,11},{4,12},{5,13},{6,14},{7,15},{16,24},{17,... | collective-permute-start | bytes 1572872 | tf_op jit(solution)/shard_map/ppermute | solution.py:161
  374.2 179.4 %all-gather.7.cloned.1.call-start = ((), (), s32[]{:S(2)}) async-start(), calls=%async_computation.5 | async-start | bytes 2359296 | tf_op jit(solution)/shard_map/all_gather | solution.py:195
  476.5 7.8 %copy-start.4 = (f32[512,512]{1,0:T(8,128)S(1)}, f32[512,512]{1,0:T(8,128)}, u32[]{:S(2)}) copy-start(f32[512,512]{1,0:T(8,128)} %fusion.7) | copy-start | bytes 3145732
  476.5 7.8 %copy-start.13 = (pred[32]{0:T(512)(128)(4,1)S(1)}, pred[32]{0:T(512)(128)(4,1)}, u32[]{:S(2)}) copy-start(pred[32]{0:T(512)(128)(4,1)} %get-tuple-element.80) | copy-start | bytes 100
  496.2 8.7 %collective-permute-start.1 = (f32[128,512]{1,0:T(8,128)S(1)}, f32[128,512]{1,0:T(8,128)S(1)}, u32[]{:S(2)}, u32[]{:S(2)}) collective-permute-start(f32[128,512]{1,0:T(8,128)S(1)} %constant_dynamic-slice_fusion.1), channel_id=1, source_target_pairs={{0,0},{1,16},{2,32},{3,48},{4,64},{5,80},{6,96},{7,112},{8,8},{9,2... | collective-permute-start | bytes 786440 | tf_op jit(solution)/shard_map/ppermute | solution.py:194
  (4 other events, 6.1 us)
Sparse Core Ops, SparseCore 0:
  106.0 123.6 all-gather.8
  374.3 83.7 all-gather.4
  505.8 47.7 all-gather.6

commit v10 on v9

--- a/solution.py
+++ b/solution.py
@@ -130,7 +130,8 @@
     share = partial.reshape(col_count, BLK // col_count, PANEL)
     share = lax.all_to_all(share, "col", split_axis=0, concat_axis=0, tiled=True)
     share = jnp.sum(share, axis=0)
-    corner = lax.all_gather(share, ("row", "col"), axis=0, tiled=True)
+    corner_row = lax.all_gather(share, "col", axis=0, tiled=True)
+    corner = lax.all_gather(corner_row, "row", axis=0, tiled=True)
 
     onward = []
     for k in range(2):

time: 588 us -> 496 us (0.84)
  waiting for transfers between devices: 199 us -> 79.8 us
  blocking collectives: 0 us -> 18 us
  starting transfers between devices: 32.5 us -> 40.2 us
    all_gather x1, waiting for transfers between devices: 83.8 us -> 0.02 us  [on_device(): corner = lax.all_gather(corner_row, 'row', axis=0, tiled=True)]
    all_gather x0 -> x1, blocking collectives: none -> 18 us  [on_device(): corner_row = lax.all_gather(share, 'col', axis=0, tiled=True)]
    all_gather x1, waiting for transfers between devices: 17.8 us -> 0.01 us  [on_device(): gathered = lax.all_gather(part, 'col', axis=0, tiled=False)]
    all_gather x1, waiting for transfers between devices: 47.9 us -> 36.4 us  [on_device(): across = lax.all_gather(piece, 'row', axis=0, tiled=True)]
    ppermute x1, starting transfers between devices: 3.7 us -> 11.3 us  [on_device(): piece = lax.ppermute(piece, ('row', 'col'), pairs)]
  transfers between devices with their start and end apart: 9 -> 9, of which waited for: 8 -> 6; matrix products, arithmetic and copies ran while one was open for 39% -> 47% of each run, Pallas kernels for 0% -> 0%
where the time goes in v10:
time: 496 us; the launch traced here: 486 us
  other arithmetic  150 us (30%)
  local copies, waits for them, and re-layouts  140 us (28%)
  waiting for transfers between devices  79.8 us (16%)
  starting transfers between devices  40.2 us (8%)
  matrix products  38.6 us (8%)
  between operations  20.2 us (4%)
  blocking collectives  18 us (4%)
    another operation x12, other arithmetic, factor_and_invert(): lpp = lax.linalg.cholesky(grid[p][p], symmetrize_input=False)  49.7 us
    another operation x8, other arithmetic, factor_and_invert(): dinv = jax.scipy.linalg.solve_triangular(lpp, eye, lower=True)  42.2 us
    all_gather x1, waiting for transfers between devices, on_device(): across = lax.all_gather(piece, 'row', axis=0, tiled=True)  36.4 us
    gather x10, local copies, waits for them, and re-layouts, take_slabs(): return jnp.take(source, indices, axis=0)  35.4 us
    all_to_all x2, waiting for transfers between devices, on_device(): lax.all_to_all(outgoing, 'row', split_axis=0, concat_axis=0, tiled=True)  32.5 us
    dot_general x1, matrix products, on_device(): update = jnp.einsum('rp,cp->rc', panel_factor, across, precision=exact_mode)  18.8 us
    all_gather x1, blocking collectives, on_device(): corner_row = lax.all_gather(share, 'col', axis=0, tiled=True)  18 us
    add x1, other arithmetic, on_device(): extended = front_matrix + placed[0] + placed[1]  13.7 us
  transfers between devices with their start and end apart: 9, of which 6 were waited for; matrix products, arithmetic and copies ran while one was open for 47% of the time, Pallas kernels for 0%

profile of v10, /device:TPU:1, one launch (start us, length us, event | category | flops | bytes accessed | tf_op | source)
XLA Modules:
  0.0 486.4 jit_solution(9524080929649849758)
XLA Ops:
  37.1 16.3 %all-to-all-done = f32[8,128,512]{2,1,0:T(8,128)S(1)} async-done(((f32[8,128,512]{2,1,0:T(8,128)}), f32[8,128,512]{2,1,0:T(8,128)S(1)}, u32[]{:S(2)}, u32[]{:S(2)}) %all-to-all-start) | async-done | bytes 2097184 | tf_op jit(solution)/shard_map/all_to_all | solution.py:112
  68.7 16.3 %all-to-all-done.1 = f32[8,128,512]{2,1,0:T(8,128)} async-done(((f32[8,128,512]{2,1,0:T(8,128)}), f32[8,128,512]{2,1,0:T(8,128)}, u32[]{:S(2)}, u32[]{:S(2)}) %all-to-all-start.1) | async-done | bytes 2097184 | tf_op jit(solution)/shard_map/all_to_all | solution.py:112
  90.8 7.8 %all-to-all-start.3 = ((f32[16,4,512]{2,1,0:T(4,128)}), f32[16,4,512]{2,1,0:T(4,128)S(1)}, u32[]{:S(2)}, u32[]{:S(2)}) async-start(f32[16,4,512]{2,1,0:T(4,128)} %reshape.479), calls=%async_computation.3 | async-start | bytes 262144 | tf_op jit(solution)/shard_map/all_to_all | solution.py:131
  105.3 18.0 %all-gather = f32[16,4,512]{2,1,0:T(4,128)S(1)} all-gather(f32[1,4,512]{2,1,0:T(4,128)S(1)} %bitcast.241), channel_id=1, replica_groups=mesh['row'=8,'col'=16] {'col'}, dimensions={0}, use_global_device_ids=true | all-gather | bytes 139264 | tf_op jit(solution)/shard_map/all_gather | solution.py:133
  143.6 12.9 %copy.244 = f32[2,1024,1024]{2,0,1:T(2,128)} copy(f32[2,1024,1024]{2,1,0:T(8,128)S(1)} %pad_maximum_fusion) | data formatting | bytes 16777216 | tf_op jit(solution)/shard_map/stack | solution.py:141
  164.8 11.7 %custom-call.16 = f32[128,128]{1,0:T(8,128)S(1)} custom-call(f32[128,128]{1,0:T(8,128)S(1)} %slice.202), custom_call_target="Cholesky" | custom-call | tf_op jit(solution)/shard_map/cholesky/custom-call.1 | solution.py:26
  177.8 9.8 %custom-call.17 = f32[1,128,128]{1,2,0:T(8,128)S(1)} custom-call(f32[1,128,128]{2,1,0:T(8,128)S(1)} %get-tuple-element.30), custom_call_target="InvertDiagBlocksLowerTriangular" | custom-call | tf_op jit(solution)/shard_map/jit(_solve_triangular)/triangular_solve | solution.py:27
  189.4 11.7 %custom-call.18 = f32[128,128]{1,0:T(8,128)S(1)} custom-call(f32[128,128]{1,0:T(8,128)S(1)} %convolution_subtract_fusion.9), custom_call_target="Cholesky" | custom-call | tf_op jit(solution)/shard_map/cholesky/custom-call.1 | solution.py:26
  202.4 10.2 %custom-call.19 = f32[1,128,128]{1,2,0:T(8,128)S(1)} custom-call(f32[1,128,128]{2,1,0:T(8,128)S(1)} %get-tuple-element.28), custom_call_target="InvertDiagBlocksLowerTriangular" | custom-call | tf_op jit(solution)/shard_map/jit(_solve_triangular)/triangular_solve | solution.py:27
  214.0 11.7 %custom-call.20 = f32[128,128]{1,0:T(8,128)S(1)} custom-call(f32[128,128]{1,0:T(8,128)S(1)} %convolution_subtract_fusion.6), custom_call_target="Cholesky" | custom-call | tf_op jit(solution)/shard_map/cholesky/custom-call.1 | solution.py:26
  227.0 9.8 %custom-call.21 = f32[1,128,128]{1,2,0:T(8,128)S(1)} custom-call(f32[1,128,128]{2,1,0:T(8,128)S(1)} %get-tuple-element.26), custom_call_target="InvertDiagBlocksLowerTriangular" | custom-call | tf_op jit(solution)/shard_map/jit(_solve_triangular)/triangular_solve | solution.py:27
  240.2 11.9 %custom-call.22 = f32[128,128]{1,0:T(8,128)S(1)} custom-call(f32[128,128]{1,0:T(8,128)S(1)} %convolution_subtract_fusion), custom_call_target="Cholesky" | custom-call | tf_op jit(solution)/shard_map/cholesky/custom-call.1 | solution.py:26
  253.4 9.8 %custom-call.23 = f32[1,128,128]{1,2,0:T(8,128)S(1)} custom-call(f32[1,128,128]{2,1,0:T(8,128)S(1)} %get-tuple-element.24), custom_call_target="InvertDiagBlocksLowerTriangular" | custom-call | tf_op jit(solution)/shard_map/jit(_solve_triangular)/triangular_solve | solution.py:27
  304.3 7.7 %gather_fusion.3 = f32[32,64,1024]{2,1,0:T(8,128)} fusion(f32[2,16,64,1024]{3,2,1,0:T(8,128)} %bitcast.215, s32[32]{0:T(128)S(1)} %reshape.594), kind=kCustom, calls=%fused_computation.13 | custom fusion | bytes 16777472 | tf_op jit(solution)/shard_map/vmap(jit(_take))/gather | solution.py:15
  318.0 8.7 %copy.278 = f32[2,1024,1024]{2,1,0:T(8,128)} copy(f32[2,1024,1024]{1,2,0:T(8,128)} %fusion.1) | data formatting | bytes 16777216 | tf_op jit(solution)/shard_map/transpose | solution.py:149
  326.7 12.6 %gather_fusion.4 = f32[64,64,1024]{2,1,0:T(8,128)} fusion(f32[2,16,64,1024]{3,2,1,0:T(8,128)} %bitcast.216, s32[64]{0:T(128)S(1)} %reshape.600), kind=kCustom, calls=%fused_computation.14 | custom fusion | bytes 33554944 | tf_op jit(solution)/shard_map/vmap(jit(_take))/gather | solution.py:15
  342.1 7.5 %select_multiply_fusion = f32[2,32,64,1024]{3,2,1,0:T(8,128)S(1)} fusion(f32[2,32,64,1024]{3,2,1,0:T(8,128)} %bitcast.217, f32[2,32]{1,0:T(2,128)S(1)} %fusion.33, pred[2,32]{1,0:T(4,128)(4,1)S(1)} %compare_and_fusion.11), kind=kLoop, calls=%fused_computation.15 | loop fusion | flops 8388608 | bytes 33554752 | tf_op jit(solution)/shard_map/mul | solution.py:150
  356.4 13.7 %bitcast_add_fusion = f32[2048,1024]{1,0:T(8,128)} fusion(f32[1,32,64,1024]{3,2,1,0:T(8,128)} %get-tuple-element.45, f32[2048,1024]{1,0:T(8,128)} %param.33, f32[1,32,64,1024]{3,2,1,0:T(8,128)} %get-tuple-element.44), kind=kLoop, calls=%fused_computation.17 | loop fusion | flops 4194304 | bytes 33554432 | tf_op jit(solution)/shard_map/add | solution.py:152
  377.1 11.4 %copy.279 = f32[2,1024,8,64]{3,2,1,0:T(8,128)} copy(f32[2,1024,8,64]{3,1,2,0:T(8,128)} %bitcast.222) | data formatting | bytes 8388608 | tf_op jit(solution)/shard_map/transpose | solution.py:172
  388.5 7.8 %dot_general.136 = f32[32,64,512]{2,1,0:T(8,128)} reshape(f32[2,1024,8,64]{3,2,1,0:T(8,128)} %copy.279) | data formatting | bytes 8388608 | tf_op jit(solution)/shard_map/rp,qp->rq/dot_general | solution.py:174
  396.3 9.6 %select_select_fusion = f32[32,64,512]{2,1,0:T(8,128)S(1)} fusion(f32[32,64,512]{2,1,0:T(8,128)} %gather_fusion.2, f32[32,64,512]{2,1,0:T(8,128)} %dot_general.136, pred[32]{0:T(512)(128)(4,1)S(1)} %copy-done.11, pred[32]{0:T(512)(128)(4,1)S(1)} %broadcast_compare_fusion.1, f32[512,512]{1,0:T(8,128)S(1)} %copy-done.4), kind=kOutput, calls=%fused_computation.25 | convolution fusion | flops 6444548096 | bytes 13631552 | tf_op jit(solution)/shard_map/rp,qp->rq/dot_general | solution.py:174
  408.2 11.3 %collective-permute-start.1 = (f32[128,512]{1,0:T(8,128)S(1)}, f32[128,512]{1,0:T(8,128)S(1)}, u32[]{:S(2)}, u32[]{:S(2)}) collective-permute-start(f32[128,512]{1,0:T(8,128)S(1)} %constant_dynamic-slice_fusion.1), channel_id=1, source_target_pairs={{0,0},{1,16},{2,32},{3,48},{4,64},{5,80},{6,96},{7,112},{8,8},{9,2... | collective-permute-start | bytes 786440 | tf_op jit(solution)/shard_map/ppermute | solution.py:195
  424.3 36.4 %all-gather.9.cloned.1.call-done = f32[1024,512]{1,0:T(8,128)} async-done(((f32[128,512]{1,0:T(8,128)}), f32[1024,512]{1,0:T(8,128)}) %all-gather.9.cloned.1.call-update) | async-done | bytes 2097168 | tf_op jit(solution)/shard_map/all_gather | solution.py:196
  460.7 18.8 %subtract_select_fusion = f32[2048,1024]{1,0:T(8,128)} fusion(f32[2048,1024]{1,0:T(8,128)} %bitcast_add_fusion, pred[1024]{0:T(1024)(128)(4,1)S(1)} %fusion.46, pred[2048]{0:T(1024)(128)(4,1)S(1)} %fusion.40, f32[2048,512]{1,0:T(8,128)} %bitcast.219, f32[1024,512]{1,0:T(8,128)} %all-gather.9.cloned.1.call-done), kind=kOutput, calls=%fused_computation.22 | convolution fusion | flops 12891193344 | bytes 23071744 | tf_op jit(solution)/shard_map/rp,cp->rc/dot_general | solution.py:197
  (244 shorter events, 162.8 us)
Async XLA Ops:
  19.5 7.7 %copy-start.14 = (s32[2,128]{1,0:T(2,128)S(1)}, s32[2,128]{1,0:T(2,128)}, u32[]{:S(2)}) copy-start(s32[2,128]{1,0:T(2,128)} %param.36) | copy-start | bytes 3076
  21.3 10.8 %copy-start.7 = (s32[2,128]{1,0:T(2,128)S(1)}, s32[2,128]{1,0:T(2,128)}, u32[]{:S(2)}) copy-start(s32[2,128]{1,0:T(2,128)} %param.35) | copy-start | bytes 3076
  21.3 32.1 %all-to-all-start = ((f32[8,128,512]{2,1,0:T(8,128)}), f32[8,128,512]{2,1,0:T(8,128)S(1)}, u32[]{:S(2)}, u32[]{:S(2)}) async-start(f32[8,128,512]{2,1,0:T(8,128)} %bitcast.231), calls=%async_computation | async-start | bytes 4194304 | tf_op jit(solution)/shard_map/all_to_all | solution.py:112
  53.4 34.9 %copy-start.3 = (f32[8,128,512]{2,1,0:T(8,128)}, f32[8,128,512]{2,1,0:T(8,128)S(1)}, u32[]{:S(2)}) copy-start(f32[8,128,512]{2,1,0:T(8,128)S(1)} %all-to-all-done) | copy-start | bytes 6291460
  53.4 31.6 %all-to-all-start.1 = ((f32[8,128,512]{2,1,0:T(8,128)}), f32[8,128,512]{2,1,0:T(8,128)}, u32[]{:S(2)}, u32[]{:S(2)}) async-start(f32[8,128,512]{2,1,0:T(8,128)} %bitcast.230), calls=%async_computation.1 | async-start | bytes 4194304 | tf_op jit(solution)/shard_map/all_to_all | solution.py:112
  65.4 36.3 %slice-start = ((f32[2048,1024]{1,0:T(8,128)}), f32[2048,64]{1,0:T(8,128)S(1)}, s32[]{:S(2)}) async-start(f32[2048,1024]{1,0:T(8,128)} %param.33), calls=%async_computation.7 | async-start | bytes 2097152 | tf_op jit(solution)/shard_map/slice | solution.py:155
  90.8 14.5 %all-to-all-start.3 = ((f32[16,4,512]{2,1,0:T(4,128)}), f32[16,4,512]{2,1,0:T(4,128)S(1)}, u32[]{:S(2)}, u32[]{:S(2)}) async-start(f32[16,4,512]{2,1,0:T(4,128)} %reshape.479), calls=%async_computation.3 | async-start | bytes 262144 | tf_op jit(solution)/shard_map/all_to_all | solution.py:131
  98.6 63.1 %all-gather.5.cloned.1.call-start = ((), (), s32[]{:S(2)}) async-start(), calls=%async_computation.4 | async-start | bytes 1179648 | tf_op jit(solution)/shard_map/all_gather | solution.py:134
  134.8 3.1 copy-start.10
  137.9 3.4 copy-start.2
  137.9 3.5 copy-start.9
  156.5 112.9 %all-to-all-start.2 = ((f32[2,1024,1024]{2,0,1:T(2,128)}), f32[2,1024,1024]{2,0,1:T(2,128)}, u32[]{:S(2)}, u32[]{:S(2)}) async-start(f32[2,1024,1024]{2,0,1:T(2,128)} %copy.244), calls=%async_computation.2 | async-start | bytes 16777216 | tf_op jit(solution)/shard_map/all_to_all | solution.py:143
  161.4 208.7 %all-gather.7.cloned.1.call-start = ((), (), s32[]{:S(2)}) async-start(), calls=%async_computation.5 | async-start | bytes 4456448 | tf_op jit(solution)/shard_map/all_gather | solution.py:169
  275.6 4.7 copy-start
  275.6 6.1 %copy-start.13 = (pred[32]{0:T(512)(128)(4,1)S(1)}, pred[32]{0:T(512)(128)(4,1)}, u32[]{:S(2)}) copy-start(pred[32]{0:T(512)(128)(4,1)} %get-tuple-element.52) | copy-start | bytes 100
  281.0 6.9 %copy-start.12 = (pred[32]{0:T(512)(128)(4,1)S(1)}, pred[32]{0:T(512)(128)(4,1)}, u32[]{:S(2)}) copy-start(pred[32]{0:T(512)(128)(4,1)} %get-tuple-element.20) | copy-start | bytes 100
  282.8 7.8 %copy-start.5 = (f32[2048,64]{0,1:T(8,128)S(1)}, f32[2048,64]{0,1:T(8,128)}, u32[]{:S(2)}) copy-start(f32[2048,64]{0,1:T(8,128)} %copy.286) | copy-start | bytes 1572868
  291.7 10.8 %collective-permute-start = (f32[2048,64]{0,1:T(8,128)S(1)}, f32[2048,64]{0,1:T(8,128)S(1)}, u32[]{:S(2)}, u32[]{:S(2)}) collective-permute-start(f32[2048,64]{0,1:T(8,128)S(1)} %add_add_fusion), channel_id=1, source_target_pairs={{0,8},{1,9},{2,10},{3,11},{4,12},{5,13},{6,14},{7,15},{16,24},{17,... | collective-permute-start | bytes 1572872 | tf_op jit(solution)/shard_map/ppermute | solution.py:162
  303.7 157.1 %all-gather.9.cloned.1.call-start = ((), (), s32[]{:S(2)}) async-start(), calls=%async_computation.6 | async-start | bytes 2359296 | tf_op jit(solution)/shard_map/all_gather | solution.py:196
  388.5 7.8 %copy-start.4 = (f32[512,512]{1,0:T(8,128)S(1)}, f32[512,512]{1,0:T(8,128)}, u32[]{:S(2)}) copy-start(f32[512,512]{1,0:T(8,128)} %fusion.7) | copy-start | bytes 3145732
  388.5 7.8 %copy-start.11 = (pred[32]{0:T(512)(128)(4,1)S(1)}, pred[32]{0:T(512)(128)(4,1)}, u32[]{:S(2)}) copy-start(pred[32]{0:T(512)(128)(4,1)} %get-tuple-element.80) | copy-start | bytes 100
  405.9 2.0 copy-start.1
  408.2 15.3 %collective-permute-start.1 = (f32[128,512]{1,0:T(8,128)S(1)}, f32[128,512]{1,0:T(8,128)S(1)}, u32[]{:S(2)}, u32[]{:S(2)}) collective-permute-start(f32[128,512]{1,0:T(8,128)S(1)} %constant_dynamic-slice_fusion.1), channel_id=1, source_target_pairs={{0,0},{1,16},{2,32},{3,48},{4,64},{5,80},{6,96},{7,112},{8,8},{9,2... | collective-permute-start | bytes 786440 | tf_op jit(solution)/shard_map/ppermute | solution.py:195
  423.5 0.7 copy-start.6
  (1 other events, 0.6 us)
Sparse Core Ops, SparseCore 0:
  124.1 27.0 all-gather.4
  303.8 58.9 all-gather.6
  424.4 36.3 all-gather.8

commit v11 on v10

--- a/solution.py
+++ b/solution.py
@@ -159,12 +159,15 @@
         lead = lead + (take_slabs(first_col, row_source[k]) * row_weight[k][:, None, None]).reshape(
             local_rows, BLK
         )
-    lifted = lax.ppermute(
-        lead, "col", [(c, c + panel_width * s) for s in range(1, spread) for c in range(panel_width)]
-    )
-    mine = jnp.where(col_place < panel_width, lead, lifted)
     part_rows = local_rows // spread
-    part = lax.dynamic_slice_in_dim(mine, (col_place // panel_width) * part_rows, part_rows, axis=0)
+    part = lead[:part_rows]
+    for h in range(1, spread):
+        moved = lax.ppermute(
+            lead[h * part_rows : (h + 1) * part_rows],
+            "col",
+            [(c, c + panel_width * h) for c in range(panel_width)],
+        )
+        part = jnp.where(col_place // panel_width == h, moved, part)
     part = part.reshape(part_rows * BLK // 128, 128)
     gathered = lax.all_gather(part, "col", axis=0, tiled=False)
     gathered, extended = lax.optimization_barrier((gathered, extended))

time: 496 us -> 486 us (0.980)
  local copies, waits for them, and re-layouts: 140 us -> 131 us
  waiting for transfers between devices: 79.8 us -> 86.2 us
  other arithmetic: 150 us -> 144 us
    all_to_all x2, waiting for transfers between devices: 32.5 us -> 37.6 us  [on_device(): lax.all_to_all(outgoing, 'row', split_axis=0, concat_axis=0, tiled=True)]
  transfers between devices with their start and end apart: 9 -> 9, of which waited for: 6 -> 6; matrix products, arithmetic and copies ran while one was open for 47% -> 46% of each run, Pallas kernels for 0% -> 0%
where the time goes in v11:
time: 486 us; the launch traced here: 477 us
  other arithmetic  144 us (30%)
  local copies, waits for them, and re-layouts  131 us (27%)
  waiting for transfers between devices  86.2 us (18%)
  starting transfers between devices  40.5 us (8%)
  matrix products  38.6 us (8%)
  between operations  20.6 us (4%)
  blocking collectives  16.6 us (3%)
    another operation x12, other arithmetic, factor_and_invert(): lpp = lax.linalg.cholesky(grid[p][p], symmetrize_input=False)  49.7 us
    another operation x8, other arithmetic, factor_and_invert(): dinv = jax.scipy.linalg.solve_triangular(lpp, eye, lower=True)  42.2 us
    all_to_all x2, waiting for transfers between devices, on_device(): lax.all_to_all(outgoing, 'row', split_axis=0, concat_axis=0, tiled=True)  37.6 us
    all_gather x1, waiting for transfers between devices, on_device(): across = lax.all_gather(piece, 'row', axis=0, tiled=True)  36.4 us
    gather x10, local copies, waits for them, and re-layouts, take_slabs(): return jnp.take(source, indices, axis=0)  35.8 us
    dot_general x1, matrix products, on_device(): update = jnp.einsum('rp,cp->rc', panel_factor, across, precision=exact_mode)  18.8 us
    all_gather x1, blocking collectives, on_device(): corner_row = lax.all_gather(share, 'col', axis=0, tiled=True)  16.6 us
    add x1, other arithmetic, on_device(): extended = front_matrix + placed[0] + placed[1]  13.8 us
  transfers between devices with their start and end apart: 9, of which 6 were waited for; matrix products, arithmetic and copies ran while one was open for 46% of the time, Pallas kernels for 0%

profile of v11, /device:TPU:1, one launch (start us, length us, event | category | flops | bytes accessed | tf_op | source)
XLA Modules:
  0.0 477.4 jit_solution(10512055601237159532)
XLA Ops:
  35.8 16.8 %all-to-all-done = f32[8,128,512]{2,1,0:T(8,128)S(1)} async-done(((f32[8,128,512]{2,1,0:T(8,128)}), f32[8,128,512]{2,1,0:T(8,128)S(1)}, u32[]{:S(2)}, u32[]{:S(2)}) %all-to-all-start) | async-done | bytes 2097184 | tf_op jit(solution)/shard_map/all_to_all | solution.py:112
  63.4 20.7 %all-to-all-done.1 = f32[8,128,512]{2,1,0:T(8,128)} async-done(((f32[8,128,512]{2,1,0:T(8,128)}), f32[8,128,512]{2,1,0:T(8,128)}, u32[]{:S(2)}, u32[]{:S(2)}) %all-to-all-start.1) | async-done | bytes 2097184 | tf_op jit(solution)/shard_map/all_to_all | solution.py:112
  87.6 7.8 %all-to-all-start.3 = ((f32[16,4,512]{2,1,0:T(4,128)}), f32[16,4,512]{2,1,0:T(4,128)S(1)}, u32[]{:S(2)}, u32[]{:S(2)}) async-start(f32[16,4,512]{2,1,0:T(4,128)} %reshape.479), calls=%async_computation.3 | async-start | bytes 262144 | tf_op jit(solution)/shard_map/all_to_all | solution.py:131
  102.1 16.6 %all-gather = f32[16,4,512]{2,1,0:T(4,128)S(1)} all-gather(f32[1,4,512]{2,1,0:T(4,128)S(1)} %bitcast.243), channel_id=1, replica_groups=mesh['row'=8,'col'=16] {'col'}, dimensions={0}, use_global_device_ids=true | all-gather | bytes 139264 | tf_op jit(solution)/shard_map/all_gather | solution.py:133
  137.5 12.9 %copy.236 = f32[2,1024,1024]{2,0,1:T(2,128)} copy(f32[2,1024,1024]{2,1,0:T(8,128)S(1)} %pad_maximum_fusion) | data formatting | bytes 16777216 | tf_op jit(solution)/shard_map/stack | solution.py:141
  158.5 11.7 %custom-call.16 = f32[128,128]{1,0:T(8,128)S(1)} custom-call(f32[128,128]{1,0:T(8,128)S(1)} %slice.210), custom_call_target="Cholesky" | custom-call | tf_op jit(solution)/shard_map/cholesky/custom-call.1 | solution.py:26
  171.5 9.8 %custom-call.17 = f32[1,128,128]{1,2,0:T(8,128)S(1)} custom-call(f32[1,128,128]{2,1,0:T(8,128)S(1)} %get-tuple-element.30), custom_call_target="InvertDiagBlocksLowerTriangular" | custom-call | tf_op jit(solution)/shard_map/jit(_solve_triangular)/triangular_solve | solution.py:27
  183.1 11.7 %custom-call.18 = f32[128,128]{1,0:T(8,128)S(1)} custom-call(f32[128,128]{1,0:T(8,128)S(1)} %convolution_subtract_fusion.9), custom_call_target="Cholesky" | custom-call | tf_op jit(solution)/shard_map/cholesky/custom-call.1 | solution.py:26
  196.2 10.2 %custom-call.19 = f32[1,128,128]{1,2,0:T(8,128)S(1)} custom-call(f32[1,128,128]{2,1,0:T(8,128)S(1)} %get-tuple-element.28), custom_call_target="InvertDiagBlocksLowerTriangular" | custom-call | tf_op jit(solution)/shard_map/jit(_solve_triangular)/triangular_solve | solution.py:27
  207.7 11.7 %custom-call.20 = f32[128,128]{1,0:T(8,128)S(1)} custom-call(f32[128,128]{1,0:T(8,128)S(1)} %convolution_subtract_fusion.6), custom_call_target="Cholesky" | custom-call | tf_op jit(solution)/shard_map/cholesky/custom-call.1 | solution.py:26
  220.8 9.8 %custom-call.21 = f32[1,128,128]{1,2,0:T(8,128)S(1)} custom-call(f32[1,128,128]{2,1,0:T(8,128)S(1)} %get-tuple-element.26), custom_call_target="InvertDiagBlocksLowerTriangular" | custom-call | tf_op jit(solution)/shard_map/jit(_solve_triangular)/triangular_solve | solution.py:27
  233.9 11.9 %custom-call.22 = f32[128,128]{1,0:T(8,128)S(1)} custom-call(f32[128,128]{1,0:T(8,128)S(1)} %convolution_subtract_fusion), custom_call_target="Cholesky" | custom-call | tf_op jit(solution)/shard_map/cholesky/custom-call.1 | solution.py:26
  247.1 9.8 %custom-call.23 = f32[1,128,128]{1,2,0:T(8,128)S(1)} custom-call(f32[1,128,128]{2,1,0:T(8,128)S(1)} %get-tuple-element.24), custom_call_target="InvertDiagBlocksLowerTriangular" | custom-call | tf_op jit(solution)/shard_map/jit(_solve_triangular)/triangular_solve | solution.py:27
  294.5 7.7 %gather_fusion.3 = f32[32,64,1024]{2,1,0:T(8,128)} fusion(f32[2,16,64,1024]{3,2,1,0:T(8,128)} %bitcast.219, s32[32]{0:T(128)S(1)} %reshape.594), kind=kCustom, calls=%fused_computation.13 | custom fusion | bytes 16777472 | tf_op jit(solution)/shard_map/vmap(jit(_take))/gather | solution.py:15
  308.2 8.7 %copy.267 = f32[2,1024,1024]{2,1,0:T(8,128)} copy(f32[2,1024,1024]{1,2,0:T(8,128)} %fusion.1) | data formatting | bytes 16777216 | tf_op jit(solution)/shard_map/transpose | solution.py:149
  316.9 12.6 %gather_fusion.4 = f32[64,64,1024]{2,1,0:T(8,128)} fusion(f32[2,16,64,1024]{3,2,1,0:T(8,128)} %bitcast.220, s32[64]{0:T(128)S(1)} %reshape.600), kind=kCustom, calls=%fused_computation.14 | custom fusion | bytes 33554944 | tf_op jit(solution)/shard_map/vmap(jit(_take))/gather | solution.py:15
  332.4 7.6 %select_multiply_fusion = f32[2,32,64,1024]{3,2,1,0:T(8,128)S(1)} fusion(f32[2,32,64,1024]{3,2,1,0:T(8,128)} %bitcast.221, f32[2,32]{1,0:T(2,128)S(1)} %fusion.33, pred[2,32]{1,0:T(4,128)(4,1)S(1)} %compare_and_fusion.11), kind=kLoop, calls=%fused_computation.15 | loop fusion | flops 8388608 | bytes 33554752 | tf_op jit(solution)/shard_map/mul | solution.py:150
  346.7 13.8 %bitcast_add_fusion = f32[2048,1024]{1,0:T(8,128)} fusion(f32[1,32,64,1024]{3,2,1,0:T(8,128)} %get-tuple-element.45, f32[2048,1024]{1,0:T(8,128)} %param.33, f32[1,32,64,1024]{3,2,1,0:T(8,128)} %get-tuple-element.44), kind=kLoop, calls=%fused_computation.17 | loop fusion | flops 4194304 | bytes 33554432 | tf_op jit(solution)/shard_map/add | solution.py:152
  367.5 11.4 %copy.268 = f32[2,1024,8,64]{3,2,1,0:T(8,128)} copy(f32[2,1024,8,64]{3,1,2,0:T(8,128)} %bitcast.226) | data formatting | bytes 8388608 | tf_op jit(solution)/shard_map/transpose | solution.py:175
  379.0 7.8 %dot_general.136 = f32[32,64,512]{2,1,0:T(8,128)} reshape(f32[2,1024,8,64]{3,2,1,0:T(8,128)} %copy.268) | data formatting | bytes 8388608 | tf_op jit(solution)/shard_map/rp,qp->rq/dot_general | solution.py:177
  386.7 9.6 %select_select_fusion = f32[32,64,512]{2,1,0:T(8,128)S(1)} fusion(f32[32,64,512]{2,1,0:T(8,128)} %gather_fusion.2, f32[32,64,512]{2,1,0:T(8,128)} %dot_general.136, pred[32]{0:T(512)(128)(4,1)S(1)} %get-tuple-element.80, pred[32]{0:T(512)(128)(4,1)S(1)} %broadcast_compare_fusion.1, f32[512,512]{1,0:T(8,128)S(1)} %copy-done.4), kind=kOutput, calls=%fused_computation.25 | convolution fusion | flops 6444548096 | bytes 13631552 | tf_op jit(solution)/shard_map/rp,qp->rq/dot_general | solution.py:177
  398.6 11.8 %collective-permute-start.1 = (f32[128,512]{1,0:T(8,128)S(1)}, f32[128,512]{1,0:T(8,128)S(1)}, u32[]{:S(2)}, u32[]{:S(2)}) collective-permute-start(f32[128,512]{1,0:T(8,128)S(1)} %constant_dynamic-slice_fusion.1), channel_id=1, source_target_pairs={{0,0},{1,16},{2,32},{3,48},{4,64},{5,80},{6,96},{7,112},{8,8},{9,2... | collective-permute-start | bytes 786440 | tf_op jit(solution)/shard_map/ppermute | solution.py:198
  415.2 36.4 %all-gather.9.cloned.1.call-done = f32[1024,512]{1,0:T(8,128)} async-done(((f32[128,512]{1,0:T(8,128)}), f32[1024,512]{1,0:T(8,128)}) %all-gather.9.cloned.1.call-update) | async-done | bytes 2097168 | tf_op jit(solution)/shard_map/all_gather | solution.py:199
  451.7 18.8 %subtract_select_fusion = f32[2048,1024]{1,0:T(8,128)} fusion(f32[2048,1024]{1,0:T(8,128)} %bitcast_add_fusion, pred[1024]{0:T(1024)(128)(4,1)S(1)} %fusion.46, pred[2048]{0:T(1024)(128)(4,1)S(1)} %fusion.40, f32[2048,512]{1,0:T(8,128)} %bitcast.223, f32[1024,512]{1,0:T(8,128)} %all-gather.9.cloned.1.call-done), kind=kOutput, calls=%fused_computation.22 | convolution fusion | flops 12891193344 | bytes 23071744 | tf_op jit(solution)/shard_map/rp,cp->rc/dot_general | solution.py:200
  (225 shorter events, 149.0 us)
Async XLA Ops:
  18.7 7.7 %copy-start.7 = (s32[2,128]{1,0:T(2,128)S(1)}, s32[2,128]{1,0:T(2,128)}, u32[]{:S(2)}) copy-start(s32[2,128]{1,0:T(2,128)} %param.36) | copy-start | bytes 3076
  20.5 10.3 %copy-start.6 = (s32[2,128]{1,0:T(2,128)S(1)}, s32[2,128]{1,0:T(2,128)}, u32[]{:S(2)}) copy-start(s32[2,128]{1,0:T(2,128)} %param.35) | copy-start | bytes 3076
  20.5 32.1 %all-to-all-start = ((f32[8,128,512]{2,1,0:T(8,128)}), f32[8,128,512]{2,1,0:T(8,128)S(1)}, u32[]{:S(2)}, u32[]{:S(2)}) async-start(f32[8,128,512]{2,1,0:T(8,128)} %bitcast.235), calls=%async_computation | async-start | bytes 4194304 | tf_op jit(solution)/shard_map/all_to_all | solution.py:112
  52.6 33.3 %copy-start.3 = (f32[8,128,512]{2,1,0:T(8,128)}, f32[8,128,512]{2,1,0:T(8,128)S(1)}, u32[]{:S(2)}) copy-start(f32[8,128,512]{2,1,0:T(8,128)S(1)} %all-to-all-done) | copy-start | bytes 6291460
  52.6 31.6 %all-to-all-start.1 = ((f32[8,128,512]{2,1,0:T(8,128)}), f32[8,128,512]{2,1,0:T(8,128)}, u32[]{:S(2)}, u32[]{:S(2)}) async-start(f32[8,128,512]{2,1,0:T(8,128)} %bitcast.234), calls=%async_computation.1 | async-start | bytes 4194304 | tf_op jit(solution)/shard_map/all_to_all | solution.py:112
  87.6 14.5 %all-to-all-start.3 = ((f32[16,4,512]{2,1,0:T(4,128)}), f32[16,4,512]{2,1,0:T(4,128)S(1)}, u32[]{:S(2)}, u32[]{:S(2)}) async-start(f32[16,4,512]{2,1,0:T(4,128)} %reshape.479), calls=%async_computation.3 | async-start | bytes 262144 | tf_op jit(solution)/shard_map/all_to_all | solution.py:131
  95.3 60.1 %all-gather.5.cloned.1.call-start = ((), (), s32[]{:S(2)}) async-start(), calls=%async_computation.4 | async-start | bytes 1179648 | tf_op jit(solution)/shard_map/all_gather | solution.py:134
  131.6 3.6 copy-start.2
  150.4 112.8 %all-to-all-start.2 = ((f32[2,1024,1024]{2,0,1:T(2,128)}), f32[2,1024,1024]{2,0,1:T(2,128)}, u32[]{:S(2)}, u32[]{:S(2)}) async-start(f32[2,1024,1024]{2,0,1:T(2,128)} %copy.236), calls=%async_computation.2 | async-start | bytes 16777216 | tf_op jit(solution)/shard_map/all_to_all | solution.py:143
  155.2 205.4 %all-gather.7.cloned.1.call-start = ((), (), s32[]{:S(2)}) async-start(), calls=%async_computation.5 | async-start | bytes 4456448 | tf_op jit(solution)/shard_map/all_gather | solution.py:172
  269.3 4.7 copy-start
  282.2 10.8 %collective-permute-start = (f32[1024,64]{1,0:T(8,128)S(1)}, f32[1024,64]{1,0:T(8,128)S(1)}, u32[]{:S(2)}, u32[]{:S(2)}) collective-permute-start(f32[1024,64]{1,0:T(8,128)S(1)} %slice.222), channel_id=1, source_target_pairs={{0,8},{1,9},{2,10},{3,11},{4,12},{5,13},{6,14},{7,15},{16,24},{17,... | collective-permute-start | bytes 786440 | tf_op jit(solution)/shard_map/ppermute | solution.py:165
  293.9 157.8 %all-gather.9.cloned.1.call-start = ((), (), s32[]{:S(2)}) async-start(), calls=%async_computation.6 | async-start | bytes 2359296 | tf_op jit(solution)/shard_map/all_gather | solution.py:199
  379.0 7.8 %copy-start.4 = (f32[512,512]{1,0:T(8,128)S(1)}, f32[512,512]{1,0:T(8,128)}, u32[]{:S(2)}) copy-start(f32[512,512]{1,0:T(8,128)} %fusion.7) | copy-start | bytes 3145732
  396.4 2.0 copy-start.1
  398.6 15.9 %collective-permute-start.1 = (f32[128,512]{1,0:T(8,128)S(1)}, f32[128,512]{1,0:T(8,128)S(1)}, u32[]{:S(2)}, u32[]{:S(2)}) collective-permute-start(f32[128,512]{1,0:T(8,128)S(1)} %constant_dynamic-slice_fusion.1), channel_id=1, source_target_pairs={{0,0},{1,16},{2,32},{3,48},{4,64},{5,80},{6,96},{7,112},{8,8},{9,2... | collective-permute-start | bytes 786440 | tf_op jit(solution)/shard_map/ppermute | solution.py:198
  414.5 0.7 copy-start.5
Sparse Core Ops, SparseCore 0:
  119.5 27.3 all-gather.4
  294.0 59.5 all-gather.6
  415.3 36.2 all-gather.8

commit v12 on v11

--- a/solution.py
+++ b/solution.py
@@ -196,7 +196,9 @@
     piece_rows = chosen.shape[0] // row_count
     piece = lax.dynamic_slice_in_dim(chosen, (col_place % row_count) * piece_rows, piece_rows, axis=0)
     piece = lax.ppermute(piece, ("row", "col"), pairs)
-    across = lax.all_gather(piece, "row", axis=0, tiled=True)
+    copies = jnp.broadcast_to(piece[None], (row_count,) + piece.shape)
+    across = lax.all_to_all(copies, "row", split_axis=0, concat_axis=0, tiled=True)
+    across = across.reshape(row_count * piece_rows, PANEL)
     update = jnp.einsum("rp,cp->rc", panel_factor, across, precision=exact_mode)
     logical_row = jnp.arange(local_rows) // BLK * row_count + row_place
     logical_col = jnp.arange(local_cols) // BLK * col_count + col_place

time: 486 us -> 493 us (1.014)
  starting transfers between devices: 40.5 us -> 56.1 us
  waiting for transfers between devices: 86.2 us -> 75.9 us
    all_gather x1 -> x0, waiting for transfers between devices: 36.4 us -> none  [on_device(): across = lax.all_gather(piece, 'row', axis=0, tiled=True)]
    all_to_all x0 -> x1, waiting for transfers between devices: none -> 26.2 us  [on_device(): lax.all_to_all(copies, 'row', split_axis=0, concat_axis=0, tiled=True)]
    all_to_all x0 -> x1, starting transfers between devices: none -> 15.8 us  [on_device(): lax.all_to_all(copies, 'row', split_axis=0, concat_axis=0, tiled=True)]
  transfers between devices with their start and end apart: 9 -> 9, of which waited for: 6 -> 6; matrix products, arithmetic and copies ran while one was open for 46% -> 45% of each run, Pallas kernels for 0% -> 0%
where the time goes in v12:
time: 493 us; the launch traced here: 483 us
  other arithmetic  144 us (29%)
  local copies, waits for them, and re-layouts  132 us (27%)
  waiting for transfers between devices  75.9 us (15%)
  starting transfers between devices  56.1 us (11%)
  matrix products  37.9 us (8%)
  between operations  20.9 us (4%)
  blocking collectives  16.6 us (3%)
    another operation x12, other arithmetic, factor_and_invert(): lpp = lax.linalg.cholesky(grid[p][p], symmetrize_input=False)  49.7 us
    another operation x8, other arithmetic, factor_and_invert(): dinv = jax.scipy.linalg.solve_triangular(lpp, eye, lower=True)  42.2 us
    all_to_all x2, waiting for transfers between devices, on_device(): lax.all_to_all(outgoing, 'row', split_axis=0, concat_axis=0, tiled=True)  37.6 us
    gather x10, local copies, waits for them, and re-layouts, take_slabs(): return jnp.take(source, indices, axis=0)  35.8 us
    all_to_all x1, waiting for transfers between devices, on_device(): lax.all_to_all(copies, 'row', split_axis=0, concat_axis=0, tiled=True)  26.2 us
    dot_general x1, matrix products, on_device(): update = jnp.einsum('rp,cp->rc', panel_factor, across, precision=exact_mode)  18.1 us
    all_gather x1, blocking collectives, on_device(): corner_row = lax.all_gather(share, 'col', axis=0, tiled=True)  16.6 us
    all_to_all x1, starting transfers between devices, on_device(): lax.all_to_all(copies, 'row', split_axis=0, concat_axis=0, tiled=True)  15.8 us
  transfers between devices with their start and end apart: 9, of which 6 were waited for; matrix products, arithmetic and copies ran while one was open for 45% of the time, Pallas kernels for 0%

profile of v12, /device:TPU:1, one launch (start us, length us, event | category | flops | bytes accessed | tf_op | source)
XLA Modules:
  0.0 483.3 jit_solution(16710100772771539573)
XLA Ops:
  35.8 16.8 %all-to-all-done = f32[8,128,512]{2,1,0:T(8,128)S(1)} async-done(((f32[8,128,512]{2,1,0:T(8,128)}), f32[8,128,512]{2,1,0:T(8,128)S(1)}, u32[]{:S(2)}, u32[]{:S(2)}) %all-to-all-start) | async-done | bytes 2097184 | tf_op jit(solution)/shard_map/all_to_all | solution.py:112
  63.4 20.7 %all-to-all-done.1 = f32[8,128,512]{2,1,0:T(8,128)} async-done(((f32[8,128,512]{2,1,0:T(8,128)}), f32[8,128,512]{2,1,0:T(8,128)}, u32[]{:S(2)}, u32[]{:S(2)}) %all-to-all-start.1) | async-done | bytes 2097184 | tf_op jit(solution)/shard_map/all_to_all | solution.py:112
  87.6 7.8 %all-to-all-start.3 = ((f32[16,4,512]{2,1,0:T(4,128)}), f32[16,4,512]{2,1,0:T(4,128)S(1)}, u32[]{:S(2)}, u32[]{:S(2)}) async-start(f32[16,4,512]{2,1,0:T(4,128)} %reshape.483), calls=%async_computation.3 | async-start | bytes 262144 | tf_op jit(solution)/shard_map/all_to_all | solution.py:131
  102.1 16.6 %all-gather = f32[16,4,512]{2,1,0:T(4,128)S(1)} all-gather(f32[1,4,512]{2,1,0:T(4,128)S(1)} %bitcast.245), channel_id=1, replica_groups=mesh['row'=8,'col'=16] {'col'}, dimensions={0}, use_global_device_ids=true | all-gather | bytes 139264 | tf_op jit(solution)/shard_map/all_gather | solution.py:133
  137.5 12.9 %copy.236 = f32[2,1024,1024]{2,0,1:T(2,128)} copy(f32[2,1024,1024]{2,1,0:T(8,128)S(1)} %pad_maximum_fusion) | data formatting | bytes 16777216 | tf_op jit(solution)/shard_map/stack | solution.py:141
  158.5 11.7 %custom-call.16 = f32[128,128]{1,0:T(8,128)S(1)} custom-call(f32[128,128]{1,0:T(8,128)S(1)} %slice.210), custom_call_target="Cholesky" | custom-call | tf_op jit(solution)/shard_map/cholesky/custom-call.1 | solution.py:26
  171.5 9.8 %custom-call.17 = f32[1,128,128]{1,2,0:T(8,128)S(1)} custom-call(f32[1,128,128]{2,1,0:T(8,128)S(1)} %get-tuple-element.30), custom_call_target="InvertDiagBlocksLowerTriangular" | custom-call | tf_op jit(solution)/shard_map/jit(_solve_triangular)/triangular_solve | solution.py:27
  183.1 11.7 %custom-call.18 = f32[128,128]{1,0:T(8,128)S(1)} custom-call(f32[128,128]{1,0:T(8,128)S(1)} %convolution_subtract_fusion.9), custom_call_target="Cholesky" | custom-call | tf_op jit(solution)/shard_map/cholesky/custom-call.1 | solution.py:26
  196.2 10.2 %custom-call.19 = f32[1,128,128]{1,2,0:T(8,128)S(1)} custom-call(f32[1,128,128]{2,1,0:T(8,128)S(1)} %get-tuple-element.28), custom_call_target="InvertDiagBlocksLowerTriangular" | custom-call | tf_op jit(solution)/shard_map/jit(_solve_triangular)/triangular_solve | solution.py:27
  207.7 11.7 %custom-call.20 = f32[128,128]{1,0:T(8,128)S(1)} custom-call(f32[128,128]{1,0:T(8,128)S(1)} %convolution_subtract_fusion.6), custom_call_target="Cholesky" | custom-call | tf_op jit(solution)/shard_map/cholesky/custom-call.1 | solution.py:26
  220.8 9.8 %custom-call.21 = f32[1,128,128]{1,2,0:T(8,128)S(1)} custom-call(f32[1,128,128]{2,1,0:T(8,128)S(1)} %get-tuple-element.26), custom_call_target="InvertDiagBlocksLowerTriangular" | custom-call | tf_op jit(solution)/shard_map/jit(_solve_triangular)/triangular_solve | solution.py:27
  233.9 11.9 %custom-call.22 = f32[128,128]{1,0:T(8,128)S(1)} custom-call(f32[128,128]{1,0:T(8,128)S(1)} %convolution_subtract_fusion), custom_call_target="Cholesky" | custom-call | tf_op jit(solution)/shard_map/cholesky/custom-call.1 | solution.py:26
  247.1 9.8 %custom-call.23 = f32[1,128,128]{1,2,0:T(8,128)S(1)} custom-call(f32[1,128,128]{2,1,0:T(8,128)S(1)} %get-tuple-element.24), custom_call_target="InvertDiagBlocksLowerTriangular" | custom-call | tf_op jit(solution)/shard_map/jit(_solve_triangular)/triangular_solve | solution.py:27
  294.5 7.7 %gather_fusion.3 = f32[32,64,1024]{2,1,0:T(8,128)} fusion(f32[2,16,64,1024]{3,2,1,0:T(8,128)} %bitcast.220, s32[32]{0:T(128)S(1)} %reshape.599), kind=kCustom, calls=%fused_computation.13 | custom fusion | bytes 16777472 | tf_op jit(solution)/shard_map/vmap(jit(_take))/gather | solution.py:15
  308.2 8.7 %copy.267 = f32[2,1024,1024]{2,1,0:T(8,128)} copy(f32[2,1024,1024]{1,2,0:T(8,128)} %fusion.1) | data formatting | bytes 16777216 | tf_op jit(solution)/shard_map/transpose | solution.py:149
  316.9 12.6 %gather_fusion.4 = f32[64,64,1024]{2,1,0:T(8,128)} fusion(f32[2,16,64,1024]{3,2,1,0:T(8,128)} %bitcast.221, s32[64]{0:T(128)S(1)} %reshape.605), kind=kCustom, calls=%fused_computation.14 | custom fusion | bytes 33554944 | tf_op jit(solution)/shard_map/vmap(jit(_take))/gather | solution.py:15
  346.7 13.8 %bitcast_add_fusion = f32[2048,1024]{1,0:T(8,128)} fusion(f32[1,32,64,1024]{3,2,1,0:T(8,128)} %get-tuple-element.45, f32[2048,1024]{1,0:T(8,128)} %param.33, f32[1,32,64,1024]{3,2,1,0:T(8,128)} %get-tuple-element.44), kind=kLoop, calls=%fused_computation.17 | loop fusion | flops 4194304 | bytes 33554432 | tf_op jit(solution)/shard_map/add | solution.py:152
  367.5 11.4 %copy.268 = f32[2,1024,8,64]{3,2,1,0:T(8,128)} copy(f32[2,1024,8,64]{3,1,2,0:T(8,128)} %bitcast.227) | data formatting | bytes 8388608 | tf_op jit(solution)/shard_map/transpose | solution.py:175
  378.9 7.8 %dot_general.136 = f32[32,64,512]{2,1,0:T(8,128)} reshape(f32[2,1024,8,64]{3,2,1,0:T(8,128)} %copy.268) | data formatting | bytes 8388608 | tf_op jit(solution)/shard_map/rp,qp->rq/dot_general | solution.py:177
  386.7 9.6 %select_select_fusion = f32[32,64,512]{2,1,0:T(8,128)S(1)} fusion(f32[32,64,512]{2,1,0:T(8,128)} %gather_fusion.2, f32[32,64,512]{2,1,0:T(8,128)} %dot_general.136, pred[32]{0:T(512)(128)(4,1)S(1)} %get-tuple-element.80, pred[32]{0:T(512)(128)(4,1)S(1)} %broadcast_compare_fusion.1, f32[512,512]{1,0:T(8,128)S(1)} %copy-done.4), kind=kOutput, calls=%fused_computation.25 | convolution fusion | flops 6444548096 | bytes 13631552 | tf_op jit(solution)/shard_map/rp,qp->rq/dot_general | solution.py:177
  398.6 11.8 %collective-permute-start.1 = (f32[128,512]{1,0:T(8,128)S(1)}, f32[128,512]{1,0:T(8,128)S(1)}, u32[]{:S(2)}, u32[]{:S(2)}) collective-permute-start(f32[128,512]{1,0:T(8,128)S(1)} %constant_dynamic-slice_fusion.1), channel_id=1, source_target_pairs={{0,0},{1,16},{2,32},{3,48},{4,64},{5,80},{6,96},{7,112},{8,8},{9,2... | collective-permute-start | bytes 786440 | tf_op jit(solution)/shard_map/ppermute | solution.py:198
  416.0 15.8 %all-to-all-start.4 = ((f32[8,128,512]{2,1,0:T(8,128)}), f32[8,128,512]{2,1,0:T(8,128)S(1)}, u32[]{:S(2)}, u32[]{:S(2)}) async-start(f32[8,128,512]{2,1,0:T(8,128)} %broadcast_in_dim.163), calls=%async_computation.4 | async-start | bytes 4194304 | tf_op jit(solution)/shard_map/all_to_all | solution.py:200
  431.8 26.2 %all-to-all-done.4 = f32[8,128,512]{2,1,0:T(8,128)S(1)} async-done(((f32[8,128,512]{2,1,0:T(8,128)}), f32[8,128,512]{2,1,0:T(8,128)S(1)}, u32[]{:S(2)}, u32[]{:S(2)}) %all-to-all-start.4) | async-done | bytes 2097184 | tf_op jit(solution)/shard_map/all_to_all | solution.py:200
  458.0 18.1 %subtract_select_fusion = f32[2048,1024]{1,0:T(8,128)} fusion(f32[2048,1024]{1,0:T(8,128)} %bitcast_add_fusion, pred[1024]{0:T(1024)(128)(4,1)S(1)} %fusion.46, pred[2048]{0:T(1024)(128)(4,1)S(1)} %fusion.40, f32[2048,512]{1,0:T(8,128)} %bitcast.224, f32[1024,512]{1,0:T(8,128)S(1)} %bitcast.235), kind=kOutput, calls=%fused_computation.22 | convolution fusion | flops 12891193344 | bytes 23071744 | tf_op jit(solution)/shard_map/rp,cp->rc/dot_general | solution.py:202
  (223 shorter events, 157.5 us)
Async XLA Ops:
  18.7 7.7 %copy-start.6 = (s32[2,128]{1,0:T(2,128)S(1)}, s32[2,128]{1,0:T(2,128)}, u32[]{:S(2)}) copy-start(s32[2,128]{1,0:T(2,128)} %param.36) | copy-start | bytes 3076
  20.5 10.3 %copy-start.5 = (s32[2,128]{1,0:T(2,128)S(1)}, s32[2,128]{1,0:T(2,128)}, u32[]{:S(2)}) copy-start(s32[2,128]{1,0:T(2,128)} %param.35) | copy-start | bytes 3076
  20.5 32.1 %all-to-all-start = ((f32[8,128,512]{2,1,0:T(8,128)}), f32[8,128,512]{2,1,0:T(8,128)S(1)}, u32[]{:S(2)}, u32[]{:S(2)}) async-start(f32[8,128,512]{2,1,0:T(8,128)} %bitcast.237), calls=%async_computation | async-start | bytes 4194304 | tf_op jit(solution)/shard_map/all_to_all | solution.py:112
  52.6 33.3 %copy-start.3 = (f32[8,128,512]{2,1,0:T(8,128)}, f32[8,128,512]{2,1,0:T(8,128)S(1)}, u32[]{:S(2)}) copy-start(f32[8,128,512]{2,1,0:T(8,128)S(1)} %all-to-all-done) | copy-start | bytes 6291460
  52.6 31.6 %all-to-all-start.1 = ((f32[8,128,512]{2,1,0:T(8,128)}), f32[8,128,512]{2,1,0:T(8,128)}, u32[]{:S(2)}, u32[]{:S(2)}) async-start(f32[8,128,512]{2,1,0:T(8,128)} %bitcast.236), calls=%async_computation.1 | async-start | bytes 4194304 | tf_op jit(solution)/shard_map/all_to_all | solution.py:112
  87.6 14.5 %all-to-all-start.3 = ((f32[16,4,512]{2,1,0:T(4,128)}), f32[16,4,512]{2,1,0:T(4,128)S(1)}, u32[]{:S(2)}, u32[]{:S(2)}) async-start(f32[16,4,512]{2,1,0:T(4,128)} %reshape.483), calls=%async_computation.3 | async-start | bytes 262144 | tf_op jit(solution)/shard_map/all_to_all | solution.py:131
  95.3 60.1 %all-gather.4.cloned.1.call-start = ((), (), s32[]{:S(2)}) async-start(), calls=%async_computation.5 | async-start | bytes 1179648 | tf_op jit(solution)/shard_map/all_gather | solution.py:134
  131.6 3.6 copy-start.2
  150.4 112.8 %all-to-all-start.2 = ((f32[2,1024,1024]{2,0,1:T(2,128)}), f32[2,1024,1024]{2,0,1:T(2,128)}, u32[]{:S(2)}, u32[]{:S(2)}) async-start(f32[2,1024,1024]{2,0,1:T(2,128)} %copy.236), calls=%async_computation.2 | async-start | bytes 16777216 | tf_op jit(solution)/shard_map/all_to_all | solution.py:143
  155.2 205.4 %all-gather.6.cloned.1.call-start = ((), (), s32[]{:S(2)}) async-start(), calls=%async_computation.6 | async-start | bytes 4456448 | tf_op jit(solution)/shard_map/all_gather | solution.py:172
  269.3 4.7 copy-start
  282.2 10.8 %collective-permute-start = (f32[1024,64]{1,0:T(8,128)S(1)}, f32[1024,64]{1,0:T(8,128)S(1)}, u32[]{:S(2)}, u32[]{:S(2)}) collective-permute-start(f32[1024,64]{1,0:T(8,128)S(1)} %slice.222), channel_id=1, source_target_pairs={{0,8},{1,9},{2,10},{3,11},{4,12},{5,13},{6,14},{7,15},{16,24},{17,... | collective-permute-start | bytes 786440 | tf_op jit(solution)/shard_map/ppermute | solution.py:165
  378.9 7.8 %copy-start.4 = (f32[512,512]{1,0:T(8,128)S(1)}, f32[512,512]{1,0:T(8,128)}, u32[]{:S(2)}) copy-start(f32[512,512]{1,0:T(8,128)} %fusion.7) | copy-start | bytes 3145732
  396.3 2.0 copy-start.1
  398.6 15.8 %collective-permute-start.1 = (f32[128,512]{1,0:T(8,128)S(1)}, f32[128,512]{1,0:T(8,128)S(1)}, u32[]{:S(2)}, u32[]{:S(2)}) collective-permute-start(f32[128,512]{1,0:T(8,128)S(1)} %constant_dynamic-slice_fusion.1), channel_id=1, source_target_pairs={{0,0},{1,16},{2,32},{3,48},{4,64},{5,80},{6,96},{7,112},{8,8},{9,2... | collective-permute-start | bytes 786440 | tf_op jit(solution)/shard_map/ppermute | solution.py:198
  416.0 42.0 %all-to-all-start.4 = ((f32[8,128,512]{2,1,0:T(8,128)}), f32[8,128,512]{2,1,0:T(8,128)S(1)}, u32[]{:S(2)}, u32[]{:S(2)}) async-start(f32[8,128,512]{2,1,0:T(8,128)} %broadcast_in_dim.163), calls=%async_computation.4 | async-start | bytes 4194304 | tf_op jit(solution)/shard_map/all_to_all | solution.py:200
Sparse Core Ops, SparseCore 0:
  119.5 27.3 all-gather.3
  294.0 59.5 all-gather.5

commit v13 on v11

--- a/solution.py
+++ b/solution.py
@@ -130,7 +130,9 @@
     share = partial.reshape(col_count, BLK // col_count, PANEL)
     share = lax.all_to_all(share, "col", split_axis=0, concat_axis=0, tiled=True)
     share = jnp.sum(share, axis=0)
-    corner_row = lax.all_gather(share, "col", axis=0, tiled=True)
+    spread_share = jnp.broadcast_to(share[None], (col_count,) + share.shape)
+    corner_row = lax.all_to_all(spread_share, "col", split_axis=0, concat_axis=0, tiled=True)
+    corner_row = corner_row.reshape(BLK, PANEL)
     corner = lax.all_gather(corner_row, "row", axis=0, tiled=True)
 
     onward = []

time: 486 us -> 493 us (1.014)
  waiting for transfers between devices: 86.2 us -> 114 us
  blocking collectives: 16.6 us -> 0 us
  starting transfers between devices: 40.5 us -> 35.2 us
    all_gather x1 -> x0, blocking collectives: 16.6 us -> none  [on_device(): corner_row = lax.all_gather(share, 'col', axis=0, tiled=True)]
    all_to_all x1, waiting for transfers between devices: 0.01 us -> 14.7 us  [on_device(): lax.all_to_all(onward, 'col', split_axis=1, concat_axis=1, tiled=True)]
    ppermute x1, starting transfers between devices: 11.8 us -> 6.3 us  [on_device(): piece = lax.ppermute(piece, ('row', 'col'), pairs)]
    all_gather x1, waiting for transfers between devices: 36.4 us -> 41.9 us  [on_device(): across = lax.all_gather(piece, 'row', axis=0, tiled=True)]
  transfers between devices with their start and end apart: 9 -> 10, of which waited for: 6 -> 8; matrix products, arithmetic and copies ran while one was open for 46% -> 45% of each run, Pallas kernels for 0% -> 0%
where the time goes in v13:
time: 493 us; the launch traced here: 484 us
  other arithmetic  144 us (29%)
  local copies, waits for them, and re-layouts  132 us (27%)
  waiting for transfers between devices  114 us (23%)
  matrix products  38.6 us (8%)
  starting transfers between devices  35.2 us (7%)
  between operations  20.6 us (4%)
    another operation x12, other arithmetic, factor_and_invert(): lpp = lax.linalg.cholesky(grid[p][p], symmetrize_input=False)  49.7 us
    another operation x8, other arithmetic, factor_and_invert(): dinv = jax.scipy.linalg.solve_triangular(lpp, eye, lower=True)  42.2 us
    all_gather x1, waiting for transfers between devices, on_device(): across = lax.all_gather(piece, 'row', axis=0, tiled=True)  41.9 us
    all_to_all x2, waiting for transfers between devices, on_device(): lax.all_to_all(outgoing, 'row', split_axis=0, concat_axis=0, tiled=True)  37.7 us
    gather x10, local copies, waits for them, and re-layouts, take_slabs(): return jnp.take(source, indices, axis=0)  35.9 us
    dot_general x1, matrix products, on_device(): update = jnp.einsum('rp,cp->rc', panel_factor, across, precision=exact_mode)  18.8 us
    all_to_all x1, waiting for transfers between devices, on_device(): lax.all_to_all(onward, 'col', split_axis=1, concat_axis=1, tiled=True)  14.7 us
    add x1, other arithmetic, on_device(): extended = front_matrix + placed[0] + placed[1]  14.1 us
  transfers between devices with their start and end apart: 10, of which 8 were waited for; matrix products, arithmetic and copies ran while one was open for 45% of the time, Pallas kernels for 0%

profile of v13, /device:TPU:1, one launch (start us, length us, event | category | flops | bytes accessed | tf_op | source)
XLA Modules:
  0.0 483.9 jit_solution(18429896151439799153)
XLA Ops:
  35.6 17.0 %all-to-all-done = f32[8,128,512]{2,1,0:T(8,128)S(1)} async-done(((f32[8,128,512]{2,1,0:T(8,128)}), f32[8,128,512]{2,1,0:T(8,128)S(1)}, u32[]{:S(2)}, u32[]{:S(2)}) %all-to-all-start) | async-done | bytes 2097184 | tf_op jit(solution)/shard_map/all_to_all | solution.py:112
  63.5 20.7 %all-to-all-done.1 = f32[8,128,512]{2,1,0:T(8,128)} async-done(((f32[8,128,512]{2,1,0:T(8,128)}), f32[8,128,512]{2,1,0:T(8,128)}, u32[]{:S(2)}, u32[]{:S(2)}) %all-to-all-start.1) | async-done | bytes 2097184 | tf_op jit(solution)/shard_map/all_to_all | solution.py:112
  87.6 7.8 %all-to-all-start.3 = ((f32[16,4,512]{2,1,0:T(4,128)}), f32[16,4,512]{2,1,0:T(4,128)S(1)}, u32[]{:S(2)}, u32[]{:S(2)}) async-start(f32[16,4,512]{2,1,0:T(4,128)} %reshape.483), calls=%async_computation.3 | async-start | bytes 262144 | tf_op jit(solution)/shard_map/all_to_all | solution.py:131
  131.8 12.9 %copy.236 = f32[2,1024,1024]{2,0,1:T(2,128)} copy(f32[2,1024,1024]{2,1,0:T(8,128)S(1)} %pad_maximum_fusion) | data formatting | bytes 16777216 | tf_op jit(solution)/shard_map/stack | solution.py:143
  152.8 11.7 %custom-call.16 = f32[128,128]{1,0:T(8,128)S(1)} custom-call(f32[128,128]{1,0:T(8,128)S(1)} %slice.210), custom_call_target="Cholesky" | custom-call | tf_op jit(solution)/shard_map/cholesky/custom-call.1 | solution.py:26
  165.9 9.8 %custom-call.17 = f32[1,128,128]{1,2,0:T(8,128)S(1)} custom-call(f32[1,128,128]{2,1,0:T(8,128)S(1)} %get-tuple-element.30), custom_call_target="InvertDiagBlocksLowerTriangular" | custom-call | tf_op jit(solution)/shard_map/jit(_solve_triangular)/triangular_solve | solution.py:27
  177.4 11.7 %custom-call.18 = f32[128,128]{1,0:T(8,128)S(1)} custom-call(f32[128,128]{1,0:T(8,128)S(1)} %convolution_subtract_fusion.9), custom_call_target="Cholesky" | custom-call | tf_op jit(solution)/shard_map/cholesky/custom-call.1 | solution.py:26
  190.5 10.2 %custom-call.19 = f32[1,128,128]{1,2,0:T(8,128)S(1)} custom-call(f32[1,128,128]{2,1,0:T(8,128)S(1)} %get-tuple-element.28), custom_call_target="InvertDiagBlocksLowerTriangular" | custom-call | tf_op jit(solution)/shard_map/jit(_solve_triangular)/triangular_solve | solution.py:27
  202.0 11.7 %custom-call.20 = f32[128,128]{1,0:T(8,128)S(1)} custom-call(f32[128,128]{1,0:T(8,128)S(1)} %convolution_subtract_fusion.6), custom_call_target="Cholesky" | custom-call | tf_op jit(solution)/shard_map/cholesky/custom-call.1 | solution.py:26
  215.1 9.8 %custom-call.21 = f32[1,128,128]{1,2,0:T(8,128)S(1)} custom-call(f32[1,128,128]{2,1,0:T(8,128)S(1)} %get-tuple-element.26), custom_call_target="InvertDiagBlocksLowerTriangular" | custom-call | tf_op jit(solution)/shard_map/jit(_solve_triangular)/triangular_solve | solution.py:27
  228.2 11.9 %custom-call.22 = f32[128,128]{1,0:T(8,128)S(1)} custom-call(f32[128,128]{1,0:T(8,128)S(1)} %convolution_subtract_fusion), custom_call_target="Cholesky" | custom-call | tf_op jit(solution)/shard_map/cholesky/custom-call.1 | solution.py:26
  241.4 9.8 %custom-call.23 = f32[1,128,128]{1,2,0:T(8,128)S(1)} custom-call(f32[1,128,128]{2,1,0:T(8,128)S(1)} %get-tuple-element.24), custom_call_target="InvertDiagBlocksLowerTriangular" | custom-call | tf_op jit(solution)/shard_map/jit(_solve_triangular)/triangular_solve | solution.py:27
  257.5 14.7 %all-to-all-done.2 = f32[2,1024,1024]{2,0,1:T(2,128)} async-done(((f32[2,1024,1024]{2,0,1:T(2,128)}), f32[2,1024,1024]{2,0,1:T(2,128)}, u32[]{:S(2)}, u32[]{:S(2)}) %all-to-all-start.2) | async-done | bytes 8388640 | tf_op jit(solution)/shard_map/all_to_all | solution.py:145
  300.9 7.7 %gather_fusion.3 = f32[32,64,1024]{2,1,0:T(8,128)} fusion(f32[2,16,64,1024]{3,2,1,0:T(8,128)} %bitcast.218, s32[32]{0:T(128)S(1)} %reshape.599), kind=kCustom, calls=%fused_computation.13 | custom fusion | bytes 16777472 | tf_op jit(solution)/shard_map/vmap(jit(_take))/gather | solution.py:15
  314.6 8.7 %copy.267 = f32[2,1024,1024]{2,1,0:T(8,128)} copy(f32[2,1024,1024]{1,2,0:T(8,128)} %fusion.1) | data formatting | bytes 16777216 | tf_op jit(solution)/shard_map/transpose | solution.py:151
  323.2 12.7 %gather_fusion.4 = f32[64,64,1024]{2,1,0:T(8,128)} fusion(f32[2,16,64,1024]{3,2,1,0:T(8,128)} %bitcast.219, s32[64]{0:T(128)S(1)} %reshape.605), kind=kCustom, calls=%fused_computation.14 | custom fusion | bytes 33554944 | tf_op jit(solution)/shard_map/vmap(jit(_take))/gather | solution.py:15
  338.8 7.4 %select_multiply_fusion = f32[2,32,64,1024]{3,2,1,0:T(8,128)S(1)} fusion(f32[2,32,64,1024]{3,2,1,0:T(8,128)} %bitcast.220, f32[2,32]{1,0:T(2,128)S(1)} %fusion.33, pred[2,32]{1,0:T(4,128)(4,1)S(1)} %compare_and_fusion.11), kind=kLoop, calls=%fused_computation.15 | loop fusion | flops 8388608 | bytes 33554752 | tf_op jit(solution)/shard_map/mul | solution.py:152
  352.9 14.1 %bitcast_add_fusion = f32[2048,1024]{1,0:T(8,128)} fusion(f32[1,32,64,1024]{3,2,1,0:T(8,128)} %get-tuple-element.45, f32[2048,1024]{1,0:T(8,128)} %param.33, f32[1,32,64,1024]{3,2,1,0:T(8,128)} %get-tuple-element.44), kind=kLoop, calls=%fused_computation.17 | loop fusion | flops 4194304 | bytes 33554432 | tf_op jit(solution)/shard_map/add | solution.py:154
  367.0 6.9 %reshape.492 = f32[2,8,1024,64]{3,2,1,0:T(8,128)} reshape(f32[16,512,128]{2,1,0:T(8,128)} %all-gather.6.cloned.1.call-done) | data formatting | bytes 8388608 | tf_op jit(solution)/shard_map/reshape | solution.py:176
  374.0 11.4 %copy.268 = f32[2,1024,8,64]{3,2,1,0:T(8,128)} copy(f32[2,1024,8,64]{3,1,2,0:T(8,128)} %bitcast.225) | data formatting | bytes 8388608 | tf_op jit(solution)/shard_map/transpose | solution.py:177
  385.4 7.8 %dot_general.136 = f32[32,64,512]{2,1,0:T(8,128)} reshape(f32[2,1024,8,64]{3,2,1,0:T(8,128)} %copy.268) | data formatting | bytes 8388608 | tf_op jit(solution)/shard_map/rp,qp->rq/dot_general | solution.py:179
  393.2 9.6 %select_select_fusion = f32[32,64,512]{2,1,0:T(8,128)S(1)} fusion(f32[32,64,512]{2,1,0:T(8,128)} %gather_fusion.2, f32[32,64,512]{2,1,0:T(8,128)} %dot_general.136, pred[32]{0:T(512)(128)(4,1)S(1)} %get-tuple-element.80, pred[32]{0:T(512)(128)(4,1)S(1)} %broadcast_compare_fusion.1, f32[512,512]{1,0:T(8,128)S(1)} %copy-done.4), kind=kOutput, calls=%fused_computation.25 | convolution fusion | flops 6444548096 | bytes 13631552 | tf_op jit(solution)/shard_map/rp,qp->rq/dot_general | solution.py:179
  416.2 41.9 %all-gather.8.cloned.1.call-done = f32[1024,512]{1,0:T(8,128)} async-done(((f32[128,512]{1,0:T(8,128)}), f32[1024,512]{1,0:T(8,128)}) %all-gather.8.cloned.1.call-update) | async-done | bytes 2097168 | tf_op jit(solution)/shard_map/all_gather | solution.py:201
  458.1 18.8 %subtract_select_fusion = f32[2048,1024]{1,0:T(8,128)} fusion(f32[2048,1024]{1,0:T(8,128)} %bitcast_add_fusion, pred[1024]{0:T(1024)(128)(4,1)S(1)} %fusion.46, pred[2048]{0:T(1024)(128)(4,1)S(1)} %fusion.40, f32[2048,512]{1,0:T(8,128)} %bitcast.222, f32[1024,512]{1,0:T(8,128)} %all-gather.8.cloned.1.call-done), kind=kOutput, calls=%fused_computation.22 | convolution fusion | flops 12891193344 | bytes 23071744 | tf_op jit(solution)/shard_map/rp,cp->rc/dot_general | solution.py:202
  (227 shorter events, 156.4 us)
Async XLA Ops:
  18.7 7.7 %copy-start.7 = (s32[2,128]{1,0:T(2,128)S(1)}, s32[2,128]{1,0:T(2,128)}, u32[]{:S(2)}) copy-start(s32[2,128]{1,0:T(2,128)} %param.36) | copy-start | bytes 3076
  20.5 10.2 %copy-start.6 = (s32[2,128]{1,0:T(2,128)S(1)}, s32[2,128]{1,0:T(2,128)}, u32[]{:S(2)}) copy-start(s32[2,128]{1,0:T(2,128)} %param.35) | copy-start | bytes 3076
  20.5 32.1 %all-to-all-start = ((f32[8,128,512]{2,1,0:T(8,128)}), f32[8,128,512]{2,1,0:T(8,128)S(1)}, u32[]{:S(2)}, u32[]{:S(2)}) async-start(f32[8,128,512]{2,1,0:T(8,128)} %bitcast.234), calls=%async_computation | async-start | bytes 4194304 | tf_op jit(solution)/shard_map/all_to_all | solution.py:112
  52.6 33.3 %copy-start.3 = (f32[8,128,512]{2,1,0:T(8,128)}, f32[8,128,512]{2,1,0:T(8,128)S(1)}, u32[]{:S(2)}) copy-start(f32[8,128,512]{2,1,0:T(8,128)S(1)} %all-to-all-done) | copy-start | bytes 6291460
  52.6 31.6 %all-to-all-start.1 = ((f32[8,128,512]{2,1,0:T(8,128)}), f32[8,128,512]{2,1,0:T(8,128)}, u32[]{:S(2)}, u32[]{:S(2)}) async-start(f32[8,128,512]{2,1,0:T(8,128)} %bitcast.233), calls=%async_computation.1 | async-start | bytes 4194304 | tf_op jit(solution)/shard_map/all_to_all | solution.py:112
  87.6 14.5 %all-to-all-start.3 = ((f32[16,4,512]{2,1,0:T(4,128)}), f32[16,4,512]{2,1,0:T(4,128)S(1)}, u32[]{:S(2)}, u32[]{:S(2)}) async-start(f32[16,4,512]{2,1,0:T(4,128)} %reshape.483), calls=%async_computation.3 | async-start | bytes 262144 | tf_op jit(solution)/shard_map/all_to_all | solution.py:131
  102.7 10.3 %all-to-all-start.4 = ((f32[16,4,512]{2,1,0:T(4,128)}), f32[16,4,512]{2,1,0:T(4,128)S(1)}, u32[]{:S(2)}, u32[]{:S(2)}) async-start(f32[16,4,512]{2,1,0:T(4,128)} %broadcast_in_dim.154), calls=%async_computation.4 | async-start | bytes 262144 | tf_op jit(solution)/shard_map/all_to_all | solution.py:134
  106.4 43.4 %all-gather.4.cloned.1.call-start = ((), (), s32[]{:S(2)}) async-start(), calls=%async_computation.5 | async-start | bytes 1179648 | tf_op jit(solution)/shard_map/all_gather | solution.py:136
  126.0 3.5 copy-start.2
  144.7 127.5 %all-to-all-start.2 = ((f32[2,1024,1024]{2,0,1:T(2,128)}), f32[2,1024,1024]{2,0,1:T(2,128)}, u32[]{:S(2)}, u32[]{:S(2)}) async-start(f32[2,1024,1024]{2,0,1:T(2,128)} %copy.236), calls=%async_computation.2 | async-start | bytes 16777216 | tf_op jit(solution)/shard_map/all_to_all | solution.py:145
  149.5 217.6 %all-gather.6.cloned.1.call-start = ((), (), s32[]{:S(2)}) async-start(), calls=%async_computation.6 | async-start | bytes 4456448 | tf_op jit(solution)/shard_map/all_gather | solution.py:174
  278.3 4.7 copy-start
  291.2 8.1 %collective-permute-start = (f32[1024,64]{1,0:T(8,128)S(1)}, f32[1024,64]{1,0:T(8,128)S(1)}, u32[]{:S(2)}, u32[]{:S(2)}) collective-permute-start(f32[1024,64]{1,0:T(8,128)S(1)} %slice.222), channel_id=1, source_target_pairs={{0,8},{1,9},{2,10},{3,11},{4,12},{5,13},{6,14},{7,15},{16,24},{17,... | collective-permute-start | bytes 786440 | tf_op jit(solution)/shard_map/ppermute | solution.py:167
  300.2 157.9 %all-gather.8.cloned.1.call-start = ((), (), s32[]{:S(2)}) async-start(), calls=%async_computation.7 | async-start | bytes 2359296 | tf_op jit(solution)/shard_map/all_gather | solution.py:201
  385.4 7.8 %copy-start.4 = (f32[512,512]{1,0:T(8,128)S(1)}, f32[512,512]{1,0:T(8,128)}, u32[]{:S(2)}) copy-start(f32[512,512]{1,0:T(8,128)} %fusion.7) | copy-start | bytes 3145732
  402.8 2.0 copy-start.1
  405.1 10.3 %collective-permute-start.1 = (f32[128,512]{1,0:T(8,128)S(1)}, f32[128,512]{1,0:T(8,128)S(1)}, u32[]{:S(2)}, u32[]{:S(2)}) collective-permute-start(f32[128,512]{1,0:T(8,128)S(1)} %constant_dynamic-slice_fusion.1), channel_id=1, source_target_pairs={{0,0},{1,16},{2,32},{3,48},{4,64},{5,80},{6,96},{7,112},{8,8},{9,2... | collective-permute-start | bytes 786440 | tf_op jit(solution)/shard_map/ppermute | solution.py:200
  415.5 0.7 copy-start.5
Sparse Core Ops, SparseCore 0:
  113.9 22.9 all-gather.3
  300.3 64.5 all-gather.5
  416.3 41.7 all-gather.7
